TPU v7x, 128 devices: a whole 4x4x4 slice. The times are simulated.
128 devices in a mesh: group: 8 (over z, core), member: 16 (over y, x).
Axes of the slice: x: 4, y: 4, z: 4, core: 2. Of those that a mesh axis runs over, the one named last changes fastest.
Arguments:
- embeddings: bfloat16 [65536, 1024], P(('group', 'member')), may hold values from -70 to 70
- coarse_ids: int32 [65536, 1], P(('group', 'member')), may hold values from 0 to 127; in each aligned block of 512 rows (0 to 511, 512 to 1023, ...) at most 8 rows name the same one
- centroid_seeds: bfloat16 [4096, 1024], P('group'), may hold values from -1 to 1
Outputs:
- refined_centroids: float32 [4096, 1024], P(('group', 'member'))
- row_energy: float32 [65536], P(('group', 'member'))
Inputs may be any that keep to these rules, and one draw needn't show every extreme that they name: `coarse_ids`: in the rows of one device no coarse cluster is named by more than 8 rows.
All inputs are finite; a program needn't handle non-finite values.
Results may differ from a plain program's by a relative error of at most 0.00092.
Values may be sent and summed in bfloat16 or wider, within the bound.
No kernel may reach another device: no remote copies, remote signals or barrier semaphores. Data moves between devices by JAX's collectives and lax.ppermute only.
A program may use at most 64 MiB of HBM per device.

v0:
```python
import math

import jax
import jax.numpy as jnp
from jax import lax
from jax.sharding import Mesh
from jax.sharding import PartitionSpec as P


K = 512
ITERS = 2


smoothing_scale = 0.004
prior_mass = 32.0
empty_mark = 2.0


ALL = ("z", "core", "yhi", "ylo", "x")
ROUTE = ("z", "yhi", "core", "ylo", "x")
TEAM = ("core", "ylo", "x")
PLANE = ("ylo", "x")


def steps(embeddings, coarse_ids, centroid_seeds):
    rows_dev, features = embeddings.shape
    cores = lax.axis_size("core")
    plane = lax.axis_size("ylo") * lax.axis_size("x")
    members = cores * plane
    clusters = members * lax.axis_size("z") * lax.axis_size("yhi")
    capacity = 2 * rows_dev // clusters
    share_rows = K // members
    core = lax.axis_index("core")
    yhi = lax.axis_index("yhi")
    spot = lax.axis_index(PLANE)
    first_row = lax.axis_index(TEAM) * share_rows
    partner = lax.ppermute(centroid_seeds, "core", [(0, 1), (1, 0)])
    seeds16 = jnp.where(core == yhi, centroid_seeds, partner)
    widened = embeddings.astype(jnp.float32)
    unit_rows = (
        widened
        * lax.rsqrt(jnp.mean(widened * widened, axis=1, keepdims=True) + 1e-06)
        / math.sqrt(features)
    ).astype(jnp.bfloat16)
    cluster_of = coarse_ids[:, 0]
    order = jnp.arange(rows_dev, dtype=jnp.int32)
    earlier_same = (cluster_of[None, :] == cluster_of[:, None]) & (order[None, :] < order[:, None])
    row_rank = jnp.sum(earlier_same.astype(jnp.int32), axis=1)
    slot_of = cluster_of * capacity + row_rank
    placement = (
        slot_of[None, :] == jnp.arange(clusters * capacity, dtype=jnp.int32)[:, None]
    ).astype(jnp.bfloat16)
    filled = jnp.sum(placement.astype(jnp.float32), axis=1) > 0.5
    empty_row = jnp.where(
        jnp.arange(features) == 0, jnp.bfloat16(empty_mark), jnp.bfloat16(0)
    ).astype(jnp.bfloat16)
    gathered = jnp.dot(placement, unit_rows, preferred_element_type=jnp.float32).astype(
        jnp.bfloat16
    )
    packed = jnp.where(filled[:, None], gathered, empty_row[None, :])
    arrived = lax.all_to_all(packed, ROUTE, split_axis=0, concat_axis=0, tiled=True)
    slot_mask = (arrived[:, 0].astype(jnp.float32) < 1.5).astype(jnp.float32)
    widened_rows = jnp.concatenate(
        [
            arrived,
            jnp.ones((arrived.shape[0], 1), jnp.bfloat16),
            jnp.zeros((arrived.shape[0], 127), jnp.bfloat16),
        ],
        axis=1,
    )
    seeds = seeds16.astype(jnp.float32)
    own = lax.dynamic_slice_in_dim(seeds, first_row, share_rows, 0)
    prototype_lowbits = seeds16
    half_quadratic_length = 0.5 * jnp.sum(seeds * seeds, axis=1)
    for iteration in range(ITERS):
        similarity_logits = (
            jnp.dot(arrived, prototype_lowbits.T, preferred_element_type=jnp.float32)
            - half_quadratic_length[None, :]
        ) / smoothing_scale
        row_max = jnp.max(similarity_logits, axis=1, keepdims=True)
        powers = jnp.exp(similarity_logits - row_max)
        row_sum = jnp.sum(powers, axis=1, keepdims=True)
        weights = (powers / row_sum * slot_mask[:, None]).astype(jnp.bfloat16)
        closing_log_partition = row_max[:, 0] + jnp.log(row_sum[:, 0])
        if iteration + 1 == ITERS:
            returned = lax.all_to_all(
                smoothing_scale * closing_log_partition, ROUTE, split_axis=0, concat_axis=0,
                tiled=True,
            )
        if iteration + 1 < ITERS:
            weighted = jnp.einsum("rk,rd->kd", weights, arrived, preferred_element_type=jnp.float32)
            masses = jnp.sum(weights.astype(jnp.float32), axis=0)
            combined = jnp.concatenate(
                [
                    weighted.reshape(members, share_rows * features),
                    jnp.pad(masses.reshape(members, share_rows), ((0, 0), (0, 128 - share_rows))),
                ],
                axis=1,
            )
            width = combined.shape[1]
            by_core = combined.reshape(cores, plane, width)
            mine = lax.dynamic_index_in_dim(by_core, core, 0, keepdims=False)
            theirs = lax.dynamic_index_in_dim(by_core, 1 - core, 0, keepdims=False)
            halves = mine + lax.ppermute(theirs, "core", [(0, 1), (1, 0)])
            reduced = lax.dynamic_index_in_dim(halves, spot, 0, keepdims=True)
            for shift in range(1, plane):
                outgoing = lax.dynamic_index_in_dim(halves, (spot + shift) % plane, 0, keepdims=True)
                incoming = lax.ppermute(
                    outgoing, PLANE, [(i, (i + shift) % plane) for i in range(plane)]
                )
                reduced = reduced + incoming
            weighted_own = reduced[0, : share_rows * features].reshape(share_rows, features)
            masses_own = reduced[0, share_rows * features : share_rows * features + share_rows]
        else:
            weighted = jnp.einsum(
                "rk,rd->kd", weights, widened_rows, preferred_element_type=jnp.float32
            )
            by_core = weighted.reshape(cores, plane, share_rows, features + 128)
            mine = lax.dynamic_index_in_dim(by_core, core, 0, keepdims=False)
            theirs = lax.dynamic_index_in_dim(by_core, 1 - core, 0, keepdims=False)
            halves = mine + lax.ppermute(theirs, "core", [(0, 1), (1, 0)])
            reduced = lax.dynamic_index_in_dim(halves, spot, 0, keepdims=True)
            for shift in range(1, plane):
                outgoing = lax.dynamic_index_in_dim(
                    halves, (spot + shift) % plane, 0, keepdims=True
                )
                incoming = lax.ppermute(
                    outgoing, PLANE, [(i, (i + shift) % plane) for i in range(plane)]
                )
                reduced = reduced + incoming
            weighted_own = reduced[0, :, :features]
            masses_own = reduced[0, :, features]
        own = (weighted_own + prior_mass * own) / (masses_own + prior_mass)[:, None]
        if iteration + 1 < ITERS:
            half_own = 0.5 * jnp.sum(own * own, axis=1)
            high = lax.reduce_precision(half_own, exponent_bits=8, mantissa_bits=7)
            rest = half_own - high
            middle = lax.reduce_precision(rest, exponent_bits=8, mantissa_bits=7)
            low = rest - middle
            block = jnp.concatenate(
                [
                    own.astype(jnp.bfloat16),
                    jnp.stack([high, middle, low], axis=1).astype(jnp.bfloat16),
                    jnp.zeros((share_rows, 125), jnp.bfloat16),
                ],
                axis=1,
            )
            on_plane = lax.all_to_all(
                jnp.broadcast_to(block[None], (plane,) + block.shape),
                PLANE,
                split_axis=0,
                concat_axis=0,
                tiled=True,
            )
            partner_plane = lax.ppermute(on_plane, "core", [(0, 1), (1, 0)])
            everyone = jnp.concatenate(
                [
                    jnp.where(core == 0, on_plane, partner_plane),
                    jnp.where(core == 0, partner_plane, on_plane),
                ],
                axis=0,
            ).reshape(K, features + 128)
            prototype_lowbits = everyone[:, :features]
            parts = everyone[:, features : features + 3].astype(jnp.float32)
            half_quadratic_length = (parts[:, 0] + parts[:, 1]) + parts[:, 2]
    own_slot = slot_of[None, :] == jnp.arange(clusters * capacity, dtype=jnp.int32)[:, None]
    row_energy = jnp.sum(jnp.where(own_slot, returned[:, None], 0.0), axis=0)
    refined = lax.ppermute(own, ("core", "yhi"), [(0, 0), (1, 2), (2, 1), (3, 3)])
    return (refined, row_energy)


def solution(mesh):
    groups, members = mesh.devices.shape
    fine = Mesh(mesh.devices.reshape(groups // 2, 2, 2, members // 8, 4), ALL)
    in_specs = (P(ALL, None), P(ALL, None), P(("z", "core"), None))
    out_specs = (P(ALL, None), P(ALL))
    return jax.shard_map(steps, mesh=fine, in_specs=in_specs, out_specs=out_specs, check_vma=False)
```

profile of v0, /device:TPU:1, one launch (start us, length us, event | category | flops | bytes accessed | tf_op | source)
XLA Modules:
  0.0 150.4 jit_solution(14689072467958234487)
XLA Ops:
  0.6 1.0 convert_reduce_fusion.2
  1.6 0.7 multiply_add_fusion
  2.6 1.5 %fusion = f32[512]{0:T(512)S(1)} fusion(bf16[512,1024]{1,0:T(8,128)(2,1)} %param.3), kind=kLoop, calls=%fused_computation.4 | loop fusion | flops 1572352 | bytes 1050624 | tf_op jit(solution)/shard_map/reduce_sum | solution.py:42
  4.2 3.9 %select_bitcast_fusion = bf16[128,8,1024]{2,1,0:T(8,128)(2,1)} fusion(pred[1024]{0:T(1024)(128)(4,1)S(1)} %broadcast_compare_fusion, bf16[512,1024]{1,0:T(8,128)(2,1)} %param.3, bf16[1024]{0:T(1024)(128)(2,1)S(1)} %fusion.31, f32[512]{0:T(512)S(1)} %add_rsqrt_fusion, s32[512]{0:T(512)S(1)} %multiply_add_fusion), kind=kOutput, calls=%fused_computation.16 | convolution fusion | flops 1078460416 | bytes 3152896 | tf_op jit(solution)/shard_map/dot_general | solution.py:57
  8.1 11.5 %all-to-all-start = ((bf16[128,8,1024]{2,1,0:T(8,128)(2,1)}), bf16[128,8,1024]{2,1,0:T(8,128)(2,1)S(1)}, u32[]{:S(2)}, u32[]{:S(2)}) async-start(bf16[128,8,1024]{2,1,0:T(8,128)(2,1)} %select_bitcast_fusion), calls=%async_computation | async-start | bytes 4194304 | tf_op jit(solution)/shard_map/all_to_all | solution.py:61
  19.6 1.1 collective-permute-start
  20.8 2.4 %collective-permute-done = bf16[512,1024]{1,0:T(8,128)(2,1)} collective-permute-done((bf16[512,1024]{1,0:T(8,128)(2,1)S(1)}, bf16[512,1024]{1,0:T(8,128)(2,1)}, u32[]{:S(2)}, u32[]{:S(2)}) %collective-permute-start) | collective-permute-done | bytes 1048608 | tf_op jit(solution)/shard_map/ppermute | solution.py:37
  23.2 2.8 %fusion.41 = (f32[512,1024]{1,0:T(8,128)}, bf16[512,1024]{1,0:T(8,128)(2,1)S(1)}) fusion(bf16[512,1024]{1,0:T(8,128)(2,1)} %param.5, bf16[512,1024]{1,0:T(8,128)(2,1)} %collective-permute-done, pred[]{:T(512)S(6)} %eq.74), kind=kLoop, calls=%fused_computation.104 | loop fusion | flops 1048576 | bytes 5242881 | tf_op jit(solution)/shard_map/convert_element_type | solution.py:71
  26.2 23.7 %all-to-all-done = bf16[128,8,1024]{2,1,0:T(8,128)(2,1)S(1)} async-done(((bf16[128,8,1024]{2,1,0:T(8,128)(2,1)}), bf16[128,8,1024]{2,1,0:T(8,128)(2,1)S(1)}, u32[]{:S(2)}, u32[]{:S(2)}) %all-to-all-start) | async-done | bytes 2097184 | tf_op jit(solution)/shard_map/all_to_all | solution.py:61
  50.1 1.3 fusion.5
  51.4 0.5 fusion.7
  51.9 0.8 convert_reduce_fusion
  52.7 2.6 %fusion.35 = f32[512,1024]{1,0:T(8,128)} fusion(bf16[1024,512]{0,1:T(8,128)(2,1)S(1)} %get-tuple-element.7, bf16[128,8,1024]{2,1,0:T(8,128)(2,1)S(1)} %all-to-all-done), kind=kOutput, calls=%fused_computation.98 | convolution fusion | flops 1073741824 | bytes 5242880 | tf_op jit(solution)/shard_map/rk,rd->kd/dot_general | solution.py:91
  55.3 1.7 %concatenate.18 = f32[2,8,32768]{2,1,0:T(8,128)S(1)} reshape(f32[512,1024]{1,0:T(8,128)} %fusion.35) | data formatting | bytes 4194304 | tf_op jit(solution)/shard_map/concatenate | solution.py:93
  57.2 1.3 collective-permute-start.1
  58.5 2.4 %collective-permute-done.1 = f32[8,32896]{1,0:T(8,128)} collective-permute-done((f32[8,32896]{1,0:T(8,128)S(1)}, f32[8,32896]{1,0:T(8,128)}, u32[]{:S(2)}, u32[]{:S(2)}) %collective-permute-start.1) | collective-permute-done | bytes 1052704 | tf_op jit(solution)/shard_map/ppermute | solution.py:104
  61.0 1.3 fusion.13
  62.3 0.6 constant_dynamic-slice_fusion.13
  63.3 1.3 collective-permute-start.3
  64.6 0.6 collective-permute-start.4
  65.2 1.7 %collective-permute-start.5 = (f32[1,32896]{1,0:T(1,128)S(1)}, f32[1,32896]{1,0:T(1,128)S(1)}, u32[]{:S(2)}, u32[]{:S(2)}) collective-permute-start(f32[1,32896]{1,0:T(1,128)S(1)} %get-tuple-element.21), channel_id=1, source_target_pairs={{0,4},{1,5},{2,6},{3,7},{4,0},{5,1},{6,2},{7,3},{8,12},{9,13},{10,... | collective-permute-start | bytes 394760 | tf_op jit(solution)/shard_map/ppermute | solution.py:108
  67.3 6.8 %collective-permute-done.2 = f32[1,32896]{1,0:T(1,128)S(1)} collective-permute-done((f32[1,32896]{1,0:T(1,128)S(1)}, f32[1,32896]{1,0:T(1,128)S(1)}, u32[]{:S(2)}, u32[]{:S(2)}) %collective-permute-start.2) | collective-permute-done | bytes 131616 | tf_op jit(solution)/shard_map/ppermute | solution.py:108
  74.1 0.4 collective-permute-done.4
  74.5 4.5 %collective-permute-done.5 = f32[1,32896]{1,0:T(1,128)S(1)} collective-permute-done((f32[1,32896]{1,0:T(1,128)S(1)}, f32[1,32896]{1,0:T(1,128)S(1)}, u32[]{:S(2)}, u32[]{:S(2)}) %collective-permute-start.5) | collective-permute-done | bytes 131616 | tf_op jit(solution)/shard_map/ppermute | solution.py:108
  79.0 0.4 collective-permute-done.7
  79.4 0.5 add_add_fusion.1
  80.3 1.3 multiply_reduce_fusion.1
  82.1 11.8 %all_to_all.23 = bf16[8,32,1152]{2,1,0:T(8,128)(2,1)S(1)} all-to-all(bf16[8,32,1152]{2,1,0:T(8,128)(2,1)S(1)} %broadcast_in_dim.78), channel_id=1, replica_groups=mesh['z'=4,'core'=2,'yhi'=2,'ylo'=2,'x'=4] {'ylo','x'}, dimensions={0} | all-to-all | bytes 1179648 | tf_op jit(solution)/shard_map/all_to_all | solution.py:148
  93.9 4.0 %collective-permute-start.9 = (bf16[8,32,1152]{2,1,0:T(8,128)(2,1)S(1)}, bf16[8,32,1152]{2,1,0:T(8,128)(2,1)}, u32[]{:S(2)}, u32[]{:S(2)}) collective-permute-start(bf16[8,32,1152]{2,1,0:T(8,128)(2,1)S(1)} %all_to_all.23), channel_id=1, source_target_pairs={{0,16},{16,0},{1,17},{17,1},{2,18},{18,2},{3,19},{19,3},{4,20},{20... | collective-permute-start | bytes 1769480 | tf_op jit(solution)/shard_map/ppermute | solution.py:155
  98.0 3.1 %concatenate.23 = bf16[1024,1152]{1,0:T(8,128)(2,1)} concatenate(bf16[1024,1024]{1,0:T(8,128)(2,1)S(1)} %bitcast.49, bf16[1024,1]{1,0:T(8,128)(2,1)S(1)} %broadcast_in_dim.79, bf16[1024,127]{1,0:T(8,128)(2,1)S(1)} %broadcast_in_dim.80), dimensions={1} | concatenate | bytes 4718592 | tf_op jit(solution)/shard_map/concatenate | solution.py:63
  101.1 1.2 broadcast_select_fusion.2
  102.8 1.3 fusion.6
  104.1 0.5 fusion.8
  104.6 1.8 %fusion.14 = f32[512,1152]{1,0:T(8,128)S(1)} fusion(bf16[1024,1152]{1,0:T(8,128)(2,1)S(1)} %copy-done.2, f32[1024,512]{0,1:T(8,128)S(1)} %get-tuple-element.30, f32[1024]{0:T(1024)S(1)} %fusion.8, f32[1024]{0:T(1024)S(1)} %get-tuple-element.29, f32[512]{0:T(512)S(1)} %fusion.27, f32[1024]{0:T(1024)S(1)} %convert_reduce_fusion.3), kind=kOutput, calls=%fused_computation.35 | convolution fusion | flops 1211105280 | bytes 6830080 | tf_op jit(solution)/shard_map/rk,rd->kd/dot_general | solution.py:115
  106.6 2.8 %collective-permute-done.10 = f32[8,32,1152]{2,1,0:T(8,128)S(1)} collective-permute-done((f32[8,32,1152]{2,1,0:T(8,128)S(1)}, f32[8,32,1152]{2,1,0:T(8,128)S(1)}, u32[]{:S(2)}, u32[]{:S(2)}) %collective-permute-start.10) | collective-permute-done | bytes 1179680 | tf_op jit(solution)/shard_map/ppermute | solution.py:121
  109.7 0.5 collective-permute-start.11
  110.2 1.7 %collective-permute-start.12 = (f32[1,32,1152]{2,1,0:T(8,128)S(1)}, f32[1,32,1152]{2,1,0:T(8,128)S(1)}, u32[]{:S(2)}, u32[]{:S(2)}) collective-permute-start(f32[1,32,1152]{2,1,0:T(8,128)S(1)} %get-tuple-element.14), channel_id=1, source_target_pairs={{0,2},{1,3},{2,4},{3,5},{4,6},{5,7},{6,0},{7,1},{8,10},{9,11},{10,... | collective-permute-start | bytes 442376 | tf_op jit(solution)/shard_map/ppermute | solution.py:127
  111.9 0.8 collective-permute-start.13
  112.7 1.2 collective-permute-start.14
  113.9 0.8 collective-permute-start.15
  114.6 7.1 %collective-permute-done.11 = f32[1,32,1152]{2,1,0:T(8,128)S(1)} collective-permute-done((f32[1,32,1152]{2,1,0:T(8,128)S(1)}, f32[1,32,1152]{2,1,0:T(8,128)S(1)}, u32[]{:S(2)}, u32[]{:S(2)}) %collective-permute-start.11) | collective-permute-done | bytes 147488 | tf_op jit(solution)/shard_map/ppermute | solution.py:127
  121.9 18.3 %all_to_all.24 = f32[128,8,1]{1,2,0:T(1,128)S(1)} all-to-all(f32[128,8,1]{1,2,0:T(1,128)S(1)} %bitcast.54), channel_id=1, replica_groups=mesh['z'=4,'core'=2,'yhi'=2,'ylo'=2,'x'=4] {'z','yhi','core','ylo','x'}, dimensions={0} | all-to-all | bytes 8192 | tf_op jit(solution)/shard_map/all_to_all | solution.py:86
  140.2 0.5 broadcast.127
  140.7 0.8 reduce.13
  141.9 3.2 %collective-permute-start.18 = (f32[32,1024]{1,0:T(8,128)S(1)}, f32[32,1024]{1,0:T(8,128)S(1)}, u32[]{:S(2)}, u32[]{:S(2)}) collective-permute-start(f32[32,1024]{1,0:T(8,128)S(1)} %fusion.29), channel_id=1, source_target_pairs={{0,0},{8,16},{16,8},{24,24},{1,1},{9,17},{17,9},{25,25},{2,2},{10,... | collective-permute-start | bytes 393224 | tf_op jit(solution)/shard_map/ppermute | solution.py:168
  145.1 0.9 select_reduce_fusion
  146.1 3.7 %collective-permute-done.18 = f32[32,1024]{1,0:T(8,128)S(1)} collective-permute-done((f32[32,1024]{1,0:T(8,128)S(1)}, f32[32,1024]{1,0:T(8,128)S(1)}, u32[]{:S(2)}, u32[]{:S(2)}) %collective-permute-start.18) | collective-permute-done | bytes 131104 | tf_op jit(solution)/shard_map/ppermute | solution.py:168
  149.7 0.7 copy.25
  (60 shorter events, 3.9 us)
Async XLA Ops:
  8.1 11.5 %copy-start.3 = (bf16[512,1024]{1,0:T(8,128)(2,1)S(1)}, bf16[512,1024]{1,0:T(8,128)(2,1)}, u32[]{:S(2)}) copy-start(bf16[512,1024]{1,0:T(8,128)(2,1)} %param.5) | copy-start | bytes 3145732
  8.1 41.8 %all-to-all-start = ((bf16[128,8,1024]{2,1,0:T(8,128)(2,1)}), bf16[128,8,1024]{2,1,0:T(8,128)(2,1)S(1)}, u32[]{:S(2)}, u32[]{:S(2)}) async-start(bf16[128,8,1024]{2,1,0:T(8,128)(2,1)} %select_bitcast_fusion), calls=%async_computation | async-start | bytes 4194304 | tf_op jit(solution)/shard_map/all_to_all | solution.py:61
  19.6 3.6 %collective-permute-start = (bf16[512,1024]{1,0:T(8,128)(2,1)S(1)}, bf16[512,1024]{1,0:T(8,128)(2,1)}, u32[]{:S(2)}, u32[]{:S(2)}) collective-permute-start(bf16[512,1024]{1,0:T(8,128)(2,1)S(1)} %copy-done.3), channel_id=1, source_target_pairs={{0,16},{16,0},{1,17},{17,1},{2,18},{18,2},{3,19},{19,3},{4,20},{20... | collective-permute-start | bytes 3145736 | tf_op jit(solution)/shard_map/ppermute | solution.py:37
  49.9 2.8 %copy-start = (bf16[128,8,1024]{2,1,0:T(8,128)(2,1)}, bf16[128,8,1024]{2,1,0:T(8,128)(2,1)S(1)}, u32[]{:S(2)}) copy-start(bf16[128,8,1024]{2,1,0:T(8,128)(2,1)S(1)} %all-to-all-done) | copy-start | bytes 6291460
  57.2 3.8 %collective-permute-start.1 = (f32[8,32896]{1,0:T(8,128)S(1)}, f32[8,32896]{1,0:T(8,128)}, u32[]{:S(2)}, u32[]{:S(2)}) collective-permute-start(f32[8,32896]{1,0:T(8,128)S(1)} %fusion.10), channel_id=1, source_target_pairs={{0,16},{16,0},{1,17},{17,1},{2,18},{18,2},{3,19},{19,3},{4,20},{20... | collective-permute-start | bytes 3158024 | tf_op jit(solution)/shard_map/ppermute | solution.py:104
  62.9 11.2 %collective-permute-start.2 = (f32[1,32896]{1,0:T(1,128)S(1)}, f32[1,32896]{1,0:T(1,128)S(1)}, u32[]{:S(2)}, u32[]{:S(2)}) collective-permute-start(f32[1,32896]{1,0:T(1,128)S(1)} %get-tuple-element.17), channel_id=1, source_target_pairs={{0,1},{1,2},{2,3},{3,4},{4,5},{5,6},{6,7},{7,0},{8,9},{9,10},{10,1... | collective-permute-start | bytes 394760 | tf_op jit(solution)/shard_map/ppermute | solution.py:108
  63.3 10.8 %collective-permute-start.3 = (f32[1,32896]{1,0:T(1,128)S(1)}, f32[1,32896]{1,0:T(1,128)S(1)}, u32[]{:S(2)}, u32[]{:S(2)}) collective-permute-start(f32[1,32896]{1,0:T(1,128)S(1)} %get-tuple-element.23), channel_id=1, source_target_pairs={{0,2},{1,3},{2,4},{3,5},{4,6},{5,7},{6,0},{7,1},{8,10},{9,11},{10,... | collective-permute-start | bytes 394760 | tf_op jit(solution)/shard_map/ppermute | solution.py:108
  64.6 9.9 %collective-permute-start.4 = (f32[1,32896]{1,0:T(1,128)S(1)}, f32[1,32896]{1,0:T(1,128)S(1)}, u32[]{:S(2)}, u32[]{:S(2)}) collective-permute-start(f32[1,32896]{1,0:T(1,128)S(1)} %get-tuple-element.22), channel_id=1, source_target_pairs={{0,3},{1,4},{2,5},{3,6},{4,7},{5,0},{6,1},{7,2},{8,11},{9,12},{10,... | collective-permute-start | bytes 394760 | tf_op jit(solution)/shard_map/ppermute | solution.py:108
  65.2 13.8 %collective-permute-start.5 = (f32[1,32896]{1,0:T(1,128)S(1)}, f32[1,32896]{1,0:T(1,128)S(1)}, u32[]{:S(2)}, u32[]{:S(2)}) collective-permute-start(f32[1,32896]{1,0:T(1,128)S(1)} %get-tuple-element.21), channel_id=1, source_target_pairs={{0,4},{1,5},{2,6},{3,7},{4,0},{5,1},{6,2},{7,3},{8,12},{9,13},{10,... | collective-permute-start | bytes 394760 | tf_op jit(solution)/shard_map/ppermute | solution.py:108
  67.0 12.0 %collective-permute-start.6 = (f32[1,32896]{1,0:T(1,128)S(1)}, f32[1,32896]{1,0:T(1,128)S(1)}, u32[]{:S(2)}, u32[]{:S(2)}) collective-permute-start(f32[1,32896]{1,0:T(1,128)S(1)} %get-tuple-element.20), channel_id=1, source_target_pairs={{0,5},{1,6},{2,7},{3,0},{4,1},{5,2},{6,3},{7,4},{8,13},{9,14},{10,... | collective-permute-start | bytes 394760 | tf_op jit(solution)/shard_map/ppermute | solution.py:108
  74.1 5.3 %collective-permute-start.7 = (f32[1,32896]{1,0:T(1,128)S(1)}, f32[1,32896]{1,0:T(1,128)S(1)}, u32[]{:S(2)}, u32[]{:S(2)}) collective-permute-start(f32[1,32896]{1,0:T(1,128)S(1)} %get-tuple-element.19), channel_id=1, source_target_pairs={{0,6},{1,7},{2,0},{3,1},{4,2},{5,3},{6,4},{7,5},{8,14},{9,15},{10,... | collective-permute-start | bytes 394760 | tf_op jit(solution)/shard_map/ppermute | solution.py:108
  74.1 5.3 %collective-permute-start.8 = (f32[1,32896]{1,0:T(1,128)S(1)}, f32[1,32896]{1,0:T(1,128)S(1)}, u32[]{:S(2)}, u32[]{:S(2)}) collective-permute-start(f32[1,32896]{1,0:T(1,128)S(1)} %get-tuple-element.18), channel_id=1, source_target_pairs={{0,7},{1,0},{2,1},{3,2},{4,3},{5,4},{6,5},{7,6},{8,15},{9,8},{10,9... | collective-permute-start | bytes 394760 | tf_op jit(solution)/shard_map/ppermute | solution.py:108
  79.9 18.1 %copy-start.1 = (bf16[128,8,1024]{2,1,0:T(8,128)(2,1)S(1)}, bf16[128,8,1024]{2,1,0:T(8,128)(2,1)}, u32[]{:S(2)}) copy-start(bf16[128,8,1024]{2,1,0:T(8,128)(2,1)} %copy-done) | copy-start | bytes 6291460
  93.9 7.2 %collective-permute-start.9 = (bf16[8,32,1152]{2,1,0:T(8,128)(2,1)S(1)}, bf16[8,32,1152]{2,1,0:T(8,128)(2,1)}, u32[]{:S(2)}, u32[]{:S(2)}) collective-permute-start(bf16[8,32,1152]{2,1,0:T(8,128)(2,1)S(1)} %all_to_all.23), channel_id=1, source_target_pairs={{0,16},{16,0},{1,17},{17,1},{2,18},{18,2},{3,19},{19,3},{4,20},{20... | collective-permute-start | bytes 1769480 | tf_op jit(solution)/shard_map/ppermute | solution.py:155
  102.7 1.8 %copy-start.2 = (bf16[1024,1152]{1,0:T(8,128)(2,1)S(1)}, bf16[1024,1152]{1,0:T(8,128)(2,1)}, u32[]{:S(2)}) copy-start(bf16[1024,1152]{1,0:T(8,128)(2,1)} %concatenate.23) | copy-start | bytes 7077892
  106.5 2.9 %collective-permute-start.10 = (f32[8,32,1152]{2,1,0:T(8,128)S(1)}, f32[8,32,1152]{2,1,0:T(8,128)S(1)}, u32[]{:S(2)}, u32[]{:S(2)}) collective-permute-start(f32[8,32,1152]{2,1,0:T(8,128)S(1)} %dynamic-slice_bitcast_fusion), channel_id=1, source_target_pairs={{0,16},{16,0},{1,17},{17,1},{2,18},{18,2},{3,19},{19,3},{4,20},{20... | collective-permute-start | bytes 3538952 | tf_op jit(solution)/shard_map/ppermute | solution.py:121
  109.7 12.1 %collective-permute-start.11 = (f32[1,32,1152]{2,1,0:T(8,128)S(1)}, f32[1,32,1152]{2,1,0:T(8,128)S(1)}, u32[]{:S(2)}, u32[]{:S(2)}) collective-permute-start(f32[1,32,1152]{2,1,0:T(8,128)S(1)} %get-tuple-element.8), channel_id=1, source_target_pairs={{0,1},{1,2},{2,3},{3,4},{4,5},{5,6},{6,7},{7,0},{8,9},{9,10},{10,1... | collective-permute-start | bytes 442376 | tf_op jit(solution)/shard_map/ppermute | solution.py:127
  110.2 11.6 %collective-permute-start.12 = (f32[1,32,1152]{2,1,0:T(8,128)S(1)}, f32[1,32,1152]{2,1,0:T(8,128)S(1)}, u32[]{:S(2)}, u32[]{:S(2)}) collective-permute-start(f32[1,32,1152]{2,1,0:T(8,128)S(1)} %get-tuple-element.14), channel_id=1, source_target_pairs={{0,2},{1,3},{2,4},{3,5},{4,6},{5,7},{6,0},{7,1},{8,10},{9,11},{10,... | collective-permute-start | bytes 442376 | tf_op jit(solution)/shard_map/ppermute | solution.py:127
  111.9 29.7 %collective-permute-start.13 = (f32[1,32,1152]{2,1,0:T(8,128)S(1)}, f32[1,32,1152]{2,1,0:T(8,128)S(1)}, u32[]{:S(2)}, u32[]{:S(2)}) collective-permute-start(f32[1,32,1152]{2,1,0:T(8,128)S(1)} %get-tuple-element.13), channel_id=1, source_target_pairs={{0,3},{1,4},{2,5},{3,6},{4,7},{5,0},{6,1},{7,2},{8,11},{9,12},{10,... | collective-permute-start | bytes 442376 | tf_op jit(solution)/shard_map/ppermute | solution.py:127
  112.7 28.9 %collective-permute-start.14 = (f32[1,32,1152]{2,1,0:T(8,128)S(1)}, f32[1,32,1152]{2,1,0:T(8,128)S(1)}, u32[]{:S(2)}, u32[]{:S(2)}) collective-permute-start(f32[1,32,1152]{2,1,0:T(8,128)S(1)} %get-tuple-element.12), channel_id=1, source_target_pairs={{0,4},{1,5},{2,6},{3,7},{4,0},{5,1},{6,2},{7,3},{8,12},{9,13},{10,... | collective-permute-start | bytes 442376 | tf_op jit(solution)/shard_map/ppermute | solution.py:127
  113.9 27.7 %collective-permute-start.15 = (f32[1,32,1152]{2,1,0:T(8,128)S(1)}, f32[1,32,1152]{2,1,0:T(8,128)S(1)}, u32[]{:S(2)}, u32[]{:S(2)}) collective-permute-start(f32[1,32,1152]{2,1,0:T(8,128)S(1)} %get-tuple-element.11), channel_id=1, source_target_pairs={{0,5},{1,6},{2,7},{3,0},{4,1},{5,2},{6,3},{7,4},{8,13},{9,14},{10,... | collective-permute-start | bytes 442376 | tf_op jit(solution)/shard_map/ppermute | solution.py:127
  121.8 19.9 %collective-permute-start.16 = (f32[1,32,1152]{2,1,0:T(8,128)S(1)}, f32[1,32,1152]{2,1,0:T(8,128)S(1)}, u32[]{:S(2)}, u32[]{:S(2)}) collective-permute-start(f32[1,32,1152]{2,1,0:T(8,128)S(1)} %get-tuple-element.10), channel_id=1, source_target_pairs={{0,6},{1,7},{2,0},{3,1},{4,2},{5,3},{6,4},{7,5},{8,14},{9,15},{10,... | collective-permute-start | bytes 442376 | tf_op jit(solution)/shard_map/ppermute | solution.py:127
  121.8 19.9 %collective-permute-start.17 = (f32[1,32,1152]{2,1,0:T(8,128)S(1)}, f32[1,32,1152]{2,1,0:T(8,128)S(1)}, u32[]{:S(2)}, u32[]{:S(2)}) collective-permute-start(f32[1,32,1152]{2,1,0:T(8,128)S(1)} %get-tuple-element.9), channel_id=1, source_target_pairs={{0,7},{1,0},{2,1},{3,2},{4,3},{5,4},{6,5},{7,6},{8,15},{9,8},{10,9... | collective-permute-start | bytes 442376 | tf_op jit(solution)/shard_map/ppermute | solution.py:127
  141.9 7.8 %collective-permute-start.18 = (f32[32,1024]{1,0:T(8,128)S(1)}, f32[32,1024]{1,0:T(8,128)S(1)}, u32[]{:S(2)}, u32[]{:S(2)}) collective-permute-start(f32[32,1024]{1,0:T(8,128)S(1)} %fusion.29), channel_id=1, source_target_pairs={{0,0},{8,16},{16,8},{24,24},{1,1},{9,17},{17,9},{25,25},{2,2},{10,... | collective-permute-start | bytes 393224 | tf_op jit(solution)/shard_map/ppermute | solution.py:168
where the time goes:
time: 151 us; the launch traced here: 150 us
  waiting for transfers between devices  54.2 us (36%)
  starting transfers between devices  30.6 us (20%)
  blocking collectives  30.2 us (20%)
  other arithmetic  15.4 us (10%)
  matrix products  11 us (7%)
  local copies, waits for them, and re-layouts  7.96 us (5%)
    all_to_all x1, waiting for transfers between devices, steps(): lax.all_to_all(packed, ROUTE, split_axis=0, concat_axis=0, tiled=True)  23.7 us
    ppermute x14, waiting for transfers between devices, steps(): lax.ppermute(outgoing, PLANE, [(i, (i + shift) % plane) for i in range(pl...  19.2 us
    all_to_all x1, blocking collectives, steps(): lax.all_to_all(smoothing_scale * closing_log_partition, ROUTE, split_axis...  18.3 us
    all_to_all x1, blocking collectives, steps(): lax.all_to_all(jnp.broadcast_to(block[None], (plane,) + block.shape), PLA...  11.8 us
    all_to_all x1, starting transfers between devices, steps(): lax.all_to_all(packed, ROUTE, split_axis=0, concat_axis=0, tiled=True)  11.5 us
    ppermute x14, starting transfers between devices, steps(): lax.ppermute(outgoing, PLANE, [(i, (i + shift) % plane) for i in range(pl...  9.35 us
    ppermute x2, waiting for transfers between devices, steps(): halves = mine + lax.ppermute(theirs, 'core', [(0, 1), (1, 0)])  5.26 us
    ppermute x1, starting transfers between devices, steps(): partner_plane = lax.ppermute(on_plane, 'core', [(0, 1), (1, 0)])  4 us
  transfers between devices with their start and end apart: 20, of which 10 were waited for; matrix products, arithmetic and copies ran while one was open for 6% of the time, Pallas kernels for 0%

commit v1 on v0

--- a/solution.py
+++ b/solution.py
@@ -43,9 +43,10 @@
         / math.sqrt(features)
     ).astype(jnp.bfloat16)
     cluster_of = coarse_ids[:, 0]
-    order = jnp.arange(rows_dev, dtype=jnp.int32)
-    earlier_same = (cluster_of[None, :] == cluster_of[:, None]) & (order[None, :] < order[:, None])
-    row_rank = jnp.sum(earlier_same.astype(jnp.int32), axis=1)
+    onehot = (cluster_of[:, None] == jnp.arange(clusters, dtype=jnp.int32)[None, :]).astype(
+        jnp.int32
+    )
+    row_rank = jnp.sum((jnp.cumsum(onehot, axis=0) - onehot) * onehot, axis=1)
     slot_of = cluster_of * capacity + row_rank
     placement = (
         slot_of[None, :] == jnp.arange(clusters * capacity, dtype=jnp.int32)[:, None]
@@ -112,13 +113,16 @@
             weighted_own = reduced[0, : share_rows * features].reshape(share_rows, features)
             masses_own = reduced[0, share_rows * features : share_rows * features + share_rows]
         else:
-            weighted = jnp.einsum(
-                "rk,rd->kd", weights, widened_rows, preferred_element_type=jnp.float32
-            )
-            by_core = weighted.reshape(cores, plane, share_rows, features + 128)
-            mine = lax.dynamic_index_in_dim(by_core, core, 0, keepdims=False)
-            theirs = lax.dynamic_index_in_dim(by_core, 1 - core, 0, keepdims=False)
-            halves = mine + lax.ppermute(theirs, "core", [(0, 1), (1, 0)])
+            half_rows = K // cores
+
+            def side_sums(side):
+                picked = lax.dynamic_slice_in_dim(weights, side * half_rows, half_rows, 1)
+                return jnp.einsum(
+                    "rk,rd->kd", picked, widened_rows, preferred_element_type=jnp.float32
+                ).reshape(plane, share_rows, features + 128)
+
+            got = lax.ppermute(side_sums(1 - core), "core", [(0, 1), (1, 0)])
+            halves = side_sums(core) + got
             reduced = lax.dynamic_index_in_dim(halves, spot, 0, keepdims=True)
             for shift in range(1, plane):
                 outgoing = lax.dynamic_index_in_dim(

time: 151 us -> 154 us (1.020)
  local copies, waits for them, and re-layouts: 7.96 us -> 11.3 us
    ppermute x2 -> x1, waiting for transfers between devices: 5.26 us -> 2.42 us  [steps(): halves = mine + lax.ppermute(theirs, 'core', [(0, 1), (1, 0)])]
    ppermute x0 -> x1, waiting for transfers between devices: none -> 2.34 us  [steps(): got = lax.ppermute(side_sums(1 - core), 'core', [(0, 1), (1, 0)])]
  transfers between devices with their start and end apart: 20 -> 20, of which waited for: 10 -> 10; matrix products, arithmetic and copies ran while one was open for 6% -> 7% of each run, Pallas kernels for 0% -> 0%
where the time goes in v1:
time: 154 us
  waiting for transfers between devices  53.8 us (35%)
  starting transfers between devices  30.5 us (20%)
  blocking collectives  30.2 us (20%)
  other arithmetic  16 us (10%)
  local copies, waits for them, and re-layouts  11.3 us (7%)
  matrix products  10.7 us (7%)
    all_to_all x1, waiting for transfers between devices, steps(): lax.all_to_all(packed, ROUTE, split_axis=0, concat_axis=0, tiled=True)  23.7 us
    ppermute x14, waiting for transfers between devices, steps(): lax.ppermute(outgoing, PLANE, [(i, (i + shift) % plane) for i in range(pl...  19.2 us
    all_to_all x1, blocking collectives, steps(): lax.all_to_all(smoothing_scale * closing_log_partition, ROUTE, split_axis...  18.3 us
    all_to_all x1, blocking collectives, steps(): lax.all_to_all(jnp.broadcast_to(block[None], (plane,) + block.shape), PLA...  11.8 us
    all_to_all x1, starting transfers between devices, steps(): lax.all_to_all(packed, ROUTE, split_axis=0, concat_axis=0, tiled=True)  11.5 us
    ppermute x14, starting transfers between devices, steps(): lax.ppermute(outgoing, PLANE, [(i, (i + shift) % plane) for i in range(pl...  9.35 us
    ppermute x1, starting transfers between devices, steps(): partner_plane = lax.ppermute(on_plane, 'core', [(0, 1), (1, 0)])  4 us
    concatenate x1, local copies, waits for them, and re-layouts, steps(): jnp.concatenate([arrived, jnp.ones((arrived.shape[0], 1), jnp.bfloat16),...  3.77 us
  transfers between devices with their start and end apart: 20, of which 10 were waited for; matrix products, arithmetic and copies ran while one was open for 7% of the time, Pallas kernels for 0%

profile of v1, /device:TPU:1, one launch (start us, length us, event | category | flops | bytes accessed | tf_op | source)
XLA Modules:
  0.0 153.5 jit_solution(10848747734577999456)
XLA Ops:
  0.7 0.9 copy.27
  1.8 0.9 fusion.26
  2.8 0.7 multiply_add_fusion
  4.1 2.8 %select_bitcast_fusion = bf16[128,8,1024]{2,1,0:T(8,128)(2,1)} fusion(pred[1024]{0:T(1024)(128)(4,1)S(1)} %broadcast_compare_fusion, bf16[512,1024]{1,0:T(8,128)(2,1)S(1)} %copy-done.2, bf16[1024]{0:T(1024)(128)(2,1)S(1)} %fusion.35, f32[512]{0:T(512)S(1)} %add_rsqrt_fusion, s32[512]{0:T(512)S(1)} %multiply_add_fusion), kind=kOutput, calls=%fused_computation.16 | convolution fusion | flops 1078460416 | bytes 3152896 | tf_op jit(solution)/shard_map/dot_general | solution.py:58
  6.8 11.5 %all-to-all-start = ((bf16[128,8,1024]{2,1,0:T(8,128)(2,1)}), bf16[128,8,1024]{2,1,0:T(8,128)(2,1)S(1)}, u32[]{:S(2)}, u32[]{:S(2)}) async-start(bf16[128,8,1024]{2,1,0:T(8,128)(2,1)} %select_bitcast_fusion), calls=%async_computation | async-start | bytes 4194304 | tf_op jit(solution)/shard_map/all_to_all | solution.py:62
  18.3 1.1 collective-permute-start
  19.5 2.4 %collective-permute-done = bf16[512,1024]{1,0:T(8,128)(2,1)} collective-permute-done((bf16[512,1024]{1,0:T(8,128)(2,1)S(1)}, bf16[512,1024]{1,0:T(8,128)(2,1)}, u32[]{:S(2)}, u32[]{:S(2)}) %collective-permute-start) | collective-permute-done | bytes 1048608 | tf_op jit(solution)/shard_map/ppermute | solution.py:37
  21.9 2.7 %fusion.44 = (f32[512,1024]{1,0:T(8,128)}, bf16[512,1024]{1,0:T(8,128)(2,1)S(1)}) fusion(bf16[512,1024]{1,0:T(8,128)(2,1)} %param.5, bf16[512,1024]{1,0:T(8,128)(2,1)} %collective-permute-done, pred[]{:T(512)S(6)} %eq.88), kind=kLoop, calls=%fused_computation.108 | loop fusion | flops 1048576 | bytes 5242881 | tf_op jit(solution)/shard_map/convert_element_type | solution.py:72
  24.9 23.7 %all-to-all-done = bf16[128,8,1024]{2,1,0:T(8,128)(2,1)S(1)} async-done(((bf16[128,8,1024]{2,1,0:T(8,128)(2,1)}), bf16[128,8,1024]{2,1,0:T(8,128)(2,1)S(1)}, u32[]{:S(2)}, u32[]{:S(2)}) %all-to-all-start) | async-done | bytes 2097184 | tf_op jit(solution)/shard_map/all_to_all | solution.py:62
  48.8 1.3 fusion.5
  50.6 0.8 convert_reduce_fusion
  51.4 2.6 %fusion.39 = f32[512,1024]{1,0:T(8,128)} fusion(bf16[1024,512]{0,1:T(8,128)(2,1)S(1)} %get-tuple-element.7, bf16[128,8,1024]{2,1,0:T(8,128)(2,1)S(1)} %all-to-all-done), kind=kOutput, calls=%fused_computation.103 | convolution fusion | flops 1073741824 | bytes 5242880 | tf_op jit(solution)/shard_map/rk,rd->kd/dot_general | solution.py:92
  54.0 1.7 %concatenate.18 = f32[2,8,32768]{2,1,0:T(8,128)S(1)} reshape(f32[512,1024]{1,0:T(8,128)} %fusion.39) | data formatting | bytes 4194304 | tf_op jit(solution)/shard_map/concatenate | solution.py:94
  55.9 1.3 collective-permute-start.1
  57.3 2.4 %collective-permute-done.1 = f32[8,32896]{1,0:T(8,128)} collective-permute-done((f32[8,32896]{1,0:T(8,128)S(1)}, f32[8,32896]{1,0:T(8,128)}, u32[]{:S(2)}, u32[]{:S(2)}) %collective-permute-start.1) | collective-permute-done | bytes 1052704 | tf_op jit(solution)/shard_map/ppermute | solution.py:105
  59.7 1.3 fusion.13
  61.0 0.6 constant_dynamic-slice_fusion.12
  62.0 1.3 collective-permute-start.3
  63.3 0.6 collective-permute-start.4
  64.0 1.7 %collective-permute-start.5 = (f32[1,32896]{1,0:T(1,128)S(1)}, f32[1,32896]{1,0:T(1,128)S(1)}, u32[]{:S(2)}, u32[]{:S(2)}) collective-permute-start(f32[1,32896]{1,0:T(1,128)S(1)} %get-tuple-element.21), channel_id=1, source_target_pairs={{0,4},{1,5},{2,6},{3,7},{4,0},{5,1},{6,2},{7,3},{8,12},{9,13},{10,... | collective-permute-start | bytes 394760 | tf_op jit(solution)/shard_map/ppermute | solution.py:109
  66.1 6.8 %collective-permute-done.2 = f32[1,32896]{1,0:T(1,128)S(1)} collective-permute-done((f32[1,32896]{1,0:T(1,128)S(1)}, f32[1,32896]{1,0:T(1,128)S(1)}, u32[]{:S(2)}, u32[]{:S(2)}) %collective-permute-start.2) | collective-permute-done | bytes 131616 | tf_op jit(solution)/shard_map/ppermute | solution.py:109
  73.3 4.5 %collective-permute-done.5 = f32[1,32896]{1,0:T(1,128)S(1)} collective-permute-done((f32[1,32896]{1,0:T(1,128)S(1)}, f32[1,32896]{1,0:T(1,128)S(1)}, u32[]{:S(2)}, u32[]{:S(2)}) %collective-permute-start.5) | collective-permute-done | bytes 131616 | tf_op jit(solution)/shard_map/ppermute | solution.py:109
  79.0 1.1 multiply_reduce_fusion.1
  80.6 11.8 %all_to_all.23 = bf16[8,32,1152]{2,1,0:T(8,128)(2,1)S(1)} all-to-all(bf16[8,32,1152]{2,1,0:T(8,128)(2,1)S(1)} %broadcast_in_dim.77), channel_id=1, replica_groups=mesh['z'=4,'core'=2,'yhi'=2,'ylo'=2,'x'=4] {'ylo','x'}, dimensions={0} | all-to-all | bytes 1179648 | tf_op jit(solution)/shard_map/all_to_all | solution.py:152
  92.5 4.0 %collective-permute-start.9 = (bf16[8,32,1152]{2,1,0:T(8,128)(2,1)S(1)}, bf16[8,32,1152]{2,1,0:T(8,128)(2,1)}, u32[]{:S(2)}, u32[]{:S(2)}) collective-permute-start(bf16[8,32,1152]{2,1,0:T(8,128)(2,1)S(1)} %all_to_all.23), channel_id=1, source_target_pairs={{0,16},{16,0},{1,17},{17,1},{2,18},{18,2},{3,19},{19,3},{4,20},{20... | collective-permute-start | bytes 1769480 | tf_op jit(solution)/shard_map/ppermute | solution.py:159
  96.5 0.7 broadcast_in_dim.79
  97.2 3.8 %concatenate.23 = bf16[1024,1152]{1,0:T(8,128)(2,1)S(1)} concatenate(bf16[1024,1024]{1,0:T(8,128)(2,1)} %bitcast.61, bf16[1024,1]{1,0:T(8,128)(2,1)S(1)} %broadcast_in_dim.78, bf16[1024,127]{1,0:T(8,128)(2,1)} %broadcast_in_dim.79), dimensions={1} | concatenate | bytes 4718592 | tf_op jit(solution)/shard_map/concatenate | solution.py:64
  101.0 1.2 broadcast_select_fusion.2
  102.7 1.1 copy-done.1
  103.8 1.3 fusion.6
  105.6 0.6 multiply_convert_fusion
  106.2 1.9 %fusion.20 = f32[256,1152]{1,0:T(8,128)} fusion(bf16[1024,1152]{1,0:T(8,128)(2,1)S(1)} %concatenate.23, bf16[1024,512]{0,1:T(8,128)(2,1)S(1)} %multiply_convert_fusion, s32[]{:T(128)S(6)} %select_n.157), kind=kOutput, calls=%fused_computation.42 | convolution fusion | flops 603979776 | bytes 4063236 | tf_op jit(solution)/shard_map/rk,rd->kd/dot_general | solution.py:120
  108.1 0.8 fusion.22
  108.9 2.3 %collective-permute-done.10 = f32[8,32,1152]{2,1,0:T(8,128)} collective-permute-done((f32[8,32,1152]{2,1,0:T(8,128)}, f32[8,32,1152]{2,1,0:T(8,128)}, u32[]{:S(2)}, u32[]{:S(2)}) %collective-permute-start.10) | collective-permute-done | bytes 1179680 | tf_op jit(solution)/shard_map/ppermute | solution.py:124
  111.3 1.4 add.284
  112.8 0.5 collective-permute-start.11
  113.3 1.7 %collective-permute-start.12 = (f32[1,32,1152]{2,1,0:T(8,128)S(1)}, f32[1,32,1152]{2,1,0:T(8,128)S(1)}, u32[]{:S(2)}, u32[]{:S(2)}) collective-permute-start(f32[1,32,1152]{2,1,0:T(8,128)S(1)} %get-tuple-element.14), channel_id=1, source_target_pairs={{0,2},{1,3},{2,4},{3,5},{4,6},{5,7},{6,0},{7,1},{8,10},{9,11},{10,... | collective-permute-start | bytes 442376 | tf_op jit(solution)/shard_map/ppermute | solution.py:131
  115.0 0.8 collective-permute-start.13
  115.8 1.2 collective-permute-start.14
  117.0 0.8 collective-permute-start.15
  117.8 7.1 %collective-permute-done.11 = f32[1,32,1152]{2,1,0:T(8,128)S(1)} collective-permute-done((f32[1,32,1152]{2,1,0:T(8,128)S(1)}, f32[1,32,1152]{2,1,0:T(8,128)S(1)}, u32[]{:S(2)}, u32[]{:S(2)}) %collective-permute-start.11) | collective-permute-done | bytes 147488 | tf_op jit(solution)/shard_map/ppermute | solution.py:131
  125.0 18.3 %all_to_all.24 = f32[128,8,1]{1,2,0:T(1,128)S(1)} all-to-all(f32[128,8,1]{1,2,0:T(1,128)S(1)} %bitcast.67), channel_id=1, replica_groups=mesh['z'=4,'core'=2,'yhi'=2,'ylo'=2,'x'=4] {'z','yhi','core','ylo','x'}, dimensions={0} | all-to-all | bytes 8192 | tf_op jit(solution)/shard_map/all_to_all | solution.py:87
  143.3 0.5 broadcast.142
  143.8 0.8 reduce.13
  145.1 3.2 %collective-permute-start.18 = (f32[32,1024]{1,0:T(8,128)S(1)}, f32[32,1024]{1,0:T(8,128)S(1)}, u32[]{:S(2)}, u32[]{:S(2)}) collective-permute-start(f32[32,1024]{1,0:T(8,128)S(1)} %fusion.30), channel_id=1, source_target_pairs={{0,0},{8,16},{16,8},{24,24},{1,1},{9,17},{17,9},{25,25},{2,2},{10,... | collective-permute-start | bytes 393224 | tf_op jit(solution)/shard_map/ppermute | solution.py:172
  148.3 0.9 select_reduce_fusion
  149.2 3.7 %collective-permute-done.18 = f32[32,1024]{1,0:T(8,128)S(1)} collective-permute-done((f32[32,1024]{1,0:T(8,128)S(1)}, f32[32,1024]{1,0:T(8,128)S(1)}, u32[]{:S(2)}, u32[]{:S(2)}) %collective-permute-start.18) | collective-permute-done | bytes 131104 | tf_op jit(solution)/shard_map/ppermute | solution.py:172
  152.9 0.7 copy.34
  (69 shorter events, 6.4 us)
Async XLA Ops:
  0.6 3.1 %copy-start.2 = (bf16[512,1024]{1,0:T(8,128)(2,1)S(1)}, bf16[512,1024]{1,0:T(8,128)(2,1)}, u32[]{:S(2)}) copy-start(bf16[512,1024]{1,0:T(8,128)(2,1)} %param.3) | copy-start | bytes 3145732
  6.8 11.5 %copy-start.3 = (bf16[512,1024]{1,0:T(8,128)(2,1)S(1)}, bf16[512,1024]{1,0:T(8,128)(2,1)}, u32[]{:S(2)}) copy-start(bf16[512,1024]{1,0:T(8,128)(2,1)} %param.5) | copy-start | bytes 3145732
  6.8 41.8 %all-to-all-start = ((bf16[128,8,1024]{2,1,0:T(8,128)(2,1)}), bf16[128,8,1024]{2,1,0:T(8,128)(2,1)S(1)}, u32[]{:S(2)}, u32[]{:S(2)}) async-start(bf16[128,8,1024]{2,1,0:T(8,128)(2,1)} %select_bitcast_fusion), calls=%async_computation | async-start | bytes 4194304 | tf_op jit(solution)/shard_map/all_to_all | solution.py:62
  18.3 3.6 %collective-permute-start = (bf16[512,1024]{1,0:T(8,128)(2,1)S(1)}, bf16[512,1024]{1,0:T(8,128)(2,1)}, u32[]{:S(2)}, u32[]{:S(2)}) collective-permute-start(bf16[512,1024]{1,0:T(8,128)(2,1)S(1)} %copy-done.3), channel_id=1, source_target_pairs={{0,16},{16,0},{1,17},{17,1},{2,18},{18,2},{3,19},{19,3},{4,20},{20... | collective-permute-start | bytes 3145736 | tf_op jit(solution)/shard_map/ppermute | solution.py:37
  48.6 2.8 %copy-start = (bf16[128,8,1024]{2,1,0:T(8,128)(2,1)}, bf16[128,8,1024]{2,1,0:T(8,128)(2,1)S(1)}, u32[]{:S(2)}) copy-start(bf16[128,8,1024]{2,1,0:T(8,128)(2,1)S(1)} %all-to-all-done) | copy-start | bytes 6291460
  55.9 3.8 %collective-permute-start.1 = (f32[8,32896]{1,0:T(8,128)S(1)}, f32[8,32896]{1,0:T(8,128)}, u32[]{:S(2)}, u32[]{:S(2)}) collective-permute-start(f32[8,32896]{1,0:T(8,128)S(1)} %fusion.10), channel_id=1, source_target_pairs={{0,16},{16,0},{1,17},{17,1},{2,18},{18,2},{3,19},{19,3},{4,20},{20... | collective-permute-start | bytes 3158024 | tf_op jit(solution)/shard_map/ppermute | solution.py:105
  61.7 11.2 %collective-permute-start.2 = (f32[1,32896]{1,0:T(1,128)S(1)}, f32[1,32896]{1,0:T(1,128)S(1)}, u32[]{:S(2)}, u32[]{:S(2)}) collective-permute-start(f32[1,32896]{1,0:T(1,128)S(1)} %get-tuple-element.17), channel_id=1, source_target_pairs={{0,1},{1,2},{2,3},{3,4},{4,5},{5,6},{6,7},{7,0},{8,9},{9,10},{10,1... | collective-permute-start | bytes 394760 | tf_op jit(solution)/shard_map/ppermute | solution.py:109
  62.0 10.8 %collective-permute-start.3 = (f32[1,32896]{1,0:T(1,128)S(1)}, f32[1,32896]{1,0:T(1,128)S(1)}, u32[]{:S(2)}, u32[]{:S(2)}) collective-permute-start(f32[1,32896]{1,0:T(1,128)S(1)} %get-tuple-element.23), channel_id=1, source_target_pairs={{0,2},{1,3},{2,4},{3,5},{4,6},{5,7},{6,0},{7,1},{8,10},{9,11},{10,... | collective-permute-start | bytes 394760 | tf_op jit(solution)/shard_map/ppermute | solution.py:109
  63.3 9.9 %collective-permute-start.4 = (f32[1,32896]{1,0:T(1,128)S(1)}, f32[1,32896]{1,0:T(1,128)S(1)}, u32[]{:S(2)}, u32[]{:S(2)}) collective-permute-start(f32[1,32896]{1,0:T(1,128)S(1)} %get-tuple-element.22), channel_id=1, source_target_pairs={{0,3},{1,4},{2,5},{3,6},{4,7},{5,0},{6,1},{7,2},{8,11},{9,12},{10,... | collective-permute-start | bytes 394760 | tf_op jit(solution)/shard_map/ppermute | solution.py:109
  64.0 13.8 %collective-permute-start.5 = (f32[1,32896]{1,0:T(1,128)S(1)}, f32[1,32896]{1,0:T(1,128)S(1)}, u32[]{:S(2)}, u32[]{:S(2)}) collective-permute-start(f32[1,32896]{1,0:T(1,128)S(1)} %get-tuple-element.21), channel_id=1, source_target_pairs={{0,4},{1,5},{2,6},{3,7},{4,0},{5,1},{6,2},{7,3},{8,12},{9,13},{10,... | collective-permute-start | bytes 394760 | tf_op jit(solution)/shard_map/ppermute | solution.py:109
  65.7 12.0 %collective-permute-start.6 = (f32[1,32896]{1,0:T(1,128)S(1)}, f32[1,32896]{1,0:T(1,128)S(1)}, u32[]{:S(2)}, u32[]{:S(2)}) collective-permute-start(f32[1,32896]{1,0:T(1,128)S(1)} %get-tuple-element.20), channel_id=1, source_target_pairs={{0,5},{1,6},{2,7},{3,0},{4,1},{5,2},{6,3},{7,4},{8,13},{9,14},{10,... | collective-permute-start | bytes 394760 | tf_op jit(solution)/shard_map/ppermute | solution.py:109
  72.8 5.3 %collective-permute-start.7 = (f32[1,32896]{1,0:T(1,128)S(1)}, f32[1,32896]{1,0:T(1,128)S(1)}, u32[]{:S(2)}, u32[]{:S(2)}) collective-permute-start(f32[1,32896]{1,0:T(1,128)S(1)} %get-tuple-element.19), channel_id=1, source_target_pairs={{0,6},{1,7},{2,0},{3,1},{4,2},{5,3},{6,4},{7,5},{8,14},{9,15},{10,... | collective-permute-start | bytes 394760 | tf_op jit(solution)/shard_map/ppermute | solution.py:109
  72.8 5.3 %collective-permute-start.8 = (f32[1,32896]{1,0:T(1,128)S(1)}, f32[1,32896]{1,0:T(1,128)S(1)}, u32[]{:S(2)}, u32[]{:S(2)}) collective-permute-start(f32[1,32896]{1,0:T(1,128)S(1)} %get-tuple-element.18), channel_id=1, source_target_pairs={{0,7},{1,0},{2,1},{3,2},{4,3},{5,4},{6,5},{7,6},{8,15},{9,8},{10,9... | collective-permute-start | bytes 394760 | tf_op jit(solution)/shard_map/ppermute | solution.py:109
  92.5 8.6 %collective-permute-start.9 = (bf16[8,32,1152]{2,1,0:T(8,128)(2,1)S(1)}, bf16[8,32,1152]{2,1,0:T(8,128)(2,1)}, u32[]{:S(2)}, u32[]{:S(2)}) collective-permute-start(bf16[8,32,1152]{2,1,0:T(8,128)(2,1)S(1)} %all_to_all.23), channel_id=1, source_target_pairs={{0,16},{16,0},{1,17},{17,1},{2,18},{18,2},{3,19},{19,3},{4,20},{20... | collective-permute-start | bytes 1769480 | tf_op jit(solution)/shard_map/ppermute | solution.py:159
  102.2 1.6 %copy-start.1 = (bf16[128,8,1024]{2,1,0:T(8,128)(2,1)S(1)}, bf16[128,8,1024]{2,1,0:T(8,128)(2,1)}, u32[]{:S(2)}) copy-start(bf16[128,8,1024]{2,1,0:T(8,128)(2,1)} %copy-done) | copy-start | bytes 6291460
  108.1 3.2 %collective-permute-start.10 = (f32[8,32,1152]{2,1,0:T(8,128)}, f32[8,32,1152]{2,1,0:T(8,128)}, u32[]{:S(2)}, u32[]{:S(2)}) collective-permute-start(f32[8,32,1152]{2,1,0:T(8,128)} %bitcast.14), channel_id=1, source_target_pairs={{0,16},{16,0},{1,17},{17,1},{2,18},{18,2},{3,19},{19,3},{4,20},{20... | collective-permute-start | bytes 3538952 | tf_op jit(solution)/shard_map/ppermute | solution.py:124
  112.8 12.1 %collective-permute-start.11 = (f32[1,32,1152]{2,1,0:T(8,128)S(1)}, f32[1,32,1152]{2,1,0:T(8,128)S(1)}, u32[]{:S(2)}, u32[]{:S(2)}) collective-permute-start(f32[1,32,1152]{2,1,0:T(8,128)S(1)} %get-tuple-element.8), channel_id=1, source_target_pairs={{0,1},{1,2},{2,3},{3,4},{4,5},{5,6},{6,7},{7,0},{8,9},{9,10},{10,1... | collective-permute-start | bytes 442376 | tf_op jit(solution)/shard_map/ppermute | solution.py:131
  113.3 11.6 %collective-permute-start.12 = (f32[1,32,1152]{2,1,0:T(8,128)S(1)}, f32[1,32,1152]{2,1,0:T(8,128)S(1)}, u32[]{:S(2)}, u32[]{:S(2)}) collective-permute-start(f32[1,32,1152]{2,1,0:T(8,128)S(1)} %get-tuple-element.14), channel_id=1, source_target_pairs={{0,2},{1,3},{2,4},{3,5},{4,6},{5,7},{6,0},{7,1},{8,10},{9,11},{10,... | collective-permute-start | bytes 442376 | tf_op jit(solution)/shard_map/ppermute | solution.py:131
  115.0 29.7 %collective-permute-start.13 = (f32[1,32,1152]{2,1,0:T(8,128)S(1)}, f32[1,32,1152]{2,1,0:T(8,128)S(1)}, u32[]{:S(2)}, u32[]{:S(2)}) collective-permute-start(f32[1,32,1152]{2,1,0:T(8,128)S(1)} %get-tuple-element.13), channel_id=1, source_target_pairs={{0,3},{1,4},{2,5},{3,6},{4,7},{5,0},{6,1},{7,2},{8,11},{9,12},{10,... | collective-permute-start | bytes 442376 | tf_op jit(solution)/shard_map/ppermute | solution.py:131
  115.8 28.9 %collective-permute-start.14 = (f32[1,32,1152]{2,1,0:T(8,128)S(1)}, f32[1,32,1152]{2,1,0:T(8,128)S(1)}, u32[]{:S(2)}, u32[]{:S(2)}) collective-permute-start(f32[1,32,1152]{2,1,0:T(8,128)S(1)} %get-tuple-element.12), channel_id=1, source_target_pairs={{0,4},{1,5},{2,6},{3,7},{4,0},{5,1},{6,2},{7,3},{8,12},{9,13},{10,... | collective-permute-start | bytes 442376 | tf_op jit(solution)/shard_map/ppermute | solution.py:131
  117.0 27.7 %collective-permute-start.15 = (f32[1,32,1152]{2,1,0:T(8,128)S(1)}, f32[1,32,1152]{2,1,0:T(8,128)S(1)}, u32[]{:S(2)}, u32[]{:S(2)}) collective-permute-start(f32[1,32,1152]{2,1,0:T(8,128)S(1)} %get-tuple-element.11), channel_id=1, source_target_pairs={{0,5},{1,6},{2,7},{3,0},{4,1},{5,2},{6,3},{7,4},{8,13},{9,14},{10,... | collective-permute-start | bytes 442376 | tf_op jit(solution)/shard_map/ppermute | solution.py:131
  124.9 19.9 %collective-permute-start.16 = (f32[1,32,1152]{2,1,0:T(8,128)S(1)}, f32[1,32,1152]{2,1,0:T(8,128)S(1)}, u32[]{:S(2)}, u32[]{:S(2)}) collective-permute-start(f32[1,32,1152]{2,1,0:T(8,128)S(1)} %get-tuple-element.10), channel_id=1, source_target_pairs={{0,6},{1,7},{2,0},{3,1},{4,2},{5,3},{6,4},{7,5},{8,14},{9,15},{10,... | collective-permute-start | bytes 442376 | tf_op jit(solution)/shard_map/ppermute | solution.py:131
  124.9 19.9 %collective-permute-start.17 = (f32[1,32,1152]{2,1,0:T(8,128)S(1)}, f32[1,32,1152]{2,1,0:T(8,128)S(1)}, u32[]{:S(2)}, u32[]{:S(2)}) collective-permute-start(f32[1,32,1152]{2,1,0:T(8,128)S(1)} %get-tuple-element.9), channel_id=1, source_target_pairs={{0,7},{1,0},{2,1},{3,2},{4,3},{5,4},{6,5},{7,6},{8,15},{9,8},{10,9... | collective-permute-start | bytes 442376 | tf_op jit(solution)/shard_map/ppermute | solution.py:131
  145.1 7.8 %collective-permute-start.18 = (f32[32,1024]{1,0:T(8,128)S(1)}, f32[32,1024]{1,0:T(8,128)S(1)}, u32[]{:S(2)}, u32[]{:S(2)}) collective-permute-start(f32[32,1024]{1,0:T(8,128)S(1)} %fusion.30), channel_id=1, source_target_pairs={{0,0},{8,16},{16,8},{24,24},{1,1},{9,17},{17,9},{25,25},{2,2},{10,... | collective-permute-start | bytes 393224 | tf_op jit(solution)/shard_map/ppermute | solution.py:172

commit v2 on v0

--- a/solution.py
+++ b/solution.py
@@ -43,9 +43,10 @@
         / math.sqrt(features)
     ).astype(jnp.bfloat16)
     cluster_of = coarse_ids[:, 0]
-    order = jnp.arange(rows_dev, dtype=jnp.int32)
-    earlier_same = (cluster_of[None, :] == cluster_of[:, None]) & (order[None, :] < order[:, None])
-    row_rank = jnp.sum(earlier_same.astype(jnp.int32), axis=1)
+    onehot = (cluster_of[:, None] == jnp.arange(clusters, dtype=jnp.int32)[None, :]).astype(
+        jnp.int32
+    )
+    row_rank = jnp.sum((jnp.cumsum(onehot, axis=0) - onehot) * onehot, axis=1)
     slot_of = cluster_of * capacity + row_rank
     placement = (
         slot_of[None, :] == jnp.arange(clusters * capacity, dtype=jnp.int32)[:, None]
@@ -90,27 +91,24 @@
         if iteration + 1 < ITERS:
             weighted = jnp.einsum("rk,rd->kd", weights, arrived, preferred_element_type=jnp.float32)
             masses = jnp.sum(weights.astype(jnp.float32), axis=0)
-            combined = jnp.concatenate(
-                [
-                    weighted.reshape(members, share_rows * features),
-                    jnp.pad(masses.reshape(members, share_rows), ((0, 0), (0, 128 - share_rows))),
-                ],
-                axis=1,
-            )
-            width = combined.shape[1]
-            by_core = combined.reshape(cores, plane, width)
+            sums = jnp.zeros((K, features + 128), jnp.float32)
+            sums = lax.dynamic_update_slice(sums, weighted, (0, 0))
+            sums = lax.dynamic_update_slice(sums, masses[:, None], (0, features))
+            by_core = sums.reshape(cores, plane, share_rows, features + 128)
             mine = lax.dynamic_index_in_dim(by_core, core, 0, keepdims=False)
             theirs = lax.dynamic_index_in_dim(by_core, 1 - core, 0, keepdims=False)
             halves = mine + lax.ppermute(theirs, "core", [(0, 1), (1, 0)])
             reduced = lax.dynamic_index_in_dim(halves, spot, 0, keepdims=True)
             for shift in range(1, plane):
-                outgoing = lax.dynamic_index_in_dim(halves, (spot + shift) % plane, 0, keepdims=True)
+                outgoing = lax.dynamic_index_in_dim(
+                    halves, (spot + shift) % plane, 0, keepdims=True
+                )
                 incoming = lax.ppermute(
                     outgoing, PLANE, [(i, (i + shift) % plane) for i in range(plane)]
                 )
                 reduced = reduced + incoming
-            weighted_own = reduced[0, : share_rows * features].reshape(share_rows, features)
-            masses_own = reduced[0, share_rows * features : share_rows * features + share_rows]
+            weighted_own = reduced[0, :, :features]
+            masses_own = reduced[0, :, features]
         else:
             weighted = jnp.einsum(
                 "rk,rd->kd", weights, widened_rows, preferred_element_type=jnp.float32

time: 151 us -> 154 us (1.020)
  local copies, waits for them, and re-layouts: 7.96 us -> 11.7 us
  matrix products: 11 us -> 8.48 us
  waiting for transfers between devices: 54.2 us -> 56.1 us
    dynamic_update_slice x0 -> x2, local copies, waits for them, and re-layouts: none -> 3.32 us  [the longest x1 1.73 us: steps(): sums = lax.dynamic_update_slice(sums, masses[:, None], (0, features))]
    concatenate x2 -> x0, local copies, waits for them, and re-layouts: 1.75 us -> none  [steps(): jnp.concatenate([weighted.reshape(members, share_rows * features), jnp.pa...]
    ppermute x14, waiting for transfers between devices: 19.2 us -> 20.9 us  [steps(): lax.ppermute(outgoing, PLANE, [(i, (i + shift) % plane) for i in range(pl...]
  transfers between devices with their start and end apart: 20 -> 20, of which waited for: 10 -> 11; matrix products, arithmetic and copies ran while one was open for 6% -> 6% of each run, Pallas kernels for 0% -> 0%
where the time goes in v2:
time: 154 us; the launch traced here: 153 us
  waiting for transfers between devices  56.1 us (36%)
  blocking collectives  30.5 us (20%)
  starting transfers between devices  30.3 us (20%)
  other arithmetic  15.4 us (10%)
  local copies, waits for them, and re-layouts  11.7 us (8%)
  matrix products  8.48 us (6%)
    all_to_all x1, waiting for transfers between devices, steps(): lax.all_to_all(packed, ROUTE, split_axis=0, concat_axis=0, tiled=True)  23.7 us
    ppermute x14, waiting for transfers between devices, steps(): lax.ppermute(outgoing, PLANE, [(i, (i + shift) % plane) for i in range(pl...  20.9 us
    all_to_all x1, blocking collectives, steps(): lax.all_to_all(smoothing_scale * closing_log_partition, ROUTE, split_axis...  18.5 us
    all_to_all x1, blocking collectives, steps(): lax.all_to_all(jnp.broadcast_to(block[None], (plane,) + block.shape), PLA...  11.9 us
    all_to_all x1, starting transfers between devices, steps(): lax.all_to_all(packed, ROUTE, split_axis=0, concat_axis=0, tiled=True)  11.5 us
    ppermute x14, starting transfers between devices, steps(): lax.ppermute(outgoing, PLANE, [(i, (i + shift) % plane) for i in range(pl...  9.28 us
    ppermute x2, waiting for transfers between devices, steps(): halves = mine + lax.ppermute(theirs, 'core', [(0, 1), (1, 0)])  5.44 us
    ppermute x1, starting transfers between devices, steps(): partner_plane = lax.ppermute(on_plane, 'core', [(0, 1), (1, 0)])  3.75 us
  transfers between devices with their start and end apart: 20, of which 11 were waited for; matrix products, arithmetic and copies ran while one was open for 6% of the time, Pallas kernels for 0%

profile of v2, /device:TPU:1, one launch (start us, length us, event | category | flops | bytes accessed | tf_op | source)
XLA Modules:
  0.0 153.5 jit_solution(12537060279048896035)
XLA Ops:
  0.7 0.9 copy.30
  1.8 0.9 fusion.23
  2.8 0.7 multiply_add_fusion
  4.1 2.8 %select_bitcast_fusion = bf16[128,8,1024]{2,1,0:T(8,128)(2,1)} fusion(pred[1024]{0:T(1024)(128)(4,1)S(1)} %broadcast_compare_fusion, bf16[512,1024]{1,0:T(8,128)(2,1)S(1)} %copy-done.1, bf16[1024]{0:T(1024)(128)(2,1)S(1)} %fusion.33, f32[512]{0:T(512)S(1)} %add_rsqrt_fusion, s32[512]{0:T(512)S(1)} %multiply_add_fusion), kind=kOutput, calls=%fused_computation.14 | convolution fusion | flops 1078460416 | bytes 3152896 | tf_op jit(solution)/shard_map/dot_general | solution.py:58
  6.8 11.5 %all-to-all-start = ((bf16[128,8,1024]{2,1,0:T(8,128)(2,1)}), bf16[128,8,1024]{2,1,0:T(8,128)(2,1)S(1)}, u32[]{:S(2)}, u32[]{:S(2)}) async-start(bf16[128,8,1024]{2,1,0:T(8,128)(2,1)} %select_bitcast_fusion), calls=%async_computation | async-start | bytes 4194304 | tf_op jit(solution)/shard_map/all_to_all | solution.py:62
  18.3 1.1 collective-permute-start
  19.5 2.4 %collective-permute-done = bf16[512,1024]{1,0:T(8,128)(2,1)} collective-permute-done((bf16[512,1024]{1,0:T(8,128)(2,1)S(1)}, bf16[512,1024]{1,0:T(8,128)(2,1)}, u32[]{:S(2)}, u32[]{:S(2)}) %collective-permute-start) | collective-permute-done | bytes 1048608 | tf_op jit(solution)/shard_map/ppermute | solution.py:37
  21.9 2.7 %fusion.43 = (f32[512,1024]{1,0:T(8,128)}, bf16[512,1024]{1,0:T(8,128)(2,1)S(1)}) fusion(bf16[512,1024]{1,0:T(8,128)(2,1)} %param.5, bf16[512,1024]{1,0:T(8,128)(2,1)} %collective-permute-done, pred[]{:T(512)S(6)} %eq.88), kind=kLoop, calls=%fused_computation.104 | loop fusion | flops 1048576 | bytes 5242881 | tf_op jit(solution)/shard_map/convert_element_type | solution.py:72
  24.9 23.7 %all-to-all-done = bf16[128,8,1024]{2,1,0:T(8,128)(2,1)S(1)} async-done(((bf16[128,8,1024]{2,1,0:T(8,128)(2,1)}), bf16[128,8,1024]{2,1,0:T(8,128)(2,1)S(1)}, u32[]{:S(2)}, u32[]{:S(2)}) %all-to-all-start) | async-done | bytes 2097184 | tf_op jit(solution)/shard_map/all_to_all | solution.py:62
  48.8 1.3 fusion.5
  50.6 0.8 convert_reduce_fusion
  51.6 1.3 fusion.36
  52.8 1.6 %dynamic_update_slice.6 = f32[512,1152]{1,0:T(8,128)} pad(f32[512,1024]{1,0:T(8,128)S(1)} %fusion.36, f32[]{:T(128)} %constant.147.clone.1), padding=0_0x0_128 | pad | bytes 4456452 | tf_op jit(solution)/shard_map/dynamic_update_slice | solution.py:95
  54.4 1.7 %dynamic_update_slice.7 = f32[512,1152]{1,0:T(8,128)} dynamic-update-slice(f32[512,1152]{1,0:T(8,128)} %dynamic_update_slice.6, f32[512,1]{1,0:T(8,128)S(1)} %copy.32, s32[]{:T(128)} %constant.146.clone.1, s32[]{:T(128)} %constant.160.clone.1) | dynamic-update-slice | bytes 4100 | tf_op jit(solution)/shard_map/dynamic_update_slice | solution.py:96
  56.1 1.3 dynamic-slice_bitcast_fusion.1
  57.5 1.3 collective-permute-start.1
  58.8 2.6 %collective-permute-done.1 = f32[8,32,1152]{2,1,0:T(8,128)} collective-permute-done((f32[8,32,1152]{2,1,0:T(8,128)S(1)}, f32[8,32,1152]{2,1,0:T(8,128)}, u32[]{:S(2)}, u32[]{:S(2)}) %collective-permute-start.1) | collective-permute-done | bytes 1179680 | tf_op jit(solution)/shard_map/ppermute | solution.py:100
  61.4 1.7 %bitcast_add_fusion.1 = f32[8,32,1152]{2,1,0:T(8,128)S(1)} fusion(f32[8,32,1152]{2,1,0:T(8,128)} %collective-permute-done.1, f32[2,8,32,1152]{3,2,1,0:T(8,128)} %bitcast.68, s32[]{:T(128)S(6)} %select_n.131), kind=kLoop, calls=%fused_computation.25 | loop fusion | flops 294912 | bytes 3538948 | tf_op jit(solution)/shard_map/add | solution.py:100
  63.2 0.9 constant_dynamic-slice_fusion.12
  64.4 1.3 collective-permute-start.3
  65.7 0.6 collective-permute-start.4
  66.3 1.7 %collective-permute-start.5 = (f32[1,32,1152]{2,1,0:T(8,128)}, f32[1,32,1152]{2,1,0:T(8,128)}, u32[]{:S(2)}, u32[]{:S(2)}) collective-permute-start(f32[1,32,1152]{2,1,0:T(8,128)} %get-tuple-element.21), channel_id=1, source_target_pairs={{0,4},{1,5},{2,6},{3,7},{4,0},{5,1},{6,2},{7,3},{8,12},{9,13},{10,... | collective-permute-start | bytes 442376 | tf_op jit(solution)/shard_map/ppermute | solution.py:106
  68.4 7.6 %collective-permute-done.2 = f32[1,32,1152]{2,1,0:T(8,128)S(1)} collective-permute-done((f32[1,32,1152]{2,1,0:T(8,128)S(1)}, f32[1,32,1152]{2,1,0:T(8,128)S(1)}, u32[]{:S(2)}, u32[]{:S(2)}) %collective-permute-start.2) | collective-permute-done | bytes 147488 | tf_op jit(solution)/shard_map/ppermute | solution.py:106
  76.1 0.9 collective-permute-done.4
  76.9 4.6 %collective-permute-done.5 = f32[1,32,1152]{2,1,0:T(8,128)} collective-permute-done((f32[1,32,1152]{2,1,0:T(8,128)}, f32[1,32,1152]{2,1,0:T(8,128)}, u32[]{:S(2)}, u32[]{:S(2)}) %collective-permute-start.5) | collective-permute-done | bytes 147488 | tf_op jit(solution)/shard_map/ppermute | solution.py:106
  82.2 1.3 add_add_fusion.1
  83.6 1.1 multiply_reduce_fusion.1
  85.2 11.9 %all_to_all.23 = bf16[8,32,1152]{2,1,0:T(8,128)(2,1)S(1)} all-to-all(bf16[8,32,1152]{2,1,0:T(8,128)(2,1)S(1)} %broadcast_in_dim.82), channel_id=1, replica_groups=mesh['z'=4,'core'=2,'yhi'=2,'ylo'=2,'x'=4] {'ylo','x'}, dimensions={0} | all-to-all | bytes 1179648 | tf_op jit(solution)/shard_map/all_to_all | solution.py:146
  97.1 3.7 %collective-permute-start.9 = (bf16[8,32,1152]{2,1,0:T(8,128)(2,1)S(1)}, bf16[8,32,1152]{2,1,0:T(8,128)(2,1)}, u32[]{:S(2)}, u32[]{:S(2)}) collective-permute-start(bf16[8,32,1152]{2,1,0:T(8,128)(2,1)S(1)} %all_to_all.23), channel_id=1, source_target_pairs={{0,16},{16,0},{1,17},{17,1},{2,18},{18,2},{3,19},{19,3},{4,20},{20... | collective-permute-start | bytes 1769480 | tf_op jit(solution)/shard_map/ppermute | solution.py:153
  100.9 3.1 %concatenate.12 = bf16[1024,1152]{1,0:T(8,128)(2,1)} concatenate(bf16[1024,1024]{1,0:T(8,128)(2,1)S(1)} %bitcast.66, bf16[1024,1]{1,0:T(8,128)(2,1)S(1)} %broadcast_in_dim.83, bf16[1024,127]{1,0:T(8,128)(2,1)S(1)} %broadcast_in_dim.84), dimensions={1} | concatenate | bytes 4718592 | tf_op jit(solution)/shard_map/concatenate | solution.py:64
  104.0 1.2 broadcast_select_fusion.2
  105.7 1.3 fusion.6
  107.0 0.5 fusion.8
  107.5 1.8 %fusion.9 = f32[512,1152]{1,0:T(8,128)S(1)} fusion(bf16[1024,1152]{1,0:T(8,128)(2,1)S(1)} %copy-done, f32[1024,512]{0,1:T(8,128)S(1)} %get-tuple-element.30, f32[1024]{0:T(1024)S(1)} %fusion.8, f32[1024]{0:T(1024)S(1)} %get-tuple-element.29, f32[512]{0:T(512)S(1)} %fusion.21, f32[1024]{0:T(1024)S(1)} %convert_reduce_fusion.2), kind=kOutput, calls=%fused_computation.28 | convolution fusion | flops 1211105280 | bytes 6830080 | tf_op jit(solution)/shard_map/rk,rd->kd/dot_general | solution.py:113
  109.5 2.8 %collective-permute-done.10 = f32[8,32,1152]{2,1,0:T(8,128)S(1)} collective-permute-done((f32[8,32,1152]{2,1,0:T(8,128)S(1)}, f32[8,32,1152]{2,1,0:T(8,128)S(1)}, u32[]{:S(2)}, u32[]{:S(2)}) %collective-permute-start.10) | collective-permute-done | bytes 1179680 | tf_op jit(solution)/shard_map/ppermute | solution.py:119
  112.6 0.5 collective-permute-start.11
  113.1 1.7 %collective-permute-start.12 = (f32[1,32,1152]{2,1,0:T(8,128)S(1)}, f32[1,32,1152]{2,1,0:T(8,128)S(1)}, u32[]{:S(2)}, u32[]{:S(2)}) collective-permute-start(f32[1,32,1152]{2,1,0:T(8,128)S(1)} %get-tuple-element.14), channel_id=1, source_target_pairs={{0,2},{1,3},{2,4},{3,5},{4,6},{5,7},{6,0},{7,1},{8,10},{9,11},{10,... | collective-permute-start | bytes 442376 | tf_op jit(solution)/shard_map/ppermute | solution.py:125
  114.8 0.8 collective-permute-start.13
  115.6 1.2 collective-permute-start.14
  116.8 0.8 collective-permute-start.15
  117.5 7.1 %collective-permute-done.11 = f32[1,32,1152]{2,1,0:T(8,128)S(1)} collective-permute-done((f32[1,32,1152]{2,1,0:T(8,128)S(1)}, f32[1,32,1152]{2,1,0:T(8,128)S(1)}, u32[]{:S(2)}, u32[]{:S(2)}) %collective-permute-start.11) | collective-permute-done | bytes 147488 | tf_op jit(solution)/shard_map/ppermute | solution.py:125
  124.8 18.5 %all_to_all.24 = f32[128,8,1]{1,2,0:T(1,128)S(1)} all-to-all(f32[128,8,1]{1,2,0:T(1,128)S(1)} %bitcast.75), channel_id=1, replica_groups=mesh['z'=4,'core'=2,'yhi'=2,'ylo'=2,'x'=4] {'z','yhi','core','ylo','x'}, dimensions={0} | all-to-all | bytes 8192 | tf_op jit(solution)/shard_map/all_to_all | solution.py:87
  143.3 0.5 broadcast.140
  143.8 0.8 reduce.11
  145.0 3.2 %collective-permute-start.18 = (f32[32,1024]{1,0:T(8,128)S(1)}, f32[32,1024]{1,0:T(8,128)S(1)}, u32[]{:S(2)}, u32[]{:S(2)}) collective-permute-start(f32[32,1024]{1,0:T(8,128)S(1)} %fusion.27), channel_id=1, source_target_pairs={{0,0},{8,16},{16,8},{24,24},{1,1},{9,17},{17,9},{25,25},{2,2},{10,... | collective-permute-start | bytes 393224 | tf_op jit(solution)/shard_map/ppermute | solution.py:166
  148.3 0.9 select_reduce_fusion
  149.2 3.7 %collective-permute-done.18 = f32[32,1024]{1,0:T(8,128)S(1)} collective-permute-done((f32[32,1024]{1,0:T(8,128)S(1)}, f32[32,1024]{1,0:T(8,128)S(1)}, u32[]{:S(2)}, u32[]{:S(2)}) %collective-permute-start.18) | collective-permute-done | bytes 131104 | tf_op jit(solution)/shard_map/ppermute | solution.py:166
  152.8 0.7 copy.39
  (64 shorter events, 5.3 us)
Async XLA Ops:
  0.6 3.1 %copy-start.1 = (bf16[512,1024]{1,0:T(8,128)(2,1)S(1)}, bf16[512,1024]{1,0:T(8,128)(2,1)}, u32[]{:S(2)}) copy-start(bf16[512,1024]{1,0:T(8,128)(2,1)} %param.3) | copy-start | bytes 3145732
  6.8 11.5 %copy-start.2 = (bf16[512,1024]{1,0:T(8,128)(2,1)S(1)}, bf16[512,1024]{1,0:T(8,128)(2,1)}, u32[]{:S(2)}) copy-start(bf16[512,1024]{1,0:T(8,128)(2,1)} %param.5) | copy-start | bytes 3145732
  6.8 41.8 %all-to-all-start = ((bf16[128,8,1024]{2,1,0:T(8,128)(2,1)}), bf16[128,8,1024]{2,1,0:T(8,128)(2,1)S(1)}, u32[]{:S(2)}, u32[]{:S(2)}) async-start(bf16[128,8,1024]{2,1,0:T(8,128)(2,1)} %select_bitcast_fusion), calls=%async_computation | async-start | bytes 4194304 | tf_op jit(solution)/shard_map/all_to_all | solution.py:62
  18.3 3.6 %collective-permute-start = (bf16[512,1024]{1,0:T(8,128)(2,1)S(1)}, bf16[512,1024]{1,0:T(8,128)(2,1)}, u32[]{:S(2)}, u32[]{:S(2)}) collective-permute-start(bf16[512,1024]{1,0:T(8,128)(2,1)S(1)} %copy-done.2), channel_id=1, source_target_pairs={{0,16},{16,0},{1,17},{17,1},{2,18},{18,2},{3,19},{19,3},{4,20},{20... | collective-permute-start | bytes 3145736 | tf_op jit(solution)/shard_map/ppermute | solution.py:37
  57.5 3.9 %collective-permute-start.1 = (f32[8,32,1152]{2,1,0:T(8,128)S(1)}, f32[8,32,1152]{2,1,0:T(8,128)}, u32[]{:S(2)}, u32[]{:S(2)}) collective-permute-start(f32[8,32,1152]{2,1,0:T(8,128)S(1)} %dynamic-slice_bitcast_fusion.1), channel_id=1, source_target_pairs={{0,16},{16,0},{1,17},{17,1},{2,18},{18,2},{3,19},{19,3},{4,20},{20... | collective-permute-start | bytes 3538952 | tf_op jit(solution)/shard_map/ppermute | solution.py:100
  64.1 11.9 %collective-permute-start.2 = (f32[1,32,1152]{2,1,0:T(8,128)S(1)}, f32[1,32,1152]{2,1,0:T(8,128)S(1)}, u32[]{:S(2)}, u32[]{:S(2)}) collective-permute-start(f32[1,32,1152]{2,1,0:T(8,128)S(1)} %get-tuple-element.17), channel_id=1, source_target_pairs={{0,1},{1,2},{2,3},{3,4},{4,5},{5,6},{6,7},{7,0},{8,9},{9,10},{10,1... | collective-permute-start | bytes 442376 | tf_op jit(solution)/shard_map/ppermute | solution.py:106
  64.4 11.7 %collective-permute-start.3 = (f32[1,32,1152]{2,1,0:T(8,128)S(1)}, f32[1,32,1152]{2,1,0:T(8,128)}, u32[]{:S(2)}, u32[]{:S(2)}) collective-permute-start(f32[1,32,1152]{2,1,0:T(8,128)S(1)} %get-tuple-element.23), channel_id=1, source_target_pairs={{0,2},{1,3},{2,4},{3,5},{4,6},{5,7},{6,0},{7,1},{8,10},{9,11},{10,... | collective-permute-start | bytes 442376 | tf_op jit(solution)/shard_map/ppermute | solution.py:106
  65.7 11.3 %collective-permute-start.4 = (f32[1,32,1152]{2,1,0:T(8,128)}, f32[1,32,1152]{2,1,0:T(8,128)}, u32[]{:S(2)}, u32[]{:S(2)}) collective-permute-start(f32[1,32,1152]{2,1,0:T(8,128)} %get-tuple-element.22), channel_id=1, source_target_pairs={{0,3},{1,4},{2,5},{3,6},{4,7},{5,0},{6,1},{7,2},{8,11},{9,12},{10,... | collective-permute-start | bytes 442376 | tf_op jit(solution)/shard_map/ppermute | solution.py:106
  66.3 15.2 %collective-permute-start.5 = (f32[1,32,1152]{2,1,0:T(8,128)}, f32[1,32,1152]{2,1,0:T(8,128)}, u32[]{:S(2)}, u32[]{:S(2)}) collective-permute-start(f32[1,32,1152]{2,1,0:T(8,128)} %get-tuple-element.21), channel_id=1, source_target_pairs={{0,4},{1,5},{2,6},{3,7},{4,0},{5,1},{6,2},{7,3},{8,12},{9,13},{10,... | collective-permute-start | bytes 442376 | tf_op jit(solution)/shard_map/ppermute | solution.py:106
  68.0 13.6 %collective-permute-start.6 = (f32[1,32,1152]{2,1,0:T(8,128)}, f32[1,32,1152]{2,1,0:T(8,128)}, u32[]{:S(2)}, u32[]{:S(2)}) collective-permute-start(f32[1,32,1152]{2,1,0:T(8,128)} %get-tuple-element.20), channel_id=1, source_target_pairs={{0,5},{1,6},{2,7},{3,0},{4,1},{5,2},{6,3},{7,4},{8,13},{9,14},{10,... | collective-permute-start | bytes 442376 | tf_op jit(solution)/shard_map/ppermute | solution.py:106
  76.0 5.8 %collective-permute-start.7 = (f32[1,32,1152]{2,1,0:T(8,128)}, f32[1,32,1152]{2,1,0:T(8,128)}, u32[]{:S(2)}, u32[]{:S(2)}) collective-permute-start(f32[1,32,1152]{2,1,0:T(8,128)} %get-tuple-element.19), channel_id=1, source_target_pairs={{0,6},{1,7},{2,0},{3,1},{4,2},{5,3},{6,4},{7,5},{8,14},{9,15},{10,... | collective-permute-start | bytes 442376 | tf_op jit(solution)/shard_map/ppermute | solution.py:106
  76.0 6.1 %collective-permute-start.8 = (f32[1,32,1152]{2,1,0:T(8,128)}, f32[1,32,1152]{2,1,0:T(8,128)}, u32[]{:S(2)}, u32[]{:S(2)}) collective-permute-start(f32[1,32,1152]{2,1,0:T(8,128)} %get-tuple-element.18), channel_id=1, source_target_pairs={{0,7},{1,0},{2,1},{3,2},{4,3},{5,4},{6,5},{7,6},{8,15},{9,8},{10,9... | collective-permute-start | bytes 442376 | tf_op jit(solution)/shard_map/ppermute | solution.py:106
  97.1 6.9 %collective-permute-start.9 = (bf16[8,32,1152]{2,1,0:T(8,128)(2,1)S(1)}, bf16[8,32,1152]{2,1,0:T(8,128)(2,1)}, u32[]{:S(2)}, u32[]{:S(2)}) collective-permute-start(bf16[8,32,1152]{2,1,0:T(8,128)(2,1)S(1)} %all_to_all.23), channel_id=1, source_target_pairs={{0,16},{16,0},{1,17},{17,1},{2,18},{18,2},{3,19},{19,3},{4,20},{20... | collective-permute-start | bytes 1769480 | tf_op jit(solution)/shard_map/ppermute | solution.py:153
  105.7 1.8 %copy-start = (bf16[1024,1152]{1,0:T(8,128)(2,1)S(1)}, bf16[1024,1152]{1,0:T(8,128)(2,1)}, u32[]{:S(2)}) copy-start(bf16[1024,1152]{1,0:T(8,128)(2,1)} %concatenate.12) | copy-start | bytes 7077892
  109.4 2.9 %collective-permute-start.10 = (f32[8,32,1152]{2,1,0:T(8,128)S(1)}, f32[8,32,1152]{2,1,0:T(8,128)S(1)}, u32[]{:S(2)}, u32[]{:S(2)}) collective-permute-start(f32[8,32,1152]{2,1,0:T(8,128)S(1)} %dynamic-slice_bitcast_fusion), channel_id=1, source_target_pairs={{0,16},{16,0},{1,17},{17,1},{2,18},{18,2},{3,19},{19,3},{4,20},{20... | collective-permute-start | bytes 3538952 | tf_op jit(solution)/shard_map/ppermute | solution.py:119
  112.6 12.1 %collective-permute-start.11 = (f32[1,32,1152]{2,1,0:T(8,128)S(1)}, f32[1,32,1152]{2,1,0:T(8,128)S(1)}, u32[]{:S(2)}, u32[]{:S(2)}) collective-permute-start(f32[1,32,1152]{2,1,0:T(8,128)S(1)} %get-tuple-element.8), channel_id=1, source_target_pairs={{0,1},{1,2},{2,3},{3,4},{4,5},{5,6},{6,7},{7,0},{8,9},{9,10},{10,1... | collective-permute-start | bytes 442376 | tf_op jit(solution)/shard_map/ppermute | solution.py:125
  113.1 11.6 %collective-permute-start.12 = (f32[1,32,1152]{2,1,0:T(8,128)S(1)}, f32[1,32,1152]{2,1,0:T(8,128)S(1)}, u32[]{:S(2)}, u32[]{:S(2)}) collective-permute-start(f32[1,32,1152]{2,1,0:T(8,128)S(1)} %get-tuple-element.14), channel_id=1, source_target_pairs={{0,2},{1,3},{2,4},{3,5},{4,6},{5,7},{6,0},{7,1},{8,10},{9,11},{10,... | collective-permute-start | bytes 442376 | tf_op jit(solution)/shard_map/ppermute | solution.py:125
  114.8 29.9 %collective-permute-start.13 = (f32[1,32,1152]{2,1,0:T(8,128)S(1)}, f32[1,32,1152]{2,1,0:T(8,128)S(1)}, u32[]{:S(2)}, u32[]{:S(2)}) collective-permute-start(f32[1,32,1152]{2,1,0:T(8,128)S(1)} %get-tuple-element.13), channel_id=1, source_target_pairs={{0,3},{1,4},{2,5},{3,6},{4,7},{5,0},{6,1},{7,2},{8,11},{9,12},{10,... | collective-permute-start | bytes 442376 | tf_op jit(solution)/shard_map/ppermute | solution.py:125
  115.6 29.1 %collective-permute-start.14 = (f32[1,32,1152]{2,1,0:T(8,128)S(1)}, f32[1,32,1152]{2,1,0:T(8,128)S(1)}, u32[]{:S(2)}, u32[]{:S(2)}) collective-permute-start(f32[1,32,1152]{2,1,0:T(8,128)S(1)} %get-tuple-element.12), channel_id=1, source_target_pairs={{0,4},{1,5},{2,6},{3,7},{4,0},{5,1},{6,2},{7,3},{8,12},{9,13},{10,... | collective-permute-start | bytes 442376 | tf_op jit(solution)/shard_map/ppermute | solution.py:125
  116.8 28.0 %collective-permute-start.15 = (f32[1,32,1152]{2,1,0:T(8,128)S(1)}, f32[1,32,1152]{2,1,0:T(8,128)S(1)}, u32[]{:S(2)}, u32[]{:S(2)}) collective-permute-start(f32[1,32,1152]{2,1,0:T(8,128)S(1)} %get-tuple-element.11), channel_id=1, source_target_pairs={{0,5},{1,6},{2,7},{3,0},{4,1},{5,2},{6,3},{7,4},{8,13},{9,14},{10,... | collective-permute-start | bytes 442376 | tf_op jit(solution)/shard_map/ppermute | solution.py:125
  124.7 20.1 %collective-permute-start.16 = (f32[1,32,1152]{2,1,0:T(8,128)S(1)}, f32[1,32,1152]{2,1,0:T(8,128)S(1)}, u32[]{:S(2)}, u32[]{:S(2)}) collective-permute-start(f32[1,32,1152]{2,1,0:T(8,128)S(1)} %get-tuple-element.10), channel_id=1, source_target_pairs={{0,6},{1,7},{2,0},{3,1},{4,2},{5,3},{6,4},{7,5},{8,14},{9,15},{10,... | collective-permute-start | bytes 442376 | tf_op jit(solution)/shard_map/ppermute | solution.py:125
  124.7 20.1 %collective-permute-start.17 = (f32[1,32,1152]{2,1,0:T(8,128)S(1)}, f32[1,32,1152]{2,1,0:T(8,128)S(1)}, u32[]{:S(2)}, u32[]{:S(2)}) collective-permute-start(f32[1,32,1152]{2,1,0:T(8,128)S(1)} %get-tuple-element.9), channel_id=1, source_target_pairs={{0,7},{1,0},{2,1},{3,2},{4,3},{5,4},{6,5},{7,6},{8,15},{9,8},{10,9... | collective-permute-start | bytes 442376 | tf_op jit(solution)/shard_map/ppermute | solution.py:125
  145.0 7.8 %collective-permute-start.18 = (f32[32,1024]{1,0:T(8,128)S(1)}, f32[32,1024]{1,0:T(8,128)S(1)}, u32[]{:S(2)}, u32[]{:S(2)}) collective-permute-start(f32[32,1024]{1,0:T(8,128)S(1)} %fusion.27), channel_id=1, source_target_pairs={{0,0},{8,16},{16,8},{24,24},{1,1},{9,17},{17,9},{25,25},{2,2},{10,... | collective-permute-start | bytes 393224 | tf_op jit(solution)/shard_map/ppermute | solution.py:166

commit v3 on v0

--- a/solution.py
+++ b/solution.py
@@ -20,6 +20,7 @@
 ROUTE = ("z", "yhi", "core", "ylo", "x")
 TEAM = ("core", "ylo", "x")
 PLANE = ("ylo", "x")
+SHIFT_ORDER = (4, 1, 7, 2, 6, 3, 5)
 
 
 def steps(embeddings, coarse_ids, centroid_seeds):
@@ -43,9 +44,10 @@
         / math.sqrt(features)
     ).astype(jnp.bfloat16)
     cluster_of = coarse_ids[:, 0]
-    order = jnp.arange(rows_dev, dtype=jnp.int32)
-    earlier_same = (cluster_of[None, :] == cluster_of[:, None]) & (order[None, :] < order[:, None])
-    row_rank = jnp.sum(earlier_same.astype(jnp.int32), axis=1)
+    onehot = (cluster_of[:, None] == jnp.arange(clusters, dtype=jnp.int32)[None, :]).astype(
+        jnp.int32
+    )
+    row_rank = jnp.sum((jnp.cumsum(onehot, axis=0) - onehot) * onehot, axis=1)
     slot_of = cluster_of * capacity + row_rank
     placement = (
         slot_of[None, :] == jnp.arange(clusters * capacity, dtype=jnp.int32)[:, None]
@@ -103,7 +105,7 @@
             theirs = lax.dynamic_index_in_dim(by_core, 1 - core, 0, keepdims=False)
             halves = mine + lax.ppermute(theirs, "core", [(0, 1), (1, 0)])
             reduced = lax.dynamic_index_in_dim(halves, spot, 0, keepdims=True)
-            for shift in range(1, plane):
+            for shift in SHIFT_ORDER:
                 outgoing = lax.dynamic_index_in_dim(halves, (spot + shift) % plane, 0, keepdims=True)
                 incoming = lax.ppermute(
                     outgoing, PLANE, [(i, (i + shift) % plane) for i in range(plane)]
@@ -120,7 +122,7 @@
             theirs = lax.dynamic_index_in_dim(by_core, 1 - core, 0, keepdims=False)
             halves = mine + lax.ppermute(theirs, "core", [(0, 1), (1, 0)])
             reduced = lax.dynamic_index_in_dim(halves, spot, 0, keepdims=True)
-            for shift in range(1, plane):
+            for shift in SHIFT_ORDER:
                 outgoing = lax.dynamic_index_in_dim(
                     halves, (spot + shift) % plane, 0, keepdims=True
                 )

time: 151 us -> 146 us (0.967)
  waiting for transfers between devices: 54.2 us -> 42.9 us
  starting transfers between devices: 30.6 us -> 39.8 us
    ppermute x14, waiting for transfers between devices: 19.2 us -> 7.89 us  [steps(): lax.ppermute(outgoing, PLANE, [(i, (i + shift) % plane) for i in range(pl...]
    ppermute x14, starting transfers between devices: 9.35 us -> 20.1 us  [steps(): lax.ppermute(outgoing, PLANE, [(i, (i + shift) % plane) for i in range(pl...]
    all_to_all x1, blocking collectives: 18.3 us -> 15.2 us  [steps(): lax.all_to_all(smoothing_scale * closing_log_partition, ROUTE, split_axis...]
    all_to_all x1, blocking collectives: 11.8 us -> 13.6 us  [steps(): lax.all_to_all(jnp.broadcast_to(block[None], (plane,) + block.shape), PLA...]
    ppermute x1, starting transfers between devices: 4 us -> 2.39 us  [steps(): partner_plane = lax.ppermute(on_plane, 'core', [(0, 1), (1, 0)])]
where the time goes in v3:
time: 146 us
  waiting for transfers between devices  42.9 us (29%)
  starting transfers between devices  39.8 us (27%)
  blocking collectives  28.8 us (20%)
  other arithmetic  14.4 us (10%)
  matrix products  9.77 us (7%)
  local copies, waits for them, and re-layouts  8.87 us (6%)
    all_to_all x1, waiting for transfers between devices, steps(): lax.all_to_all(packed, ROUTE, split_axis=0, concat_axis=0, tiled=True)  23.7 us
    ppermute x14, starting transfers between devices, steps(): lax.ppermute(outgoing, PLANE, [(i, (i + shift) % plane) for i in range(pl...  20.1 us
    all_to_all x1, blocking collectives, steps(): lax.all_to_all(smoothing_scale * closing_log_partition, ROUTE, split_axis...  15.2 us
    all_to_all x1, blocking collectives, steps(): lax.all_to_all(jnp.broadcast_to(block[None], (plane,) + block.shape), PLA...  13.6 us
    all_to_all x1, starting transfers between devices, steps(): lax.all_to_all(packed, ROUTE, split_axis=0, concat_axis=0, tiled=True)  11.5 us
    ppermute x14, waiting for transfers between devices, steps(): lax.ppermute(outgoing, PLANE, [(i, (i + shift) % plane) for i in range(pl...  7.89 us
    ppermute x2, waiting for transfers between devices, steps(): halves = mine + lax.ppermute(theirs, 'core', [(0, 1), (1, 0)])  5.26 us
    ppermute x1, waiting for transfers between devices, steps(): lax.ppermute(own, ('core', 'yhi'), [(0, 0), (1, 2), (2, 1), (3, 3)])  3.65 us
  transfers between devices with their start and end apart: 20, of which 10 were waited for; matrix products, arithmetic and copies ran while one was open for 6% of the time, Pallas kernels for 0%

profile of v3, /device:TPU:1, one launch (start us, length us, event | category | flops | bytes accessed | tf_op | source)
XLA Modules:
  0.0 145.5 jit_solution(15161662879929982258)
XLA Ops:
  0.7 0.9 copy.27
  1.8 0.9 fusion.28
  2.8 0.7 multiply_add_fusion
  4.1 2.7 %select_bitcast_fusion = bf16[128,8,1024]{2,1,0:T(8,128)(2,1)} fusion(pred[1024]{0:T(1024)(128)(4,1)S(1)} %broadcast_compare_fusion, bf16[512,1024]{1,0:T(8,128)(2,1)S(1)} %copy-done.3, bf16[1024]{0:T(1024)(128)(2,1)S(1)} %fusion.35, f32[512]{0:T(512)S(1)} %add_rsqrt_fusion, s32[512]{0:T(512)S(1)} %multiply_add_fusion), kind=kOutput, calls=%fused_computation.16 | convolution fusion | flops 1078460416 | bytes 3152896 | tf_op jit(solution)/shard_map/dot_general | solution.py:59
  6.8 11.5 %all-to-all-start = ((bf16[128,8,1024]{2,1,0:T(8,128)(2,1)}), bf16[128,8,1024]{2,1,0:T(8,128)(2,1)S(1)}, u32[]{:S(2)}, u32[]{:S(2)}) async-start(bf16[128,8,1024]{2,1,0:T(8,128)(2,1)} %select_bitcast_fusion), calls=%async_computation | async-start | bytes 4194304 | tf_op jit(solution)/shard_map/all_to_all | solution.py:63
  18.3 1.1 collective-permute-start
  19.4 2.4 %collective-permute-done = bf16[512,1024]{1,0:T(8,128)(2,1)} collective-permute-done((bf16[512,1024]{1,0:T(8,128)(2,1)S(1)}, bf16[512,1024]{1,0:T(8,128)(2,1)}, u32[]{:S(2)}, u32[]{:S(2)}) %collective-permute-start) | collective-permute-done | bytes 1048608 | tf_op jit(solution)/shard_map/ppermute | solution.py:38
  21.9 2.8 %fusion.45 = (f32[512,1024]{1,0:T(8,128)}, bf16[512,1024]{1,0:T(8,128)(2,1)S(1)}) fusion(bf16[512,1024]{1,0:T(8,128)(2,1)} %param.5, bf16[512,1024]{1,0:T(8,128)(2,1)} %collective-permute-done, pred[]{:T(512)S(6)} %eq.88), kind=kLoop, calls=%fused_computation.111 | loop fusion | flops 1048576 | bytes 5242881 | tf_op jit(solution)/shard_map/convert_element_type | solution.py:73
  24.9 23.7 %all-to-all-done = bf16[128,8,1024]{2,1,0:T(8,128)(2,1)S(1)} async-done(((bf16[128,8,1024]{2,1,0:T(8,128)(2,1)}), bf16[128,8,1024]{2,1,0:T(8,128)(2,1)S(1)}, u32[]{:S(2)}, u32[]{:S(2)}) %all-to-all-start) | async-done | bytes 2097184 | tf_op jit(solution)/shard_map/all_to_all | solution.py:63
  48.7 1.3 fusion.5
  50.0 0.5 fusion.7
  50.5 0.8 convert_reduce_fusion
  51.3 2.6 %fusion.39 = f32[512,1024]{1,0:T(8,128)} fusion(bf16[1024,512]{0,1:T(8,128)(2,1)S(1)} %get-tuple-element.7, bf16[128,8,1024]{2,1,0:T(8,128)(2,1)S(1)} %all-to-all-done), kind=kOutput, calls=%fused_computation.105 | convolution fusion | flops 1073741824 | bytes 5242880 | tf_op jit(solution)/shard_map/rk,rd->kd/dot_general | solution.py:93
  53.9 1.7 %concatenate.18 = f32[2,8,32768]{2,1,0:T(8,128)S(1)} reshape(f32[512,1024]{1,0:T(8,128)} %fusion.39) | data formatting | bytes 4194304 | tf_op jit(solution)/shard_map/concatenate | solution.py:95
  55.9 1.3 collective-permute-start.1
  57.2 2.4 %collective-permute-done.1 = f32[8,32896]{1,0:T(8,128)} collective-permute-done((f32[8,32896]{1,0:T(8,128)S(1)}, f32[8,32896]{1,0:T(8,128)}, u32[]{:S(2)}, u32[]{:S(2)}) %collective-permute-start.1) | collective-permute-done | bytes 1052704 | tf_op jit(solution)/shard_map/ppermute | solution.py:106
  59.6 1.3 fusion.13
  61.0 0.6 constant_dynamic-slice_fusion.12
  61.7 0.4 collective-permute-start.3
  62.1 3.3 %collective-permute-start.4 = (f32[1,32896]{1,0:T(1,128)S(1)}, f32[1,32896]{1,0:T(1,128)S(1)}, u32[]{:S(2)}, u32[]{:S(2)}) collective-permute-start(f32[1,32896]{1,0:T(1,128)S(1)} %get-tuple-element.22), channel_id=1, source_target_pairs={{0,7},{1,0},{2,1},{3,2},{4,3},{5,4},{6,5},{7,6},{8,15},{9,8},{10,9... | collective-permute-start | bytes 394760 | tf_op jit(solution)/shard_map/ppermute | solution.py:110
  65.4 3.9 %collective-permute-start.6 = (f32[1,32896]{1,0:T(1,128)S(1)}, f32[1,32896]{1,0:T(1,128)S(1)}, u32[]{:S(2)}, u32[]{:S(2)}) collective-permute-start(f32[1,32896]{1,0:T(1,128)S(1)} %get-tuple-element.20), channel_id=1, source_target_pairs={{0,6},{1,7},{2,0},{3,1},{4,2},{5,3},{6,4},{7,5},{8,14},{9,15},{10,... | collective-permute-start | bytes 394760 | tf_op jit(solution)/shard_map/ppermute | solution.py:110
  69.2 2.4 %collective-permute-start.8 = (f32[1,32896]{1,0:T(1,128)S(1)}, f32[1,32896]{1,0:T(1,128)S(1)}, u32[]{:S(2)}, u32[]{:S(2)}) collective-permute-start(f32[1,32896]{1,0:T(1,128)S(1)} %get-tuple-element.18), channel_id=1, source_target_pairs={{0,5},{1,6},{2,7},{3,0},{4,1},{5,2},{6,3},{7,4},{8,13},{9,14},{10,... | collective-permute-start | bytes 394760 | tf_op jit(solution)/shard_map/ppermute | solution.py:110
  71.6 1.8 %collective-permute-done.4 = f32[1,32896]{1,0:T(1,128)S(1)} collective-permute-done((f32[1,32896]{1,0:T(1,128)S(1)}, f32[1,32896]{1,0:T(1,128)S(1)}, u32[]{:S(2)}, u32[]{:S(2)}) %collective-permute-start.4) | collective-permute-done | bytes 131616 | tf_op jit(solution)/shard_map/ppermute | solution.py:110
  73.4 1.3 collective-permute-done.6
  74.6 1.7 %collective-permute-done.7 = f32[1,32896]{1,0:T(1,128)S(1)} collective-permute-done((f32[1,32896]{1,0:T(1,128)S(1)}, f32[1,32896]{1,0:T(1,128)S(1)}, u32[]{:S(2)}, u32[]{:S(2)}) %collective-permute-start.7) | collective-permute-done | bytes 131616 | tf_op jit(solution)/shard_map/ppermute | solution.py:110
  76.3 2.4 %collective-permute-done.8 = f32[1,32896]{1,0:T(1,128)S(1)} collective-permute-done((f32[1,32896]{1,0:T(1,128)S(1)}, f32[1,32896]{1,0:T(1,128)S(1)}, u32[]{:S(2)}, u32[]{:S(2)}) %collective-permute-start.8) | collective-permute-done | bytes 131616 | tf_op jit(solution)/shard_map/ppermute | solution.py:110
  78.8 0.5 add_add_fusion.1
  79.6 1.3 multiply_reduce_fusion.1
  81.4 13.6 %all_to_all.23 = bf16[8,32,1152]{2,1,0:T(8,128)(2,1)S(1)} all-to-all(bf16[8,32,1152]{2,1,0:T(8,128)(2,1)S(1)} %broadcast_in_dim.77), channel_id=1, replica_groups=mesh['z'=4,'core'=2,'yhi'=2,'ylo'=2,'x'=4] {'ylo','x'}, dimensions={0} | all-to-all | bytes 1179648 | tf_op jit(solution)/shard_map/all_to_all | solution.py:150
  95.0 2.4 %collective-permute-start.9 = (bf16[8,32,1152]{2,1,0:T(8,128)(2,1)S(1)}, bf16[8,32,1152]{2,1,0:T(8,128)(2,1)}, u32[]{:S(2)}, u32[]{:S(2)}) collective-permute-start(bf16[8,32,1152]{2,1,0:T(8,128)(2,1)S(1)} %all_to_all.23), channel_id=1, source_target_pairs={{0,16},{16,0},{1,17},{17,1},{2,18},{18,2},{3,19},{19,3},{4,20},{20... | collective-permute-start | bytes 1769480 | tf_op jit(solution)/shard_map/ppermute | solution.py:157
  97.5 3.1 %concatenate.23 = bf16[1024,1152]{1,0:T(8,128)(2,1)} concatenate(bf16[1024,1024]{1,0:T(8,128)(2,1)S(1)} %bitcast.63, bf16[1024,1]{1,0:T(8,128)(2,1)S(1)} %broadcast_in_dim.78, bf16[1024,127]{1,0:T(8,128)(2,1)S(1)} %broadcast_in_dim.79), dimensions={1} | concatenate | bytes 4718592 | tf_op jit(solution)/shard_map/concatenate | solution.py:65
  100.6 1.2 broadcast_select_fusion.2
  102.2 1.3 fusion.6
  103.5 0.5 fusion.8
  104.0 1.8 %fusion.14 = f32[512,1152]{1,0:T(8,128)S(1)} fusion(bf16[1024,1152]{1,0:T(8,128)(2,1)S(1)} %copy-done.2, f32[1024,512]{0,1:T(8,128)S(1)} %get-tuple-element.30, f32[1024]{0:T(1024)S(1)} %fusion.8, f32[1024]{0:T(1024)S(1)} %get-tuple-element.29, f32[512]{0:T(512)S(1)} %fusion.26, f32[1024]{0:T(1024)S(1)} %convert_reduce_fusion.2), kind=kOutput, calls=%fused_computation.35 | convolution fusion | flops 1211105280 | bytes 6830080 | tf_op jit(solution)/shard_map/rk,rd->kd/dot_general | solution.py:117
  106.1 2.8 %collective-permute-done.10 = f32[8,32,1152]{2,1,0:T(8,128)S(1)} collective-permute-done((f32[8,32,1152]{2,1,0:T(8,128)S(1)}, f32[8,32,1152]{2,1,0:T(8,128)S(1)}, u32[]{:S(2)}, u32[]{:S(2)}) %collective-permute-start.10) | collective-permute-done | bytes 1179680 | tf_op jit(solution)/shard_map/ppermute | solution.py:123
  109.5 0.5 collective-permute-start.12
  109.9 3.1 %collective-permute-start.13 = (f32[1,32,1152]{2,1,0:T(8,128)S(1)}, f32[1,32,1152]{2,1,0:T(8,128)S(1)}, u32[]{:S(2)}, u32[]{:S(2)}) collective-permute-start(f32[1,32,1152]{2,1,0:T(8,128)S(1)} %get-tuple-element.13), channel_id=1, source_target_pairs={{0,7},{1,0},{2,1},{3,2},{4,3},{5,4},{6,5},{7,6},{8,15},{9,8},{10,9... | collective-permute-start | bytes 442376 | tf_op jit(solution)/shard_map/ppermute | solution.py:129
  113.1 3.9 %collective-permute-start.15 = (f32[1,32,1152]{2,1,0:T(8,128)S(1)}, f32[1,32,1152]{2,1,0:T(8,128)S(1)}, u32[]{:S(2)}, u32[]{:S(2)}) collective-permute-start(f32[1,32,1152]{2,1,0:T(8,128)S(1)} %get-tuple-element.11), channel_id=1, source_target_pairs={{0,6},{1,7},{2,0},{3,1},{4,2},{5,3},{6,4},{7,5},{8,14},{9,15},{10,... | collective-permute-start | bytes 442376 | tf_op jit(solution)/shard_map/ppermute | solution.py:129
  116.9 0.7 collective-permute-done.11
  117.6 2.4 %collective-permute-start.17 = (f32[1,32,1152]{2,1,0:T(8,128)S(1)}, f32[1,32,1152]{2,1,0:T(8,128)S(1)}, u32[]{:S(2)}, u32[]{:S(2)}) collective-permute-start(f32[1,32,1152]{2,1,0:T(8,128)S(1)} %get-tuple-element.9), channel_id=1, source_target_pairs={{0,5},{1,6},{2,7},{3,0},{4,1},{5,2},{6,3},{7,4},{8,13},{9,14},{10,... | collective-permute-start | bytes 442376 | tf_op jit(solution)/shard_map/ppermute | solution.py:129
  120.1 15.2 %all_to_all.24 = f32[128,8,1]{1,2,0:T(1,128)S(1)} all-to-all(f32[128,8,1]{1,2,0:T(1,128)S(1)} %bitcast.70), channel_id=1, replica_groups=mesh['z'=4,'core'=2,'yhi'=2,'ylo'=2,'x'=4] {'z','yhi','core','ylo','x'}, dimensions={0} | all-to-all | bytes 8192 | tf_op jit(solution)/shard_map/all_to_all | solution.py:88
  135.3 0.5 broadcast.145
  135.8 0.8 reduce.13
  137.1 3.2 %collective-permute-start.18 = (f32[32,1024]{1,0:T(8,128)S(1)}, f32[32,1024]{1,0:T(8,128)S(1)}, u32[]{:S(2)}, u32[]{:S(2)}) collective-permute-start(f32[32,1024]{1,0:T(8,128)S(1)} %fusion.32), channel_id=1, source_target_pairs={{0,0},{8,16},{16,8},{24,24},{1,1},{9,17},{17,9},{25,25},{2,2},{10,... | collective-permute-start | bytes 393224 | tf_op jit(solution)/shard_map/ppermute | solution.py:170
  140.3 0.9 select_reduce_fusion
  141.2 3.7 %collective-permute-done.18 = f32[32,1024]{1,0:T(8,128)S(1)} collective-permute-done((f32[32,1024]{1,0:T(8,128)S(1)}, f32[32,1024]{1,0:T(8,128)S(1)}, u32[]{:S(2)}, u32[]{:S(2)}) %collective-permute-start.18) | collective-permute-done | bytes 131104 | tf_op jit(solution)/shard_map/ppermute | solution.py:170
  144.9 0.7 copy.34
  (70 shorter events, 4.2 us)
Async XLA Ops:
  0.6 3.1 %copy-start.3 = (bf16[512,1024]{1,0:T(8,128)(2,1)S(1)}, bf16[512,1024]{1,0:T(8,128)(2,1)}, u32[]{:S(2)}) copy-start(bf16[512,1024]{1,0:T(8,128)(2,1)} %param.3) | copy-start | bytes 3145732
  6.8 11.5 %copy-start.4 = (bf16[512,1024]{1,0:T(8,128)(2,1)S(1)}, bf16[512,1024]{1,0:T(8,128)(2,1)}, u32[]{:S(2)}) copy-start(bf16[512,1024]{1,0:T(8,128)(2,1)} %param.5) | copy-start | bytes 3145732
  6.8 41.8 %all-to-all-start = ((bf16[128,8,1024]{2,1,0:T(8,128)(2,1)}), bf16[128,8,1024]{2,1,0:T(8,128)(2,1)S(1)}, u32[]{:S(2)}, u32[]{:S(2)}) async-start(bf16[128,8,1024]{2,1,0:T(8,128)(2,1)} %select_bitcast_fusion), calls=%async_computation | async-start | bytes 4194304 | tf_op jit(solution)/shard_map/all_to_all | solution.py:63
  18.3 3.6 %collective-permute-start = (bf16[512,1024]{1,0:T(8,128)(2,1)S(1)}, bf16[512,1024]{1,0:T(8,128)(2,1)}, u32[]{:S(2)}, u32[]{:S(2)}) collective-permute-start(bf16[512,1024]{1,0:T(8,128)(2,1)S(1)} %copy-done.4), channel_id=1, source_target_pairs={{0,16},{16,0},{1,17},{17,1},{2,18},{18,2},{3,19},{19,3},{4,20},{20... | collective-permute-start | bytes 3145736 | tf_op jit(solution)/shard_map/ppermute | solution.py:38
  48.6 2.8 %copy-start = (bf16[128,8,1024]{2,1,0:T(8,128)(2,1)}, bf16[128,8,1024]{2,1,0:T(8,128)(2,1)S(1)}, u32[]{:S(2)}) copy-start(bf16[128,8,1024]{2,1,0:T(8,128)(2,1)S(1)} %all-to-all-done) | copy-start | bytes 6291460
  55.9 3.8 %collective-permute-start.1 = (f32[8,32896]{1,0:T(8,128)S(1)}, f32[8,32896]{1,0:T(8,128)}, u32[]{:S(2)}, u32[]{:S(2)}) collective-permute-start(f32[8,32896]{1,0:T(8,128)S(1)} %fusion.10), channel_id=1, source_target_pairs={{0,16},{16,0},{1,17},{17,1},{2,18},{18,2},{3,19},{19,3},{4,20},{20... | collective-permute-start | bytes 3158024 | tf_op jit(solution)/shard_map/ppermute | solution.py:106
  61.6 7.6 %collective-permute-start.2 = (f32[1,32896]{1,0:T(1,128)S(1)}, f32[1,32896]{1,0:T(1,128)S(1)}, u32[]{:S(2)}, u32[]{:S(2)}) collective-permute-start(f32[1,32896]{1,0:T(1,128)S(1)} %get-tuple-element.17), channel_id=1, source_target_pairs={{0,4},{1,5},{2,6},{3,7},{4,0},{5,1},{6,2},{7,3},{8,12},{9,13},{10,... | collective-permute-start | bytes 394760 | tf_op jit(solution)/shard_map/ppermute | solution.py:110
  61.7 7.5 %collective-permute-start.3 = (f32[1,32896]{1,0:T(1,128)S(1)}, f32[1,32896]{1,0:T(1,128)S(1)}, u32[]{:S(2)}, u32[]{:S(2)}) collective-permute-start(f32[1,32896]{1,0:T(1,128)S(1)} %get-tuple-element.23), channel_id=1, source_target_pairs={{0,1},{1,2},{2,3},{3,4},{4,5},{5,6},{6,7},{7,0},{8,9},{9,10},{10,1... | collective-permute-start | bytes 394760 | tf_op jit(solution)/shard_map/ppermute | solution.py:110
  62.1 11.3 %collective-permute-start.4 = (f32[1,32896]{1,0:T(1,128)S(1)}, f32[1,32896]{1,0:T(1,128)S(1)}, u32[]{:S(2)}, u32[]{:S(2)}) collective-permute-start(f32[1,32896]{1,0:T(1,128)S(1)} %get-tuple-element.22), channel_id=1, source_target_pairs={{0,7},{1,0},{2,1},{3,2},{4,3},{5,4},{6,5},{7,6},{8,15},{9,8},{10,9... | collective-permute-start | bytes 394760 | tf_op jit(solution)/shard_map/ppermute | solution.py:110
  65.4 8.0 %collective-permute-start.5 = (f32[1,32896]{1,0:T(1,128)S(1)}, f32[1,32896]{1,0:T(1,128)S(1)}, u32[]{:S(2)}, u32[]{:S(2)}) collective-permute-start(f32[1,32896]{1,0:T(1,128)S(1)} %get-tuple-element.21), channel_id=1, source_target_pairs={{0,2},{1,3},{2,4},{3,5},{4,6},{5,7},{6,0},{7,1},{8,10},{9,11},{10,... | collective-permute-start | bytes 394760 | tf_op jit(solution)/shard_map/ppermute | solution.py:110
  65.4 9.3 %collective-permute-start.6 = (f32[1,32896]{1,0:T(1,128)S(1)}, f32[1,32896]{1,0:T(1,128)S(1)}, u32[]{:S(2)}, u32[]{:S(2)}) collective-permute-start(f32[1,32896]{1,0:T(1,128)S(1)} %get-tuple-element.20), channel_id=1, source_target_pairs={{0,6},{1,7},{2,0},{3,1},{4,2},{5,3},{6,4},{7,5},{8,14},{9,15},{10,... | collective-permute-start | bytes 394760 | tf_op jit(solution)/shard_map/ppermute | solution.py:110
  69.2 7.1 %collective-permute-start.7 = (f32[1,32896]{1,0:T(1,128)S(1)}, f32[1,32896]{1,0:T(1,128)S(1)}, u32[]{:S(2)}, u32[]{:S(2)}) collective-permute-start(f32[1,32896]{1,0:T(1,128)S(1)} %get-tuple-element.19), channel_id=1, source_target_pairs={{0,3},{1,4},{2,5},{3,6},{4,7},{5,0},{6,1},{7,2},{8,11},{9,12},{10,... | collective-permute-start | bytes 394760 | tf_op jit(solution)/shard_map/ppermute | solution.py:110
  69.2 9.5 %collective-permute-start.8 = (f32[1,32896]{1,0:T(1,128)S(1)}, f32[1,32896]{1,0:T(1,128)S(1)}, u32[]{:S(2)}, u32[]{:S(2)}) collective-permute-start(f32[1,32896]{1,0:T(1,128)S(1)} %get-tuple-element.18), channel_id=1, source_target_pairs={{0,5},{1,6},{2,7},{3,0},{4,1},{5,2},{6,3},{7,4},{8,13},{9,14},{10,... | collective-permute-start | bytes 394760 | tf_op jit(solution)/shard_map/ppermute | solution.py:110
  79.2 18.2 %copy-start.1 = (bf16[128,8,1024]{2,1,0:T(8,128)(2,1)S(1)}, bf16[128,8,1024]{2,1,0:T(8,128)(2,1)}, u32[]{:S(2)}) copy-start(bf16[128,8,1024]{2,1,0:T(8,128)(2,1)} %copy-done) | copy-start | bytes 6291460
  95.0 5.5 %collective-permute-start.9 = (bf16[8,32,1152]{2,1,0:T(8,128)(2,1)S(1)}, bf16[8,32,1152]{2,1,0:T(8,128)(2,1)}, u32[]{:S(2)}, u32[]{:S(2)}) collective-permute-start(bf16[8,32,1152]{2,1,0:T(8,128)(2,1)S(1)} %all_to_all.23), channel_id=1, source_target_pairs={{0,16},{16,0},{1,17},{17,1},{2,18},{18,2},{3,19},{19,3},{4,20},{20... | collective-permute-start | bytes 1769480 | tf_op jit(solution)/shard_map/ppermute | solution.py:157
  102.2 1.8 %copy-start.2 = (bf16[1024,1152]{1,0:T(8,128)(2,1)S(1)}, bf16[1024,1152]{1,0:T(8,128)(2,1)}, u32[]{:S(2)}) copy-start(bf16[1024,1152]{1,0:T(8,128)(2,1)} %concatenate.23) | copy-start | bytes 7077892
  106.0 2.9 %collective-permute-start.10 = (f32[8,32,1152]{2,1,0:T(8,128)S(1)}, f32[8,32,1152]{2,1,0:T(8,128)S(1)}, u32[]{:S(2)}, u32[]{:S(2)}) collective-permute-start(f32[8,32,1152]{2,1,0:T(8,128)S(1)} %dynamic-slice_bitcast_fusion), channel_id=1, source_target_pairs={{0,16},{16,0},{1,17},{17,1},{2,18},{18,2},{3,19},{19,3},{4,20},{20... | collective-permute-start | bytes 3538952 | tf_op jit(solution)/shard_map/ppermute | solution.py:123
  109.1 8.5 %collective-permute-start.11 = (f32[1,32,1152]{2,1,0:T(8,128)S(1)}, f32[1,32,1152]{2,1,0:T(8,128)S(1)}, u32[]{:S(2)}, u32[]{:S(2)}) collective-permute-start(f32[1,32,1152]{2,1,0:T(8,128)S(1)} %get-tuple-element.8), channel_id=1, source_target_pairs={{0,4},{1,5},{2,6},{3,7},{4,0},{5,1},{6,2},{7,3},{8,12},{9,13},{10,... | collective-permute-start | bytes 442376 | tf_op jit(solution)/shard_map/ppermute | solution.py:129
  109.5 8.2 %collective-permute-start.12 = (f32[1,32,1152]{2,1,0:T(8,128)S(1)}, f32[1,32,1152]{2,1,0:T(8,128)S(1)}, u32[]{:S(2)}, u32[]{:S(2)}) collective-permute-start(f32[1,32,1152]{2,1,0:T(8,128)S(1)} %get-tuple-element.14), channel_id=1, source_target_pairs={{0,1},{1,2},{2,3},{3,4},{4,5},{5,6},{6,7},{7,0},{8,9},{9,10},{10,1... | collective-permute-start | bytes 442376 | tf_op jit(solution)/shard_map/ppermute | solution.py:129
  109.9 26.8 %collective-permute-start.13 = (f32[1,32,1152]{2,1,0:T(8,128)S(1)}, f32[1,32,1152]{2,1,0:T(8,128)S(1)}, u32[]{:S(2)}, u32[]{:S(2)}) collective-permute-start(f32[1,32,1152]{2,1,0:T(8,128)S(1)} %get-tuple-element.13), channel_id=1, source_target_pairs={{0,7},{1,0},{2,1},{3,2},{4,3},{5,4},{6,5},{7,6},{8,15},{9,8},{10,9... | collective-permute-start | bytes 442376 | tf_op jit(solution)/shard_map/ppermute | solution.py:129
  113.1 23.7 %collective-permute-start.14 = (f32[1,32,1152]{2,1,0:T(8,128)S(1)}, f32[1,32,1152]{2,1,0:T(8,128)S(1)}, u32[]{:S(2)}, u32[]{:S(2)}) collective-permute-start(f32[1,32,1152]{2,1,0:T(8,128)S(1)} %get-tuple-element.12), channel_id=1, source_target_pairs={{0,2},{1,3},{2,4},{3,5},{4,6},{5,7},{6,0},{7,1},{8,10},{9,11},{10,... | collective-permute-start | bytes 442376 | tf_op jit(solution)/shard_map/ppermute | solution.py:129
  113.1 23.7 %collective-permute-start.15 = (f32[1,32,1152]{2,1,0:T(8,128)S(1)}, f32[1,32,1152]{2,1,0:T(8,128)S(1)}, u32[]{:S(2)}, u32[]{:S(2)}) collective-permute-start(f32[1,32,1152]{2,1,0:T(8,128)S(1)} %get-tuple-element.11), channel_id=1, source_target_pairs={{0,6},{1,7},{2,0},{3,1},{4,2},{5,3},{6,4},{7,5},{8,14},{9,15},{10,... | collective-permute-start | bytes 442376 | tf_op jit(solution)/shard_map/ppermute | solution.py:129
  117.6 19.1 %collective-permute-start.16 = (f32[1,32,1152]{2,1,0:T(8,128)S(1)}, f32[1,32,1152]{2,1,0:T(8,128)S(1)}, u32[]{:S(2)}, u32[]{:S(2)}) collective-permute-start(f32[1,32,1152]{2,1,0:T(8,128)S(1)} %get-tuple-element.10), channel_id=1, source_target_pairs={{0,3},{1,4},{2,5},{3,6},{4,7},{5,0},{6,1},{7,2},{8,11},{9,12},{10,... | collective-permute-start | bytes 442376 | tf_op jit(solution)/shard_map/ppermute | solution.py:129
  117.6 19.1 %collective-permute-start.17 = (f32[1,32,1152]{2,1,0:T(8,128)S(1)}, f32[1,32,1152]{2,1,0:T(8,128)S(1)}, u32[]{:S(2)}, u32[]{:S(2)}) collective-permute-start(f32[1,32,1152]{2,1,0:T(8,128)S(1)} %get-tuple-element.9), channel_id=1, source_target_pairs={{0,5},{1,6},{2,7},{3,0},{4,1},{5,2},{6,3},{7,4},{8,13},{9,14},{10,... | collective-permute-start | bytes 442376 | tf_op jit(solution)/shard_map/ppermute | solution.py:129
  137.1 7.8 %collective-permute-start.18 = (f32[32,1024]{1,0:T(8,128)S(1)}, f32[32,1024]{1,0:T(8,128)S(1)}, u32[]{:S(2)}, u32[]{:S(2)}) collective-permute-start(f32[32,1024]{1,0:T(8,128)S(1)} %fusion.32), channel_id=1, source_target_pairs={{0,0},{8,16},{16,8},{24,24},{1,1},{9,17},{17,9},{25,25},{2,2},{10,... | collective-permute-start | bytes 393224 | tf_op jit(solution)/shard_map/ppermute | solution.py:170

commit v4 on v3

--- a/solution.py
+++ b/solution.py
@@ -20,7 +20,6 @@
 ROUTE = ("z", "yhi", "core", "ylo", "x")
 TEAM = ("core", "ylo", "x")
 PLANE = ("ylo", "x")
-SHIFT_ORDER = (4, 1, 7, 2, 6, 3, 5)
 
 
 def steps(embeddings, coarse_ids, centroid_seeds):
@@ -105,7 +104,7 @@
             theirs = lax.dynamic_index_in_dim(by_core, 1 - core, 0, keepdims=False)
             halves = mine + lax.ppermute(theirs, "core", [(0, 1), (1, 0)])
             reduced = lax.dynamic_index_in_dim(halves, spot, 0, keepdims=True)
-            for shift in SHIFT_ORDER:
+            for shift in range(1, plane):
                 outgoing = lax.dynamic_index_in_dim(halves, (spot + shift) % plane, 0, keepdims=True)
                 incoming = lax.ppermute(
                     outgoing, PLANE, [(i, (i + shift) % plane) for i in range(plane)]
@@ -118,11 +117,11 @@
                 "rk,rd->kd", weights, widened_rows, preferred_element_type=jnp.float32
             )
             by_core = weighted.reshape(cores, plane, share_rows, features + 128)
-            mine = lax.dynamic_index_in_dim(by_core, core, 0, keepdims=False)
-            theirs = lax.dynamic_index_in_dim(by_core, 1 - core, 0, keepdims=False)
+            mine = by_core[0]
+            theirs = by_core[1]
             halves = mine + lax.ppermute(theirs, "core", [(0, 1), (1, 0)])
             reduced = lax.dynamic_index_in_dim(halves, spot, 0, keepdims=True)
-            for shift in SHIFT_ORDER:
+            for shift in range(1, plane):
                 outgoing = lax.dynamic_index_in_dim(
                     halves, (spot + shift) % plane, 0, keepdims=True
                 )
@@ -155,13 +154,9 @@
                 tiled=True,
             )
             partner_plane = lax.ppermute(on_plane, "core", [(0, 1), (1, 0)])
-            everyone = jnp.concatenate(
-                [
-                    jnp.where(core == 0, on_plane, partner_plane),
-                    jnp.where(core == 0, partner_plane, on_plane),
-                ],
-                axis=0,
-            ).reshape(K, features + 128)
+            everyone = jnp.concatenate([on_plane, partner_plane], axis=0).reshape(
+                K, features + 128
+            )
             prototype_lowbits = everyone[:, :features]
             parts = everyone[:, features : features + 3].astype(jnp.float32)
             half_quadratic_length = (parts[:, 0] + parts[:, 1]) + parts[:, 2]

time: 146 us -> 149 us (1.021)
  waiting for transfers between devices: 42.9 us -> 54.2 us
  starting transfers between devices: 39.8 us -> 30.6 us
    ppermute x14, waiting for transfers between devices: 7.89 us -> 19.2 us  [steps(): lax.ppermute(outgoing, PLANE, [(i, (i + shift) % plane) for i in range(pl...]
    ppermute x14, starting transfers between devices: 20.1 us -> 9.34 us  [steps(): lax.ppermute(outgoing, PLANE, [(i, (i + shift) % plane) for i in range(pl...]
    all_to_all x1, blocking collectives: 15.2 us -> 18.3 us  [steps(): lax.all_to_all(smoothing_scale * closing_log_partition, ROUTE, split_axis...]
    all_to_all x1, blocking collectives: 13.6 us -> 11.8 us  [steps(): lax.all_to_all(jnp.broadcast_to(block[None], (plane,) + block.shape), PLA...]
    ppermute x1, starting transfers between devices: 2.39 us -> 4 us  [steps(): partner_plane = lax.ppermute(on_plane, 'core', [(0, 1), (1, 0)])]
where the time goes in v4:
time: 149 us
  waiting for transfers between devices  54.2 us (36%)
  starting transfers between devices  30.6 us (21%)
  blocking collectives  30.1 us (20%)
  other arithmetic  14.3 us (10%)
  matrix products  9.77 us (7%)
  local copies, waits for them, and re-layouts  8.94 us (6%)
    all_to_all x1, waiting for transfers between devices, steps(): lax.all_to_all(packed, ROUTE, split_axis=0, concat_axis=0, tiled=True)  23.7 us
    ppermute x14, waiting for transfers between devices, steps(): lax.ppermute(outgoing, PLANE, [(i, (i + shift) % plane) for i in range(pl...  19.2 us
    all_to_all x1, blocking collectives, steps(): lax.all_to_all(smoothing_scale * closing_log_partition, ROUTE, split_axis...  18.3 us
    all_to_all x1, blocking collectives, steps(): lax.all_to_all(jnp.broadcast_to(block[None], (plane,) + block.shape), PLA...  11.8 us
    all_to_all x1, starting transfers between devices, steps(): lax.all_to_all(packed, ROUTE, split_axis=0, concat_axis=0, tiled=True)  11.5 us
    ppermute x14, starting transfers between devices, steps(): lax.ppermute(outgoing, PLANE, [(i, (i + shift) % plane) for i in range(pl...  9.34 us
    ppermute x2, waiting for transfers between devices, steps(): halves = mine + lax.ppermute(theirs, 'core', [(0, 1), (1, 0)])  5.26 us
    ppermute x1, starting transfers between devices, steps(): partner_plane = lax.ppermute(on_plane, 'core', [(0, 1), (1, 0)])  4 us
  transfers between devices with their start and end apart: 20, of which 10 were waited for; matrix products, arithmetic and copies ran while one was open for 6% of the time, Pallas kernels for 0%

profile of v4, /device:TPU:1, one launch (start us, length us, event | category | flops | bytes accessed | tf_op | source)
XLA Modules:
  0.0 149.0 jit_solution(3163632854562713669)
XLA Ops:
  0.7 0.9 copy.27
  1.8 0.9 fusion.28
  2.8 0.7 multiply_add_fusion
  4.1 2.7 %select_bitcast_fusion = bf16[128,8,1024]{2,1,0:T(8,128)(2,1)} fusion(pred[1024]{0:T(1024)(128)(4,1)S(1)} %broadcast_compare_fusion, bf16[512,1024]{1,0:T(8,128)(2,1)S(1)} %copy-done.3, bf16[1024]{0:T(1024)(128)(2,1)S(1)} %fusion.35, f32[512]{0:T(512)S(1)} %add_rsqrt_fusion, s32[512]{0:T(512)S(1)} %multiply_add_fusion), kind=kOutput, calls=%fused_computation.16 | convolution fusion | flops 1078460416 | bytes 3152896 | tf_op jit(solution)/shard_map/dot_general | solution.py:58
  6.8 11.5 %all-to-all-start = ((bf16[128,8,1024]{2,1,0:T(8,128)(2,1)}), bf16[128,8,1024]{2,1,0:T(8,128)(2,1)S(1)}, u32[]{:S(2)}, u32[]{:S(2)}) async-start(bf16[128,8,1024]{2,1,0:T(8,128)(2,1)} %select_bitcast_fusion), calls=%async_computation | async-start | bytes 4194304 | tf_op jit(solution)/shard_map/all_to_all | solution.py:62
  18.3 1.1 collective-permute-start
  19.4 2.4 %collective-permute-done = bf16[512,1024]{1,0:T(8,128)(2,1)} collective-permute-done((bf16[512,1024]{1,0:T(8,128)(2,1)S(1)}, bf16[512,1024]{1,0:T(8,128)(2,1)}, u32[]{:S(2)}, u32[]{:S(2)}) %collective-permute-start) | collective-permute-done | bytes 1048608 | tf_op jit(solution)/shard_map/ppermute | solution.py:37
  21.9 2.8 %fusion.45 = (f32[512,1024]{1,0:T(8,128)}, bf16[512,1024]{1,0:T(8,128)(2,1)S(1)}) fusion(bf16[512,1024]{1,0:T(8,128)(2,1)} %param.5, bf16[512,1024]{1,0:T(8,128)(2,1)} %collective-permute-done, pred[]{:T(512)S(6)} %eq.83), kind=kLoop, calls=%fused_computation.107 | loop fusion | flops 1048576 | bytes 5242881 | tf_op jit(solution)/shard_map/convert_element_type | solution.py:72
  24.9 23.7 %all-to-all-done = bf16[128,8,1024]{2,1,0:T(8,128)(2,1)S(1)} async-done(((bf16[128,8,1024]{2,1,0:T(8,128)(2,1)}), bf16[128,8,1024]{2,1,0:T(8,128)(2,1)S(1)}, u32[]{:S(2)}, u32[]{:S(2)}) %all-to-all-start) | async-done | bytes 2097184 | tf_op jit(solution)/shard_map/all_to_all | solution.py:62
  48.7 1.3 fusion.5
  50.0 0.5 fusion.7
  50.5 0.8 convert_reduce_fusion
  51.3 2.6 %fusion.39 = f32[512,1024]{1,0:T(8,128)} fusion(bf16[1024,512]{0,1:T(8,128)(2,1)S(1)} %get-tuple-element.7, bf16[128,8,1024]{2,1,0:T(8,128)(2,1)S(1)} %all-to-all-done), kind=kOutput, calls=%fused_computation.101 | convolution fusion | flops 1073741824 | bytes 5242880 | tf_op jit(solution)/shard_map/rk,rd->kd/dot_general | solution.py:92
  53.9 1.7 %concatenate.18 = f32[2,8,32768]{2,1,0:T(8,128)S(1)} reshape(f32[512,1024]{1,0:T(8,128)} %fusion.39) | data formatting | bytes 4194304 | tf_op jit(solution)/shard_map/concatenate | solution.py:94
  55.9 1.3 collective-permute-start.1
  57.2 2.4 %collective-permute-done.1 = f32[8,32896]{1,0:T(8,128)} collective-permute-done((f32[8,32896]{1,0:T(8,128)S(1)}, f32[8,32896]{1,0:T(8,128)}, u32[]{:S(2)}, u32[]{:S(2)}) %collective-permute-start.1) | collective-permute-done | bytes 1052704 | tf_op jit(solution)/shard_map/ppermute | solution.py:105
  59.6 1.3 fusion.13
  61.0 0.6 constant_dynamic-slice_fusion.12
  62.0 1.3 collective-permute-start.3
  63.3 0.6 collective-permute-start.4
  63.9 1.7 %collective-permute-start.5 = (f32[1,32896]{1,0:T(1,128)S(1)}, f32[1,32896]{1,0:T(1,128)S(1)}, u32[]{:S(2)}, u32[]{:S(2)}) collective-permute-start(f32[1,32896]{1,0:T(1,128)S(1)} %get-tuple-element.21), channel_id=1, source_target_pairs={{0,4},{1,5},{2,6},{3,7},{4,0},{5,1},{6,2},{7,3},{8,12},{9,13},{10,... | collective-permute-start | bytes 394760 | tf_op jit(solution)/shard_map/ppermute | solution.py:109
  66.0 6.8 %collective-permute-done.2 = f32[1,32896]{1,0:T(1,128)S(1)} collective-permute-done((f32[1,32896]{1,0:T(1,128)S(1)}, f32[1,32896]{1,0:T(1,128)S(1)}, u32[]{:S(2)}, u32[]{:S(2)}) %collective-permute-start.2) | collective-permute-done | bytes 131616 | tf_op jit(solution)/shard_map/ppermute | solution.py:109
  72.8 0.4 collective-permute-done.4
  73.2 4.5 %collective-permute-done.5 = f32[1,32896]{1,0:T(1,128)S(1)} collective-permute-done((f32[1,32896]{1,0:T(1,128)S(1)}, f32[1,32896]{1,0:T(1,128)S(1)}, u32[]{:S(2)}, u32[]{:S(2)}) %collective-permute-start.5) | collective-permute-done | bytes 131616 | tf_op jit(solution)/shard_map/ppermute | solution.py:109
  77.7 0.4 collective-permute-done.7
  78.1 0.5 add_add_fusion.1
  79.0 1.3 multiply_reduce_fusion.1
  80.8 11.8 %all_to_all.23 = bf16[8,32,1152]{2,1,0:T(8,128)(2,1)S(1)} all-to-all(bf16[8,32,1152]{2,1,0:T(8,128)(2,1)S(1)} %broadcast_in_dim.77), channel_id=1, replica_groups=mesh['z'=4,'core'=2,'yhi'=2,'ylo'=2,'x'=4] {'ylo','x'}, dimensions={0} | all-to-all | bytes 1179648 | tf_op jit(solution)/shard_map/all_to_all | solution.py:149
  92.6 4.0 %collective-permute-start.9 = (bf16[8,32,1152]{2,1,0:T(8,128)(2,1)S(1)}, bf16[8,32,1152]{2,1,0:T(8,128)(2,1)}, u32[]{:S(2)}, u32[]{:S(2)}) collective-permute-start(bf16[8,32,1152]{2,1,0:T(8,128)(2,1)S(1)} %all_to_all.23), channel_id=1, source_target_pairs={{0,16},{16,0},{1,17},{17,1},{2,18},{18,2},{3,19},{19,3},{4,20},{20... | collective-permute-start | bytes 1769480 | tf_op jit(solution)/shard_map/ppermute | solution.py:156
  96.7 3.1 %concatenate.23 = bf16[1024,1152]{1,0:T(8,128)(2,1)} concatenate(bf16[1024,1024]{1,0:T(8,128)(2,1)S(1)} %bitcast.60, bf16[1024,1]{1,0:T(8,128)(2,1)S(1)} %broadcast_in_dim.78, bf16[1024,127]{1,0:T(8,128)(2,1)S(1)} %broadcast_in_dim.79), dimensions={1} | concatenate | bytes 4718592 | tf_op jit(solution)/shard_map/concatenate | solution.py:64
  99.8 1.2 pad_maximum_fusion
  101.3 1.3 fusion.6
  102.6 0.5 fusion.8
  103.1 1.8 %fusion.14 = f32[512,1152]{1,0:T(8,128)S(1)} fusion(bf16[1024,1152]{1,0:T(8,128)(2,1)S(1)} %copy-done.2, f32[1024,512]{0,1:T(8,128)S(1)} %get-tuple-element.30, f32[1024]{0:T(1024)S(1)} %fusion.8, f32[1024]{0:T(1024)S(1)} %get-tuple-element.29, f32[512]{0:T(512)S(1)} %fusion.26, f32[1024]{0:T(1024)S(1)} %convert_reduce_fusion.2), kind=kOutput, calls=%fused_computation.33 | convolution fusion | flops 1211105280 | bytes 6830080 | tf_op jit(solution)/shard_map/rk,rd->kd/dot_general | solution.py:116
  105.2 2.8 %collective-permute-done.10 = f32[8,32,1152]{2,1,0:T(8,128)S(1)} collective-permute-done((f32[8,32,1152]{2,1,0:T(8,128)S(1)}, f32[8,32,1152]{2,1,0:T(8,128)S(1)}, u32[]{:S(2)}, u32[]{:S(2)}) %collective-permute-start.10) | collective-permute-done | bytes 1179680 | tf_op jit(solution)/shard_map/ppermute | solution.py:122
  108.3 0.5 collective-permute-start.11
  108.8 1.7 %collective-permute-start.12 = (f32[1,32,1152]{2,1,0:T(8,128)S(1)}, f32[1,32,1152]{2,1,0:T(8,128)S(1)}, u32[]{:S(2)}, u32[]{:S(2)}) collective-permute-start(f32[1,32,1152]{2,1,0:T(8,128)S(1)} %get-tuple-element.16), channel_id=1, source_target_pairs={{0,2},{1,3},{2,4},{3,5},{4,6},{5,7},{6,0},{7,1},{8,10},{9,11},{10,... | collective-permute-start | bytes 442376 | tf_op jit(solution)/shard_map/ppermute | solution.py:128
  110.5 0.8 collective-permute-start.13
  111.3 1.2 collective-permute-start.14
  112.5 0.8 collective-permute-start.15
  113.3 7.1 %collective-permute-done.11 = f32[1,32,1152]{2,1,0:T(8,128)S(1)} collective-permute-done((f32[1,32,1152]{2,1,0:T(8,128)S(1)}, f32[1,32,1152]{2,1,0:T(8,128)S(1)}, u32[]{:S(2)}, u32[]{:S(2)}) %collective-permute-start.11) | collective-permute-done | bytes 147488 | tf_op jit(solution)/shard_map/ppermute | solution.py:128
  120.5 18.3 %all_to_all.24 = f32[128,8,1]{1,2,0:T(1,128)S(1)} all-to-all(f32[128,8,1]{1,2,0:T(1,128)S(1)} %bitcast.67), channel_id=1, replica_groups=mesh['z'=4,'core'=2,'yhi'=2,'ylo'=2,'x'=4] {'z','yhi','core','ylo','x'}, dimensions={0} | all-to-all | bytes 8192 | tf_op jit(solution)/shard_map/all_to_all | solution.py:87
  138.8 0.5 broadcast.145
  139.3 0.8 reduce.13
  140.6 3.2 %collective-permute-start.18 = (f32[32,1024]{1,0:T(8,128)S(1)}, f32[32,1024]{1,0:T(8,128)S(1)}, u32[]{:S(2)}, u32[]{:S(2)}) collective-permute-start(f32[32,1024]{1,0:T(8,128)S(1)} %fusion.32), channel_id=1, source_target_pairs={{0,0},{8,16},{16,8},{24,24},{1,1},{9,17},{17,9},{25,25},{2,2},{10,... | collective-permute-start | bytes 393224 | tf_op jit(solution)/shard_map/ppermute | solution.py:165
  143.8 0.9 select_reduce_fusion
  144.7 3.7 %collective-permute-done.18 = f32[32,1024]{1,0:T(8,128)S(1)} collective-permute-done((f32[32,1024]{1,0:T(8,128)S(1)}, f32[32,1024]{1,0:T(8,128)S(1)}, u32[]{:S(2)}, u32[]{:S(2)}) %collective-permute-start.18) | collective-permute-done | bytes 131104 | tf_op jit(solution)/shard_map/ppermute | solution.py:165
  148.3 0.7 copy.34
  (69 shorter events, 4.4 us)
Async XLA Ops:
  0.6 3.1 %copy-start.3 = (bf16[512,1024]{1,0:T(8,128)(2,1)S(1)}, bf16[512,1024]{1,0:T(8,128)(2,1)}, u32[]{:S(2)}) copy-start(bf16[512,1024]{1,0:T(8,128)(2,1)} %param.3) | copy-start | bytes 3145732
  6.8 11.5 %copy-start.4 = (bf16[512,1024]{1,0:T(8,128)(2,1)S(1)}, bf16[512,1024]{1,0:T(8,128)(2,1)}, u32[]{:S(2)}) copy-start(bf16[512,1024]{1,0:T(8,128)(2,1)} %param.5) | copy-start | bytes 3145732
  6.8 41.8 %all-to-all-start = ((bf16[128,8,1024]{2,1,0:T(8,128)(2,1)}), bf16[128,8,1024]{2,1,0:T(8,128)(2,1)S(1)}, u32[]{:S(2)}, u32[]{:S(2)}) async-start(bf16[128,8,1024]{2,1,0:T(8,128)(2,1)} %select_bitcast_fusion), calls=%async_computation | async-start | bytes 4194304 | tf_op jit(solution)/shard_map/all_to_all | solution.py:62
  18.3 3.6 %collective-permute-start = (bf16[512,1024]{1,0:T(8,128)(2,1)S(1)}, bf16[512,1024]{1,0:T(8,128)(2,1)}, u32[]{:S(2)}, u32[]{:S(2)}) collective-permute-start(bf16[512,1024]{1,0:T(8,128)(2,1)S(1)} %copy-done.4), channel_id=1, source_target_pairs={{0,16},{16,0},{1,17},{17,1},{2,18},{18,2},{3,19},{19,3},{4,20},{20... | collective-permute-start | bytes 3145736 | tf_op jit(solution)/shard_map/ppermute | solution.py:37
  48.6 2.8 %copy-start = (bf16[128,8,1024]{2,1,0:T(8,128)(2,1)}, bf16[128,8,1024]{2,1,0:T(8,128)(2,1)S(1)}, u32[]{:S(2)}) copy-start(bf16[128,8,1024]{2,1,0:T(8,128)(2,1)S(1)} %all-to-all-done) | copy-start | bytes 6291460
  55.9 3.8 %collective-permute-start.1 = (f32[8,32896]{1,0:T(8,128)S(1)}, f32[8,32896]{1,0:T(8,128)}, u32[]{:S(2)}, u32[]{:S(2)}) collective-permute-start(f32[8,32896]{1,0:T(8,128)S(1)} %fusion.10), channel_id=1, source_target_pairs={{0,16},{16,0},{1,17},{17,1},{2,18},{18,2},{3,19},{19,3},{4,20},{20... | collective-permute-start | bytes 3158024 | tf_op jit(solution)/shard_map/ppermute | solution.py:105
  61.6 11.2 %collective-permute-start.2 = (f32[1,32896]{1,0:T(1,128)S(1)}, f32[1,32896]{1,0:T(1,128)S(1)}, u32[]{:S(2)}, u32[]{:S(2)}) collective-permute-start(f32[1,32896]{1,0:T(1,128)S(1)} %get-tuple-element.17), channel_id=1, source_target_pairs={{0,1},{1,2},{2,3},{3,4},{4,5},{5,6},{6,7},{7,0},{8,9},{9,10},{10,1... | collective-permute-start | bytes 394760 | tf_op jit(solution)/shard_map/ppermute | solution.py:109
  62.0 10.8 %collective-permute-start.3 = (f32[1,32896]{1,0:T(1,128)S(1)}, f32[1,32896]{1,0:T(1,128)S(1)}, u32[]{:S(2)}, u32[]{:S(2)}) collective-permute-start(f32[1,32896]{1,0:T(1,128)S(1)} %get-tuple-element.23), channel_id=1, source_target_pairs={{0,2},{1,3},{2,4},{3,5},{4,6},{5,7},{6,0},{7,1},{8,10},{9,11},{10,... | collective-permute-start | bytes 394760 | tf_op jit(solution)/shard_map/ppermute | solution.py:109
  63.3 9.9 %collective-permute-start.4 = (f32[1,32896]{1,0:T(1,128)S(1)}, f32[1,32896]{1,0:T(1,128)S(1)}, u32[]{:S(2)}, u32[]{:S(2)}) collective-permute-start(f32[1,32896]{1,0:T(1,128)S(1)} %get-tuple-element.22), channel_id=1, source_target_pairs={{0,3},{1,4},{2,5},{3,6},{4,7},{5,0},{6,1},{7,2},{8,11},{9,12},{10,... | collective-permute-start | bytes 394760 | tf_op jit(solution)/shard_map/ppermute | solution.py:109
  63.9 13.8 %collective-permute-start.5 = (f32[1,32896]{1,0:T(1,128)S(1)}, f32[1,32896]{1,0:T(1,128)S(1)}, u32[]{:S(2)}, u32[]{:S(2)}) collective-permute-start(f32[1,32896]{1,0:T(1,128)S(1)} %get-tuple-element.21), channel_id=1, source_target_pairs={{0,4},{1,5},{2,6},{3,7},{4,0},{5,1},{6,2},{7,3},{8,12},{9,13},{10,... | collective-permute-start | bytes 394760 | tf_op jit(solution)/shard_map/ppermute | solution.py:109
  65.6 12.0 %collective-permute-start.6 = (f32[1,32896]{1,0:T(1,128)S(1)}, f32[1,32896]{1,0:T(1,128)S(1)}, u32[]{:S(2)}, u32[]{:S(2)}) collective-permute-start(f32[1,32896]{1,0:T(1,128)S(1)} %get-tuple-element.20), channel_id=1, source_target_pairs={{0,5},{1,6},{2,7},{3,0},{4,1},{5,2},{6,3},{7,4},{8,13},{9,14},{10,... | collective-permute-start | bytes 394760 | tf_op jit(solution)/shard_map/ppermute | solution.py:109
  72.8 5.3 %collective-permute-start.7 = (f32[1,32896]{1,0:T(1,128)S(1)}, f32[1,32896]{1,0:T(1,128)S(1)}, u32[]{:S(2)}, u32[]{:S(2)}) collective-permute-start(f32[1,32896]{1,0:T(1,128)S(1)} %get-tuple-element.19), channel_id=1, source_target_pairs={{0,6},{1,7},{2,0},{3,1},{4,2},{5,3},{6,4},{7,5},{8,14},{9,15},{10,... | collective-permute-start | bytes 394760 | tf_op jit(solution)/shard_map/ppermute | solution.py:109
  72.8 5.3 %collective-permute-start.8 = (f32[1,32896]{1,0:T(1,128)S(1)}, f32[1,32896]{1,0:T(1,128)S(1)}, u32[]{:S(2)}, u32[]{:S(2)}) collective-permute-start(f32[1,32896]{1,0:T(1,128)S(1)} %get-tuple-element.18), channel_id=1, source_target_pairs={{0,7},{1,0},{2,1},{3,2},{4,3},{5,4},{6,5},{7,6},{8,15},{9,8},{10,9... | collective-permute-start | bytes 394760 | tf_op jit(solution)/shard_map/ppermute | solution.py:109
  78.6 18.1 %copy-start.1 = (bf16[128,8,1024]{2,1,0:T(8,128)(2,1)S(1)}, bf16[128,8,1024]{2,1,0:T(8,128)(2,1)}, u32[]{:S(2)}) copy-start(bf16[128,8,1024]{2,1,0:T(8,128)(2,1)} %copy-done) | copy-start | bytes 6291460
  92.6 7.2 %collective-permute-start.9 = (bf16[8,32,1152]{2,1,0:T(8,128)(2,1)S(1)}, bf16[8,32,1152]{2,1,0:T(8,128)(2,1)}, u32[]{:S(2)}, u32[]{:S(2)}) collective-permute-start(bf16[8,32,1152]{2,1,0:T(8,128)(2,1)S(1)} %all_to_all.23), channel_id=1, source_target_pairs={{0,16},{16,0},{1,17},{17,1},{2,18},{18,2},{3,19},{19,3},{4,20},{20... | collective-permute-start | bytes 1769480 | tf_op jit(solution)/shard_map/ppermute | solution.py:156
  101.3 1.8 %copy-start.2 = (bf16[1024,1152]{1,0:T(8,128)(2,1)S(1)}, bf16[1024,1152]{1,0:T(8,128)(2,1)}, u32[]{:S(2)}) copy-start(bf16[1024,1152]{1,0:T(8,128)(2,1)} %concatenate.23) | copy-start | bytes 7077892
  105.1 2.9 %collective-permute-start.10 = (f32[8,32,1152]{2,1,0:T(8,128)S(1)}, f32[8,32,1152]{2,1,0:T(8,128)S(1)}, u32[]{:S(2)}, u32[]{:S(2)}) collective-permute-start(f32[8,32,1152]{2,1,0:T(8,128)S(1)} %bitcast.64), channel_id=1, source_target_pairs={{0,16},{16,0},{1,17},{17,1},{2,18},{18,2},{3,19},{19,3},{4,20},{20... | collective-permute-start | bytes 3538952 | tf_op jit(solution)/shard_map/ppermute | solution.py:122
  108.3 12.1 %collective-permute-start.11 = (f32[1,32,1152]{2,1,0:T(8,128)S(1)}, f32[1,32,1152]{2,1,0:T(8,128)S(1)}, u32[]{:S(2)}, u32[]{:S(2)}) collective-permute-start(f32[1,32,1152]{2,1,0:T(8,128)S(1)} %get-tuple-element.10), channel_id=1, source_target_pairs={{0,1},{1,2},{2,3},{3,4},{4,5},{5,6},{6,7},{7,0},{8,9},{9,10},{10,1... | collective-permute-start | bytes 442376 | tf_op jit(solution)/shard_map/ppermute | solution.py:128
  108.8 11.6 %collective-permute-start.12 = (f32[1,32,1152]{2,1,0:T(8,128)S(1)}, f32[1,32,1152]{2,1,0:T(8,128)S(1)}, u32[]{:S(2)}, u32[]{:S(2)}) collective-permute-start(f32[1,32,1152]{2,1,0:T(8,128)S(1)} %get-tuple-element.16), channel_id=1, source_target_pairs={{0,2},{1,3},{2,4},{3,5},{4,6},{5,7},{6,0},{7,1},{8,10},{9,11},{10,... | collective-permute-start | bytes 442376 | tf_op jit(solution)/shard_map/ppermute | solution.py:128
  110.5 29.7 %collective-permute-start.13 = (f32[1,32,1152]{2,1,0:T(8,128)S(1)}, f32[1,32,1152]{2,1,0:T(8,128)S(1)}, u32[]{:S(2)}, u32[]{:S(2)}) collective-permute-start(f32[1,32,1152]{2,1,0:T(8,128)S(1)} %get-tuple-element.15), channel_id=1, source_target_pairs={{0,3},{1,4},{2,5},{3,6},{4,7},{5,0},{6,1},{7,2},{8,11},{9,12},{10,... | collective-permute-start | bytes 442376 | tf_op jit(solution)/shard_map/ppermute | solution.py:128
  111.3 28.9 %collective-permute-start.14 = (f32[1,32,1152]{2,1,0:T(8,128)S(1)}, f32[1,32,1152]{2,1,0:T(8,128)S(1)}, u32[]{:S(2)}, u32[]{:S(2)}) collective-permute-start(f32[1,32,1152]{2,1,0:T(8,128)S(1)} %get-tuple-element.14), channel_id=1, source_target_pairs={{0,4},{1,5},{2,6},{3,7},{4,0},{5,1},{6,2},{7,3},{8,12},{9,13},{10,... | collective-permute-start | bytes 442376 | tf_op jit(solution)/shard_map/ppermute | solution.py:128
  112.5 27.7 %collective-permute-start.15 = (f32[1,32,1152]{2,1,0:T(8,128)S(1)}, f32[1,32,1152]{2,1,0:T(8,128)S(1)}, u32[]{:S(2)}, u32[]{:S(2)}) collective-permute-start(f32[1,32,1152]{2,1,0:T(8,128)S(1)} %get-tuple-element.13), channel_id=1, source_target_pairs={{0,5},{1,6},{2,7},{3,0},{4,1},{5,2},{6,3},{7,4},{8,13},{9,14},{10,... | collective-permute-start | bytes 442376 | tf_op jit(solution)/shard_map/ppermute | solution.py:128
  120.4 19.9 %collective-permute-start.16 = (f32[1,32,1152]{2,1,0:T(8,128)S(1)}, f32[1,32,1152]{2,1,0:T(8,128)S(1)}, u32[]{:S(2)}, u32[]{:S(2)}) collective-permute-start(f32[1,32,1152]{2,1,0:T(8,128)S(1)} %get-tuple-element.12), channel_id=1, source_target_pairs={{0,6},{1,7},{2,0},{3,1},{4,2},{5,3},{6,4},{7,5},{8,14},{9,15},{10,... | collective-permute-start | bytes 442376 | tf_op jit(solution)/shard_map/ppermute | solution.py:128
  120.4 19.9 %collective-permute-start.17 = (f32[1,32,1152]{2,1,0:T(8,128)S(1)}, f32[1,32,1152]{2,1,0:T(8,128)S(1)}, u32[]{:S(2)}, u32[]{:S(2)}) collective-permute-start(f32[1,32,1152]{2,1,0:T(8,128)S(1)} %get-tuple-element.11), channel_id=1, source_target_pairs={{0,7},{1,0},{2,1},{3,2},{4,3},{5,4},{6,5},{7,6},{8,15},{9,8},{10,9... | collective-permute-start | bytes 442376 | tf_op jit(solution)/shard_map/ppermute | solution.py:128
  140.6 7.8 %collective-permute-start.18 = (f32[32,1024]{1,0:T(8,128)S(1)}, f32[32,1024]{1,0:T(8,128)S(1)}, u32[]{:S(2)}, u32[]{:S(2)}) collective-permute-start(f32[32,1024]{1,0:T(8,128)S(1)} %fusion.32), channel_id=1, source_target_pairs={{0,0},{8,16},{16,8},{24,24},{1,1},{9,17},{17,9},{25,25},{2,2},{10,... | collective-permute-start | bytes 393224 | tf_op jit(solution)/shard_map/ppermute | solution.py:165

commit v5 on v3

--- a/solution.py
+++ b/solution.py
@@ -20,7 +20,6 @@
 ROUTE = ("z", "yhi", "core", "ylo", "x")
 TEAM = ("core", "ylo", "x")
 PLANE = ("ylo", "x")
-SHIFT_ORDER = (4, 1, 7, 2, 6, 3, 5)
 
 
 def steps(embeddings, coarse_ids, centroid_seeds):
@@ -105,7 +104,7 @@
             theirs = lax.dynamic_index_in_dim(by_core, 1 - core, 0, keepdims=False)
             halves = mine + lax.ppermute(theirs, "core", [(0, 1), (1, 0)])
             reduced = lax.dynamic_index_in_dim(halves, spot, 0, keepdims=True)
-            for shift in SHIFT_ORDER:
+            for shift in range(1, plane):
                 outgoing = lax.dynamic_index_in_dim(halves, (spot + shift) % plane, 0, keepdims=True)
                 incoming = lax.ppermute(
                     outgoing, PLANE, [(i, (i + shift) % plane) for i in range(plane)]
@@ -122,7 +121,7 @@
             theirs = lax.dynamic_index_in_dim(by_core, 1 - core, 0, keepdims=False)
             halves = mine + lax.ppermute(theirs, "core", [(0, 1), (1, 0)])
             reduced = lax.dynamic_index_in_dim(halves, spot, 0, keepdims=True)
-            for shift in SHIFT_ORDER:
+            for shift in range(1, plane):
                 outgoing = lax.dynamic_index_in_dim(
                     halves, (spot + shift) % plane, 0, keepdims=True
                 )

time: 146 us -> 150 us (1.027)
  waiting for transfers between devices: 42.9 us -> 54.2 us
  starting transfers between devices: 39.8 us -> 30.6 us
    ppermute x14, waiting for transfers between devices: 7.89 us -> 19.2 us  [steps(): lax.ppermute(outgoing, PLANE, [(i, (i + shift) % plane) for i in range(pl...]
    ppermute x14, starting transfers between devices: 20.1 us -> 9.35 us  [steps(): lax.ppermute(outgoing, PLANE, [(i, (i + shift) % plane) for i in range(pl...]
    all_to_all x1, blocking collectives: 15.2 us -> 18.3 us  [steps(): lax.all_to_all(smoothing_scale * closing_log_partition, ROUTE, split_axis...]
    all_to_all x1, blocking collectives: 13.6 us -> 11.8 us  [steps(): lax.all_to_all(jnp.broadcast_to(block[None], (plane,) + block.shape), PLA...]
    ppermute x1, starting transfers between devices: 2.39 us -> 4 us  [steps(): partner_plane = lax.ppermute(on_plane, 'core', [(0, 1), (1, 0)])]
where the time goes in v5:
time: 150 us; the launch traced here: 149 us
  waiting for transfers between devices  54.2 us (36%)
  starting transfers between devices  30.6 us (20%)
  blocking collectives  30.1 us (20%)
  other arithmetic  14.4 us (10%)
  matrix products  9.77 us (7%)
  local copies, waits for them, and re-layouts  8.87 us (6%)
    all_to_all x1, waiting for transfers between devices, steps(): lax.all_to_all(packed, ROUTE, split_axis=0, concat_axis=0, tiled=True)  23.7 us
    ppermute x14, waiting for transfers between devices, steps(): lax.ppermute(outgoing, PLANE, [(i, (i + shift) % plane) for i in range(pl...  19.2 us
    all_to_all x1, blocking collectives, steps(): lax.all_to_all(smoothing_scale * closing_log_partition, ROUTE, split_axis...  18.3 us
    all_to_all x1, blocking collectives, steps(): lax.all_to_all(jnp.broadcast_to(block[None], (plane,) + block.shape), PLA...  11.8 us
    all_to_all x1, starting transfers between devices, steps(): lax.all_to_all(packed, ROUTE, split_axis=0, concat_axis=0, tiled=True)  11.5 us
    ppermute x14, starting transfers between devices, steps(): lax.ppermute(outgoing, PLANE, [(i, (i + shift) % plane) for i in range(pl...  9.35 us
    ppermute x2, waiting for transfers between devices, steps(): halves = mine + lax.ppermute(theirs, 'core', [(0, 1), (1, 0)])  5.26 us
    ppermute x1, starting transfers between devices, steps(): partner_plane = lax.ppermute(on_plane, 'core', [(0, 1), (1, 0)])  4 us
  transfers between devices with their start and end apart: 20, of which 10 were waited for; matrix products, arithmetic and copies ran while one was open for 6% of the time, Pallas kernels for 0%

profile of v5, /device:TPU:1, one launch (start us, length us, event | category | flops | bytes accessed | tf_op | source)
XLA Modules:
  0.0 149.1 jit_solution(2102965092389433276)
XLA Ops:
  0.7 0.9 copy.27
  1.8 0.9 fusion.28
  2.8 0.7 multiply_add_fusion
  4.1 2.7 %select_bitcast_fusion = bf16[128,8,1024]{2,1,0:T(8,128)(2,1)} fusion(pred[1024]{0:T(1024)(128)(4,1)S(1)} %broadcast_compare_fusion, bf16[512,1024]{1,0:T(8,128)(2,1)S(1)} %copy-done.3, bf16[1024]{0:T(1024)(128)(2,1)S(1)} %fusion.35, f32[512]{0:T(512)S(1)} %add_rsqrt_fusion, s32[512]{0:T(512)S(1)} %multiply_add_fusion), kind=kOutput, calls=%fused_computation.16 | convolution fusion | flops 1078460416 | bytes 3152896 | tf_op jit(solution)/shard_map/dot_general | solution.py:58
  6.8 11.5 %all-to-all-start = ((bf16[128,8,1024]{2,1,0:T(8,128)(2,1)}), bf16[128,8,1024]{2,1,0:T(8,128)(2,1)S(1)}, u32[]{:S(2)}, u32[]{:S(2)}) async-start(bf16[128,8,1024]{2,1,0:T(8,128)(2,1)} %select_bitcast_fusion), calls=%async_computation | async-start | bytes 4194304 | tf_op jit(solution)/shard_map/all_to_all | solution.py:62
  18.3 1.1 collective-permute-start
  19.4 2.4 %collective-permute-done = bf16[512,1024]{1,0:T(8,128)(2,1)} collective-permute-done((bf16[512,1024]{1,0:T(8,128)(2,1)S(1)}, bf16[512,1024]{1,0:T(8,128)(2,1)}, u32[]{:S(2)}, u32[]{:S(2)}) %collective-permute-start) | collective-permute-done | bytes 1048608 | tf_op jit(solution)/shard_map/ppermute | solution.py:37
  21.9 2.8 %fusion.45 = (f32[512,1024]{1,0:T(8,128)}, bf16[512,1024]{1,0:T(8,128)(2,1)S(1)}) fusion(bf16[512,1024]{1,0:T(8,128)(2,1)} %param.5, bf16[512,1024]{1,0:T(8,128)(2,1)} %collective-permute-done, pred[]{:T(512)S(6)} %eq.88), kind=kLoop, calls=%fused_computation.111 | loop fusion | flops 1048576 | bytes 5242881 | tf_op jit(solution)/shard_map/convert_element_type | solution.py:72
  24.9 23.7 %all-to-all-done = bf16[128,8,1024]{2,1,0:T(8,128)(2,1)S(1)} async-done(((bf16[128,8,1024]{2,1,0:T(8,128)(2,1)}), bf16[128,8,1024]{2,1,0:T(8,128)(2,1)S(1)}, u32[]{:S(2)}, u32[]{:S(2)}) %all-to-all-start) | async-done | bytes 2097184 | tf_op jit(solution)/shard_map/all_to_all | solution.py:62
  48.7 1.3 fusion.5
  50.0 0.5 fusion.7
  50.5 0.8 convert_reduce_fusion
  51.3 2.6 %fusion.39 = f32[512,1024]{1,0:T(8,128)} fusion(bf16[1024,512]{0,1:T(8,128)(2,1)S(1)} %get-tuple-element.7, bf16[128,8,1024]{2,1,0:T(8,128)(2,1)S(1)} %all-to-all-done), kind=kOutput, calls=%fused_computation.105 | convolution fusion | flops 1073741824 | bytes 5242880 | tf_op jit(solution)/shard_map/rk,rd->kd/dot_general | solution.py:92
  53.9 1.7 %concatenate.18 = f32[2,8,32768]{2,1,0:T(8,128)S(1)} reshape(f32[512,1024]{1,0:T(8,128)} %fusion.39) | data formatting | bytes 4194304 | tf_op jit(solution)/shard_map/concatenate | solution.py:94
  55.9 1.3 collective-permute-start.1
  57.2 2.4 %collective-permute-done.1 = f32[8,32896]{1,0:T(8,128)} collective-permute-done((f32[8,32896]{1,0:T(8,128)S(1)}, f32[8,32896]{1,0:T(8,128)}, u32[]{:S(2)}, u32[]{:S(2)}) %collective-permute-start.1) | collective-permute-done | bytes 1052704 | tf_op jit(solution)/shard_map/ppermute | solution.py:105
  59.6 1.3 fusion.13
  61.0 0.6 constant_dynamic-slice_fusion.12
  62.0 1.3 collective-permute-start.3
  63.3 0.6 collective-permute-start.4
  63.9 1.7 %collective-permute-start.5 = (f32[1,32896]{1,0:T(1,128)S(1)}, f32[1,32896]{1,0:T(1,128)S(1)}, u32[]{:S(2)}, u32[]{:S(2)}) collective-permute-start(f32[1,32896]{1,0:T(1,128)S(1)} %get-tuple-element.21), channel_id=1, source_target_pairs={{0,4},{1,5},{2,6},{3,7},{4,0},{5,1},{6,2},{7,3},{8,12},{9,13},{10,... | collective-permute-start | bytes 394760 | tf_op jit(solution)/shard_map/ppermute | solution.py:109
  66.0 6.8 %collective-permute-done.2 = f32[1,32896]{1,0:T(1,128)S(1)} collective-permute-done((f32[1,32896]{1,0:T(1,128)S(1)}, f32[1,32896]{1,0:T(1,128)S(1)}, u32[]{:S(2)}, u32[]{:S(2)}) %collective-permute-start.2) | collective-permute-done | bytes 131616 | tf_op jit(solution)/shard_map/ppermute | solution.py:109
  72.8 0.4 collective-permute-done.4
  73.2 4.5 %collective-permute-done.5 = f32[1,32896]{1,0:T(1,128)S(1)} collective-permute-done((f32[1,32896]{1,0:T(1,128)S(1)}, f32[1,32896]{1,0:T(1,128)S(1)}, u32[]{:S(2)}, u32[]{:S(2)}) %collective-permute-start.5) | collective-permute-done | bytes 131616 | tf_op jit(solution)/shard_map/ppermute | solution.py:109
  77.7 0.4 collective-permute-done.7
  78.1 0.5 add_add_fusion.1
  79.0 1.3 multiply_reduce_fusion.1
  80.8 11.8 %all_to_all.23 = bf16[8,32,1152]{2,1,0:T(8,128)(2,1)S(1)} all-to-all(bf16[8,32,1152]{2,1,0:T(8,128)(2,1)S(1)} %broadcast_in_dim.77), channel_id=1, replica_groups=mesh['z'=4,'core'=2,'yhi'=2,'ylo'=2,'x'=4] {'ylo','x'}, dimensions={0} | all-to-all | bytes 1179648 | tf_op jit(solution)/shard_map/all_to_all | solution.py:149
  92.6 4.0 %collective-permute-start.9 = (bf16[8,32,1152]{2,1,0:T(8,128)(2,1)S(1)}, bf16[8,32,1152]{2,1,0:T(8,128)(2,1)}, u32[]{:S(2)}, u32[]{:S(2)}) collective-permute-start(bf16[8,32,1152]{2,1,0:T(8,128)(2,1)S(1)} %all_to_all.23), channel_id=1, source_target_pairs={{0,16},{16,0},{1,17},{17,1},{2,18},{18,2},{3,19},{19,3},{4,20},{20... | collective-permute-start | bytes 1769480 | tf_op jit(solution)/shard_map/ppermute | solution.py:156
  96.7 3.1 %concatenate.23 = bf16[1024,1152]{1,0:T(8,128)(2,1)} concatenate(bf16[1024,1024]{1,0:T(8,128)(2,1)S(1)} %bitcast.63, bf16[1024,1]{1,0:T(8,128)(2,1)S(1)} %broadcast_in_dim.78, bf16[1024,127]{1,0:T(8,128)(2,1)S(1)} %broadcast_in_dim.79), dimensions={1} | concatenate | bytes 4718592 | tf_op jit(solution)/shard_map/concatenate | solution.py:64
  99.8 1.2 broadcast_select_fusion.2
  101.4 1.3 fusion.6
  102.8 0.5 fusion.8
  103.3 1.8 %fusion.14 = f32[512,1152]{1,0:T(8,128)S(1)} fusion(bf16[1024,1152]{1,0:T(8,128)(2,1)S(1)} %copy-done.2, f32[1024,512]{0,1:T(8,128)S(1)} %get-tuple-element.30, f32[1024]{0:T(1024)S(1)} %fusion.8, f32[1024]{0:T(1024)S(1)} %get-tuple-element.29, f32[512]{0:T(512)S(1)} %fusion.26, f32[1024]{0:T(1024)S(1)} %convert_reduce_fusion.2), kind=kOutput, calls=%fused_computation.35 | convolution fusion | flops 1211105280 | bytes 6830080 | tf_op jit(solution)/shard_map/rk,rd->kd/dot_general | solution.py:116
  105.3 2.8 %collective-permute-done.10 = f32[8,32,1152]{2,1,0:T(8,128)S(1)} collective-permute-done((f32[8,32,1152]{2,1,0:T(8,128)S(1)}, f32[8,32,1152]{2,1,0:T(8,128)S(1)}, u32[]{:S(2)}, u32[]{:S(2)}) %collective-permute-start.10) | collective-permute-done | bytes 1179680 | tf_op jit(solution)/shard_map/ppermute | solution.py:122
  108.3 0.5 collective-permute-start.11
  108.9 1.7 %collective-permute-start.12 = (f32[1,32,1152]{2,1,0:T(8,128)S(1)}, f32[1,32,1152]{2,1,0:T(8,128)S(1)}, u32[]{:S(2)}, u32[]{:S(2)}) collective-permute-start(f32[1,32,1152]{2,1,0:T(8,128)S(1)} %get-tuple-element.14), channel_id=1, source_target_pairs={{0,2},{1,3},{2,4},{3,5},{4,6},{5,7},{6,0},{7,1},{8,10},{9,11},{10,... | collective-permute-start | bytes 442376 | tf_op jit(solution)/shard_map/ppermute | solution.py:128
  110.6 0.8 collective-permute-start.13
  111.4 1.2 collective-permute-start.14
  112.5 0.8 collective-permute-start.15
  113.3 7.1 %collective-permute-done.11 = f32[1,32,1152]{2,1,0:T(8,128)S(1)} collective-permute-done((f32[1,32,1152]{2,1,0:T(8,128)S(1)}, f32[1,32,1152]{2,1,0:T(8,128)S(1)}, u32[]{:S(2)}, u32[]{:S(2)}) %collective-permute-start.11) | collective-permute-done | bytes 147488 | tf_op jit(solution)/shard_map/ppermute | solution.py:128
  120.5 18.3 %all_to_all.24 = f32[128,8,1]{1,2,0:T(1,128)S(1)} all-to-all(f32[128,8,1]{1,2,0:T(1,128)S(1)} %bitcast.70), channel_id=1, replica_groups=mesh['z'=4,'core'=2,'yhi'=2,'ylo'=2,'x'=4] {'z','yhi','core','ylo','x'}, dimensions={0} | all-to-all | bytes 8192 | tf_op jit(solution)/shard_map/all_to_all | solution.py:87
  138.9 0.5 broadcast.145
  139.4 0.8 reduce.13
  140.6 3.2 %collective-permute-start.18 = (f32[32,1024]{1,0:T(8,128)S(1)}, f32[32,1024]{1,0:T(8,128)S(1)}, u32[]{:S(2)}, u32[]{:S(2)}) collective-permute-start(f32[32,1024]{1,0:T(8,128)S(1)} %fusion.32), channel_id=1, source_target_pairs={{0,0},{8,16},{16,8},{24,24},{1,1},{9,17},{17,9},{25,25},{2,2},{10,... | collective-permute-start | bytes 393224 | tf_op jit(solution)/shard_map/ppermute | solution.py:169
  143.8 0.9 select_reduce_fusion
  144.7 3.7 %collective-permute-done.18 = f32[32,1024]{1,0:T(8,128)S(1)} collective-permute-done((f32[32,1024]{1,0:T(8,128)S(1)}, f32[32,1024]{1,0:T(8,128)S(1)}, u32[]{:S(2)}, u32[]{:S(2)}) %collective-permute-start.18) | collective-permute-done | bytes 131104 | tf_op jit(solution)/shard_map/ppermute | solution.py:169
  148.4 0.7 copy.34
  (70 shorter events, 4.4 us)
Async XLA Ops:
  0.6 3.1 %copy-start.3 = (bf16[512,1024]{1,0:T(8,128)(2,1)S(1)}, bf16[512,1024]{1,0:T(8,128)(2,1)}, u32[]{:S(2)}) copy-start(bf16[512,1024]{1,0:T(8,128)(2,1)} %param.3) | copy-start | bytes 3145732
  6.8 11.5 %copy-start.4 = (bf16[512,1024]{1,0:T(8,128)(2,1)S(1)}, bf16[512,1024]{1,0:T(8,128)(2,1)}, u32[]{:S(2)}) copy-start(bf16[512,1024]{1,0:T(8,128)(2,1)} %param.5) | copy-start | bytes 3145732
  6.8 41.8 %all-to-all-start = ((bf16[128,8,1024]{2,1,0:T(8,128)(2,1)}), bf16[128,8,1024]{2,1,0:T(8,128)(2,1)S(1)}, u32[]{:S(2)}, u32[]{:S(2)}) async-start(bf16[128,8,1024]{2,1,0:T(8,128)(2,1)} %select_bitcast_fusion), calls=%async_computation | async-start | bytes 4194304 | tf_op jit(solution)/shard_map/all_to_all | solution.py:62
  18.3 3.6 %collective-permute-start = (bf16[512,1024]{1,0:T(8,128)(2,1)S(1)}, bf16[512,1024]{1,0:T(8,128)(2,1)}, u32[]{:S(2)}, u32[]{:S(2)}) collective-permute-start(bf16[512,1024]{1,0:T(8,128)(2,1)S(1)} %copy-done.4), channel_id=1, source_target_pairs={{0,16},{16,0},{1,17},{17,1},{2,18},{18,2},{3,19},{19,3},{4,20},{20... | collective-permute-start | bytes 3145736 | tf_op jit(solution)/shard_map/ppermute | solution.py:37
  48.6 2.8 %copy-start = (bf16[128,8,1024]{2,1,0:T(8,128)(2,1)}, bf16[128,8,1024]{2,1,0:T(8,128)(2,1)S(1)}, u32[]{:S(2)}) copy-start(bf16[128,8,1024]{2,1,0:T(8,128)(2,1)S(1)} %all-to-all-done) | copy-start | bytes 6291460
  55.9 3.8 %collective-permute-start.1 = (f32[8,32896]{1,0:T(8,128)S(1)}, f32[8,32896]{1,0:T(8,128)}, u32[]{:S(2)}, u32[]{:S(2)}) collective-permute-start(f32[8,32896]{1,0:T(8,128)S(1)} %fusion.10), channel_id=1, source_target_pairs={{0,16},{16,0},{1,17},{17,1},{2,18},{18,2},{3,19},{19,3},{4,20},{20... | collective-permute-start | bytes 3158024 | tf_op jit(solution)/shard_map/ppermute | solution.py:105
  61.6 11.2 %collective-permute-start.2 = (f32[1,32896]{1,0:T(1,128)S(1)}, f32[1,32896]{1,0:T(1,128)S(1)}, u32[]{:S(2)}, u32[]{:S(2)}) collective-permute-start(f32[1,32896]{1,0:T(1,128)S(1)} %get-tuple-element.17), channel_id=1, source_target_pairs={{0,1},{1,2},{2,3},{3,4},{4,5},{5,6},{6,7},{7,0},{8,9},{9,10},{10,1... | collective-permute-start | bytes 394760 | tf_op jit(solution)/shard_map/ppermute | solution.py:109
  62.0 10.8 %collective-permute-start.3 = (f32[1,32896]{1,0:T(1,128)S(1)}, f32[1,32896]{1,0:T(1,128)S(1)}, u32[]{:S(2)}, u32[]{:S(2)}) collective-permute-start(f32[1,32896]{1,0:T(1,128)S(1)} %get-tuple-element.23), channel_id=1, source_target_pairs={{0,2},{1,3},{2,4},{3,5},{4,6},{5,7},{6,0},{7,1},{8,10},{9,11},{10,... | collective-permute-start | bytes 394760 | tf_op jit(solution)/shard_map/ppermute | solution.py:109
  63.3 9.9 %collective-permute-start.4 = (f32[1,32896]{1,0:T(1,128)S(1)}, f32[1,32896]{1,0:T(1,128)S(1)}, u32[]{:S(2)}, u32[]{:S(2)}) collective-permute-start(f32[1,32896]{1,0:T(1,128)S(1)} %get-tuple-element.22), channel_id=1, source_target_pairs={{0,3},{1,4},{2,5},{3,6},{4,7},{5,0},{6,1},{7,2},{8,11},{9,12},{10,... | collective-permute-start | bytes 394760 | tf_op jit(solution)/shard_map/ppermute | solution.py:109
  63.9 13.8 %collective-permute-start.5 = (f32[1,32896]{1,0:T(1,128)S(1)}, f32[1,32896]{1,0:T(1,128)S(1)}, u32[]{:S(2)}, u32[]{:S(2)}) collective-permute-start(f32[1,32896]{1,0:T(1,128)S(1)} %get-tuple-element.21), channel_id=1, source_target_pairs={{0,4},{1,5},{2,6},{3,7},{4,0},{5,1},{6,2},{7,3},{8,12},{9,13},{10,... | collective-permute-start | bytes 394760 | tf_op jit(solution)/shard_map/ppermute | solution.py:109
  65.6 12.0 %collective-permute-start.6 = (f32[1,32896]{1,0:T(1,128)S(1)}, f32[1,32896]{1,0:T(1,128)S(1)}, u32[]{:S(2)}, u32[]{:S(2)}) collective-permute-start(f32[1,32896]{1,0:T(1,128)S(1)} %get-tuple-element.20), channel_id=1, source_target_pairs={{0,5},{1,6},{2,7},{3,0},{4,1},{5,2},{6,3},{7,4},{8,13},{9,14},{10,... | collective-permute-start | bytes 394760 | tf_op jit(solution)/shard_map/ppermute | solution.py:109
  72.8 5.3 %collective-permute-start.7 = (f32[1,32896]{1,0:T(1,128)S(1)}, f32[1,32896]{1,0:T(1,128)S(1)}, u32[]{:S(2)}, u32[]{:S(2)}) collective-permute-start(f32[1,32896]{1,0:T(1,128)S(1)} %get-tuple-element.19), channel_id=1, source_target_pairs={{0,6},{1,7},{2,0},{3,1},{4,2},{5,3},{6,4},{7,5},{8,14},{9,15},{10,... | collective-permute-start | bytes 394760 | tf_op jit(solution)/shard_map/ppermute | solution.py:109
  72.8 5.3 %collective-permute-start.8 = (f32[1,32896]{1,0:T(1,128)S(1)}, f32[1,32896]{1,0:T(1,128)S(1)}, u32[]{:S(2)}, u32[]{:S(2)}) collective-permute-start(f32[1,32896]{1,0:T(1,128)S(1)} %get-tuple-element.18), channel_id=1, source_target_pairs={{0,7},{1,0},{2,1},{3,2},{4,3},{5,4},{6,5},{7,6},{8,15},{9,8},{10,9... | collective-permute-start | bytes 394760 | tf_op jit(solution)/shard_map/ppermute | solution.py:109
  78.6 18.1 %copy-start.1 = (bf16[128,8,1024]{2,1,0:T(8,128)(2,1)S(1)}, bf16[128,8,1024]{2,1,0:T(8,128)(2,1)}, u32[]{:S(2)}) copy-start(bf16[128,8,1024]{2,1,0:T(8,128)(2,1)} %copy-done) | copy-start | bytes 6291460
  92.6 7.2 %collective-permute-start.9 = (bf16[8,32,1152]{2,1,0:T(8,128)(2,1)S(1)}, bf16[8,32,1152]{2,1,0:T(8,128)(2,1)}, u32[]{:S(2)}, u32[]{:S(2)}) collective-permute-start(bf16[8,32,1152]{2,1,0:T(8,128)(2,1)S(1)} %all_to_all.23), channel_id=1, source_target_pairs={{0,16},{16,0},{1,17},{17,1},{2,18},{18,2},{3,19},{19,3},{4,20},{20... | collective-permute-start | bytes 1769480 | tf_op jit(solution)/shard_map/ppermute | solution.py:156
  101.4 1.8 %copy-start.2 = (bf16[1024,1152]{1,0:T(8,128)(2,1)S(1)}, bf16[1024,1152]{1,0:T(8,128)(2,1)}, u32[]{:S(2)}) copy-start(bf16[1024,1152]{1,0:T(8,128)(2,1)} %concatenate.23) | copy-start | bytes 7077892
  105.2 2.9 %collective-permute-start.10 = (f32[8,32,1152]{2,1,0:T(8,128)S(1)}, f32[8,32,1152]{2,1,0:T(8,128)S(1)}, u32[]{:S(2)}, u32[]{:S(2)}) collective-permute-start(f32[8,32,1152]{2,1,0:T(8,128)S(1)} %dynamic-slice_bitcast_fusion), channel_id=1, source_target_pairs={{0,16},{16,0},{1,17},{17,1},{2,18},{18,2},{3,19},{19,3},{4,20},{20... | collective-permute-start | bytes 3538952 | tf_op jit(solution)/shard_map/ppermute | solution.py:122
  108.3 12.1 %collective-permute-start.11 = (f32[1,32,1152]{2,1,0:T(8,128)S(1)}, f32[1,32,1152]{2,1,0:T(8,128)S(1)}, u32[]{:S(2)}, u32[]{:S(2)}) collective-permute-start(f32[1,32,1152]{2,1,0:T(8,128)S(1)} %get-tuple-element.8), channel_id=1, source_target_pairs={{0,1},{1,2},{2,3},{3,4},{4,5},{5,6},{6,7},{7,0},{8,9},{9,10},{10,1... | collective-permute-start | bytes 442376 | tf_op jit(solution)/shard_map/ppermute | solution.py:128
  108.9 11.6 %collective-permute-start.12 = (f32[1,32,1152]{2,1,0:T(8,128)S(1)}, f32[1,32,1152]{2,1,0:T(8,128)S(1)}, u32[]{:S(2)}, u32[]{:S(2)}) collective-permute-start(f32[1,32,1152]{2,1,0:T(8,128)S(1)} %get-tuple-element.14), channel_id=1, source_target_pairs={{0,2},{1,3},{2,4},{3,5},{4,6},{5,7},{6,0},{7,1},{8,10},{9,11},{10,... | collective-permute-start | bytes 442376 | tf_op jit(solution)/shard_map/ppermute | solution.py:128
  110.6 29.7 %collective-permute-start.13 = (f32[1,32,1152]{2,1,0:T(8,128)S(1)}, f32[1,32,1152]{2,1,0:T(8,128)S(1)}, u32[]{:S(2)}, u32[]{:S(2)}) collective-permute-start(f32[1,32,1152]{2,1,0:T(8,128)S(1)} %get-tuple-element.13), channel_id=1, source_target_pairs={{0,3},{1,4},{2,5},{3,6},{4,7},{5,0},{6,1},{7,2},{8,11},{9,12},{10,... | collective-permute-start | bytes 442376 | tf_op jit(solution)/shard_map/ppermute | solution.py:128
  111.4 28.9 %collective-permute-start.14 = (f32[1,32,1152]{2,1,0:T(8,128)S(1)}, f32[1,32,1152]{2,1,0:T(8,128)S(1)}, u32[]{:S(2)}, u32[]{:S(2)}) collective-permute-start(f32[1,32,1152]{2,1,0:T(8,128)S(1)} %get-tuple-element.12), channel_id=1, source_target_pairs={{0,4},{1,5},{2,6},{3,7},{4,0},{5,1},{6,2},{7,3},{8,12},{9,13},{10,... | collective-permute-start | bytes 442376 | tf_op jit(solution)/shard_map/ppermute | solution.py:128
  112.5 27.8 %collective-permute-start.15 = (f32[1,32,1152]{2,1,0:T(8,128)S(1)}, f32[1,32,1152]{2,1,0:T(8,128)S(1)}, u32[]{:S(2)}, u32[]{:S(2)}) collective-permute-start(f32[1,32,1152]{2,1,0:T(8,128)S(1)} %get-tuple-element.11), channel_id=1, source_target_pairs={{0,5},{1,6},{2,7},{3,0},{4,1},{5,2},{6,3},{7,4},{8,13},{9,14},{10,... | collective-permute-start | bytes 442376 | tf_op jit(solution)/shard_map/ppermute | solution.py:128
  120.4 19.9 %collective-permute-start.16 = (f32[1,32,1152]{2,1,0:T(8,128)S(1)}, f32[1,32,1152]{2,1,0:T(8,128)S(1)}, u32[]{:S(2)}, u32[]{:S(2)}) collective-permute-start(f32[1,32,1152]{2,1,0:T(8,128)S(1)} %get-tuple-element.10), channel_id=1, source_target_pairs={{0,6},{1,7},{2,0},{3,1},{4,2},{5,3},{6,4},{7,5},{8,14},{9,15},{10,... | collective-permute-start | bytes 442376 | tf_op jit(solution)/shard_map/ppermute | solution.py:128
  120.4 19.9 %collective-permute-start.17 = (f32[1,32,1152]{2,1,0:T(8,128)S(1)}, f32[1,32,1152]{2,1,0:T(8,128)S(1)}, u32[]{:S(2)}, u32[]{:S(2)}) collective-permute-start(f32[1,32,1152]{2,1,0:T(8,128)S(1)} %get-tuple-element.9), channel_id=1, source_target_pairs={{0,7},{1,0},{2,1},{3,2},{4,3},{5,4},{6,5},{7,6},{8,15},{9,8},{10,9... | collective-permute-start | bytes 442376 | tf_op jit(solution)/shard_map/ppermute | solution.py:128
  140.6 7.8 %collective-permute-start.18 = (f32[32,1024]{1,0:T(8,128)S(1)}, f32[32,1024]{1,0:T(8,128)S(1)}, u32[]{:S(2)}, u32[]{:S(2)}) collective-permute-start(f32[32,1024]{1,0:T(8,128)S(1)} %fusion.32), channel_id=1, source_target_pairs={{0,0},{8,16},{16,8},{24,24},{1,1},{9,17},{17,9},{25,25},{2,2},{10,... | collective-permute-start | bytes 393224 | tf_op jit(solution)/shard_map/ppermute | solution.py:169

commit v6 on v5

--- a/solution.py
+++ b/solution.py
@@ -90,7 +90,10 @@
             )
         if iteration + 1 < ITERS:
             weighted = jnp.einsum("rk,rd->kd", weights, arrived, preferred_element_type=jnp.float32)
-            masses = jnp.sum(weights.astype(jnp.float32), axis=0)
+            masses = jnp.dot(
+                jnp.ones((1, weights.shape[0]), jnp.bfloat16), weights,
+                preferred_element_type=jnp.float32,
+            )[0]
             combined = jnp.concatenate(
                 [
                     weighted.reshape(members, share_rows * features),

time: 150 us -> 150 us (level)
  no operation moved by 1% of the time
where the time goes in v6:
time: 150 us
  waiting for transfers between devices  54.2 us (36%)
  starting transfers between devices  30.6 us (20%)
  blocking collectives  30.2 us (20%)
  other arithmetic  14.2 us (9%)
  matrix products  10.5 us (7%)
  local copies, waits for them, and re-layouts  8.79 us (6%)
    all_to_all x1, waiting for transfers between devices, steps(): lax.all_to_all(packed, ROUTE, split_axis=0, concat_axis=0, tiled=True)  23.7 us
    ppermute x14, waiting for transfers between devices, steps(): lax.ppermute(outgoing, PLANE, [(i, (i + shift) % plane) for i in range(pl...  19.2 us
    all_to_all x1, blocking collectives, steps(): lax.all_to_all(smoothing_scale * closing_log_partition, ROUTE, split_axis...  18.3 us
    all_to_all x1, blocking collectives, steps(): lax.all_to_all(jnp.broadcast_to(block[None], (plane,) + block.shape), PLA...  11.8 us
    all_to_all x1, starting transfers between devices, steps(): lax.all_to_all(packed, ROUTE, split_axis=0, concat_axis=0, tiled=True)  11.5 us
    ppermute x14, starting transfers between devices, steps(): lax.ppermute(outgoing, PLANE, [(i, (i + shift) % plane) for i in range(pl...  9.35 us
    ppermute x2, waiting for transfers between devices, steps(): halves = mine + lax.ppermute(theirs, 'core', [(0, 1), (1, 0)])  5.26 us
    ppermute x1, starting transfers between devices, steps(): partner_plane = lax.ppermute(on_plane, 'core', [(0, 1), (1, 0)])  4 us
  transfers between devices with their start and end apart: 20, of which 10 were waited for; matrix products, arithmetic and copies ran while one was open for 6% of the time, Pallas kernels for 0%

profile of v6, /device:TPU:1, one launch (start us, length us, event | category | flops | bytes accessed | tf_op | source)
XLA Modules:
  0.0 149.6 jit_solution(3379769202582103108)
XLA Ops:
  0.7 0.9 copy.27
  1.8 0.9 fusion.28
  2.8 0.7 multiply_add_fusion
  4.1 2.7 %select_bitcast_fusion = bf16[128,8,1024]{2,1,0:T(8,128)(2,1)} fusion(pred[1024]{0:T(1024)(128)(4,1)S(1)} %broadcast_compare_fusion, bf16[512,1024]{1,0:T(8,128)(2,1)S(1)} %copy-done.3, bf16[1024]{0:T(1024)(128)(2,1)S(1)} %fusion.35, f32[512]{0:T(512)S(1)} %add_rsqrt_fusion, s32[512]{0:T(512)S(1)} %multiply_add_fusion), kind=kOutput, calls=%fused_computation.15 | convolution fusion | flops 1078460416 | bytes 3152896 | tf_op jit(solution)/shard_map/dot_general | solution.py:58
  6.8 11.5 %all-to-all-start = ((bf16[128,8,1024]{2,1,0:T(8,128)(2,1)}), bf16[128,8,1024]{2,1,0:T(8,128)(2,1)S(1)}, u32[]{:S(2)}, u32[]{:S(2)}) async-start(bf16[128,8,1024]{2,1,0:T(8,128)(2,1)} %select_bitcast_fusion), calls=%async_computation | async-start | bytes 4194304 | tf_op jit(solution)/shard_map/all_to_all | solution.py:62
  18.3 1.1 collective-permute-start
  19.4 2.4 %collective-permute-done = bf16[512,1024]{1,0:T(8,128)(2,1)} collective-permute-done((bf16[512,1024]{1,0:T(8,128)(2,1)S(1)}, bf16[512,1024]{1,0:T(8,128)(2,1)}, u32[]{:S(2)}, u32[]{:S(2)}) %collective-permute-start) | collective-permute-done | bytes 1048608 | tf_op jit(solution)/shard_map/ppermute | solution.py:37
  21.9 2.8 %fusion.48 = (f32[512,1024]{1,0:T(8,128)}, bf16[512,1024]{1,0:T(8,128)(2,1)S(1)}) fusion(bf16[512,1024]{1,0:T(8,128)(2,1)} %param.5, bf16[512,1024]{1,0:T(8,128)(2,1)} %collective-permute-done, pred[]{:T(512)S(6)} %eq.88), kind=kLoop, calls=%fused_computation.113 | loop fusion | flops 1048576 | bytes 5242881 | tf_op jit(solution)/shard_map/convert_element_type | solution.py:72
  24.9 23.7 %all-to-all-done = bf16[128,8,1024]{2,1,0:T(8,128)(2,1)S(1)} async-done(((bf16[128,8,1024]{2,1,0:T(8,128)(2,1)}), bf16[128,8,1024]{2,1,0:T(8,128)(2,1)S(1)}, u32[]{:S(2)}, u32[]{:S(2)}) %all-to-all-start) | async-done | bytes 2097184 | tf_op jit(solution)/shard_map/all_to_all | solution.py:62
  48.7 1.3 fusion.5
  50.0 0.5 fusion.7
  50.5 0.6 multiply_convert_fusion.1
  51.1 2.6 %fusion.41 = f32[512,1024]{1,0:T(8,128)} fusion(bf16[1024,512]{0,1:T(8,128)(2,1)S(1)} %multiply_convert_fusion.1, bf16[128,8,1024]{2,1,0:T(8,128)(2,1)S(1)} %all-to-all-done), kind=kOutput, calls=%fused_computation.106 | convolution fusion | flops 1073741824 | bytes 5242880 | tf_op jit(solution)/shard_map/rk,rd->kd/dot_general | solution.py:92
  53.7 1.7 %concatenate.18 = f32[2,8,32768]{2,1,0:T(8,128)S(1)} reshape(f32[512,1024]{1,0:T(8,128)} %fusion.41) | data formatting | bytes 4194304 | tf_op jit(solution)/shard_map/concatenate | solution.py:97
  55.5 0.8 fusion.36
  56.4 1.3 collective-permute-start.1
  57.7 2.4 %collective-permute-done.1 = f32[8,32896]{1,0:T(8,128)} collective-permute-done((f32[8,32896]{1,0:T(8,128)S(1)}, f32[8,32896]{1,0:T(8,128)}, u32[]{:S(2)}, u32[]{:S(2)}) %collective-permute-start.1) | collective-permute-done | bytes 1052704 | tf_op jit(solution)/shard_map/ppermute | solution.py:108
  60.1 1.3 fusion.13
  61.5 0.6 constant_dynamic-slice_fusion.12
  62.5 1.3 collective-permute-start.3
  63.8 0.6 collective-permute-start.4
  64.4 1.7 %collective-permute-start.5 = (f32[1,32896]{1,0:T(1,128)S(1)}, f32[1,32896]{1,0:T(1,128)S(1)}, u32[]{:S(2)}, u32[]{:S(2)}) collective-permute-start(f32[1,32896]{1,0:T(1,128)S(1)} %get-tuple-element.19), channel_id=1, source_target_pairs={{0,4},{1,5},{2,6},{3,7},{4,0},{5,1},{6,2},{7,3},{8,12},{9,13},{10,... | collective-permute-start | bytes 394760 | tf_op jit(solution)/shard_map/ppermute | solution.py:112
  66.5 6.8 %collective-permute-done.2 = f32[1,32896]{1,0:T(1,128)S(1)} collective-permute-done((f32[1,32896]{1,0:T(1,128)S(1)}, f32[1,32896]{1,0:T(1,128)S(1)}, u32[]{:S(2)}, u32[]{:S(2)}) %collective-permute-start.2) | collective-permute-done | bytes 131616 | tf_op jit(solution)/shard_map/ppermute | solution.py:112
  73.7 4.5 %collective-permute-done.5 = f32[1,32896]{1,0:T(1,128)S(1)} collective-permute-done((f32[1,32896]{1,0:T(1,128)S(1)}, f32[1,32896]{1,0:T(1,128)S(1)}, u32[]{:S(2)}, u32[]{:S(2)}) %collective-permute-start.5) | collective-permute-done | bytes 131616 | tf_op jit(solution)/shard_map/ppermute | solution.py:112
  78.2 0.4 collective-permute-done.7
  78.6 0.5 add_add_fusion.1
  79.5 1.3 multiply_reduce_fusion.1
  81.3 11.8 %all_to_all.23 = bf16[8,32,1152]{2,1,0:T(8,128)(2,1)S(1)} all-to-all(bf16[8,32,1152]{2,1,0:T(8,128)(2,1)S(1)} %broadcast_in_dim.81), channel_id=1, replica_groups=mesh['z'=4,'core'=2,'yhi'=2,'ylo'=2,'x'=4] {'ylo','x'}, dimensions={0} | all-to-all | bytes 1179648 | tf_op jit(solution)/shard_map/all_to_all | solution.py:152
  93.1 4.0 %collective-permute-start.9 = (bf16[8,32,1152]{2,1,0:T(8,128)(2,1)S(1)}, bf16[8,32,1152]{2,1,0:T(8,128)(2,1)}, u32[]{:S(2)}, u32[]{:S(2)}) collective-permute-start(bf16[8,32,1152]{2,1,0:T(8,128)(2,1)S(1)} %all_to_all.23), channel_id=1, source_target_pairs={{0,16},{16,0},{1,17},{17,1},{2,18},{18,2},{3,19},{19,3},{4,20},{20... | collective-permute-start | bytes 1769480 | tf_op jit(solution)/shard_map/ppermute | solution.py:159
  97.2 3.1 %concatenate.23 = bf16[1024,1152]{1,0:T(8,128)(2,1)} concatenate(bf16[1024,1024]{1,0:T(8,128)(2,1)S(1)} %bitcast.69, bf16[1024,1]{1,0:T(8,128)(2,1)S(1)} %broadcast_in_dim.82, bf16[1024,127]{1,0:T(8,128)(2,1)S(1)} %broadcast_in_dim.83), dimensions={1} | concatenate | bytes 4718592 | tf_op jit(solution)/shard_map/concatenate | solution.py:64
  100.3 1.2 broadcast_select_fusion.2
  101.9 1.3 fusion.6
  103.2 0.5 fusion.8
  103.8 1.8 %fusion.14 = f32[512,1152]{1,0:T(8,128)S(1)} fusion(bf16[1024,1152]{1,0:T(8,128)(2,1)S(1)} %copy-done.2, f32[1024,512]{0,1:T(8,128)S(1)} %get-tuple-element.28, f32[1024]{0:T(1024)S(1)} %fusion.8, f32[1024]{0:T(1024)S(1)} %get-tuple-element.27, f32[512]{0:T(512)S(1)} %fusion.26, f32[1024]{0:T(1024)S(1)} %convert_reduce_fusion.1), kind=kOutput, calls=%fused_computation.34 | convolution fusion | flops 1211105280 | bytes 6830080 | tf_op jit(solution)/shard_map/rk,rd->kd/dot_general | solution.py:119
  105.8 2.8 %collective-permute-done.10 = f32[8,32,1152]{2,1,0:T(8,128)S(1)} collective-permute-done((f32[8,32,1152]{2,1,0:T(8,128)S(1)}, f32[8,32,1152]{2,1,0:T(8,128)S(1)}, u32[]{:S(2)}, u32[]{:S(2)}) %collective-permute-start.10) | collective-permute-done | bytes 1179680 | tf_op jit(solution)/shard_map/ppermute | solution.py:125
  108.8 0.5 collective-permute-start.11
  109.4 1.7 %collective-permute-start.12 = (f32[1,32,1152]{2,1,0:T(8,128)S(1)}, f32[1,32,1152]{2,1,0:T(8,128)S(1)}, u32[]{:S(2)}, u32[]{:S(2)}) collective-permute-start(f32[1,32,1152]{2,1,0:T(8,128)S(1)} %get-tuple-element.12), channel_id=1, source_target_pairs={{0,2},{1,3},{2,4},{3,5},{4,6},{5,7},{6,0},{7,1},{8,10},{9,11},{10,... | collective-permute-start | bytes 442376 | tf_op jit(solution)/shard_map/ppermute | solution.py:131
  111.1 0.8 collective-permute-start.13
  111.9 1.2 collective-permute-start.14
  113.1 0.8 collective-permute-start.15
  113.8 7.1 %collective-permute-done.11 = f32[1,32,1152]{2,1,0:T(8,128)S(1)} collective-permute-done((f32[1,32,1152]{2,1,0:T(8,128)S(1)}, f32[1,32,1152]{2,1,0:T(8,128)S(1)}, u32[]{:S(2)}, u32[]{:S(2)}) %collective-permute-start.11) | collective-permute-done | bytes 147488 | tf_op jit(solution)/shard_map/ppermute | solution.py:131
  121.0 18.3 %all_to_all.24 = f32[128,8,1]{1,2,0:T(1,128)S(1)} all-to-all(f32[128,8,1]{1,2,0:T(1,128)S(1)} %bitcast.77), channel_id=1, replica_groups=mesh['z'=4,'core'=2,'yhi'=2,'ylo'=2,'x'=4] {'z','yhi','core','ylo','x'}, dimensions={0} | all-to-all | bytes 8192 | tf_op jit(solution)/shard_map/all_to_all | solution.py:87
  139.4 0.5 broadcast.161
  139.9 0.8 reduce.13
  141.1 3.2 %collective-permute-start.18 = (f32[32,1024]{1,0:T(8,128)S(1)}, f32[32,1024]{1,0:T(8,128)S(1)}, u32[]{:S(2)}, u32[]{:S(2)}) collective-permute-start(f32[32,1024]{1,0:T(8,128)S(1)} %fusion.32), channel_id=1, source_target_pairs={{0,0},{8,16},{16,8},{24,24},{1,1},{9,17},{17,9},{25,25},{2,2},{10,... | collective-permute-start | bytes 393224 | tf_op jit(solution)/shard_map/ppermute | solution.py:172
  144.3 0.9 select_reduce_fusion
  145.2 3.7 %collective-permute-done.18 = f32[32,1024]{1,0:T(8,128)S(1)} collective-permute-done((f32[32,1024]{1,0:T(8,128)S(1)}, f32[32,1024]{1,0:T(8,128)S(1)}, u32[]{:S(2)}, u32[]{:S(2)}) %collective-permute-start.18) | collective-permute-done | bytes 131104 | tf_op jit(solution)/shard_map/ppermute | solution.py:172
  148.9 0.7 copy.35
  (70 shorter events, 4.8 us)
Async XLA Ops:
  0.6 3.1 %copy-start.3 = (bf16[512,1024]{1,0:T(8,128)(2,1)S(1)}, bf16[512,1024]{1,0:T(8,128)(2,1)}, u32[]{:S(2)}) copy-start(bf16[512,1024]{1,0:T(8,128)(2,1)} %param.3) | copy-start | bytes 3145732
  6.8 11.5 %copy-start.4 = (bf16[512,1024]{1,0:T(8,128)(2,1)S(1)}, bf16[512,1024]{1,0:T(8,128)(2,1)}, u32[]{:S(2)}) copy-start(bf16[512,1024]{1,0:T(8,128)(2,1)} %param.5) | copy-start | bytes 3145732
  6.8 41.8 %all-to-all-start = ((bf16[128,8,1024]{2,1,0:T(8,128)(2,1)}), bf16[128,8,1024]{2,1,0:T(8,128)(2,1)S(1)}, u32[]{:S(2)}, u32[]{:S(2)}) async-start(bf16[128,8,1024]{2,1,0:T(8,128)(2,1)} %select_bitcast_fusion), calls=%async_computation | async-start | bytes 4194304 | tf_op jit(solution)/shard_map/all_to_all | solution.py:62
  18.3 3.6 %collective-permute-start = (bf16[512,1024]{1,0:T(8,128)(2,1)S(1)}, bf16[512,1024]{1,0:T(8,128)(2,1)}, u32[]{:S(2)}, u32[]{:S(2)}) collective-permute-start(bf16[512,1024]{1,0:T(8,128)(2,1)S(1)} %copy-done.4), channel_id=1, source_target_pairs={{0,16},{16,0},{1,17},{17,1},{2,18},{18,2},{3,19},{19,3},{4,20},{20... | collective-permute-start | bytes 3145736 | tf_op jit(solution)/shard_map/ppermute | solution.py:37
  48.6 2.6 %copy-start = (bf16[128,8,1024]{2,1,0:T(8,128)(2,1)}, bf16[128,8,1024]{2,1,0:T(8,128)(2,1)S(1)}, u32[]{:S(2)}) copy-start(bf16[128,8,1024]{2,1,0:T(8,128)(2,1)S(1)} %all-to-all-done) | copy-start | bytes 6291460
  56.4 3.8 %collective-permute-start.1 = (f32[8,32896]{1,0:T(8,128)S(1)}, f32[8,32896]{1,0:T(8,128)}, u32[]{:S(2)}, u32[]{:S(2)}) collective-permute-start(f32[8,32896]{1,0:T(8,128)S(1)} %fusion.10), channel_id=1, source_target_pairs={{0,16},{16,0},{1,17},{17,1},{2,18},{18,2},{3,19},{19,3},{4,20},{20... | collective-permute-start | bytes 3158024 | tf_op jit(solution)/shard_map/ppermute | solution.py:108
  62.1 11.2 %collective-permute-start.2 = (f32[1,32896]{1,0:T(1,128)S(1)}, f32[1,32896]{1,0:T(1,128)S(1)}, u32[]{:S(2)}, u32[]{:S(2)}) collective-permute-start(f32[1,32896]{1,0:T(1,128)S(1)} %get-tuple-element.15), channel_id=1, source_target_pairs={{0,1},{1,2},{2,3},{3,4},{4,5},{5,6},{6,7},{7,0},{8,9},{9,10},{10,1... | collective-permute-start | bytes 394760 | tf_op jit(solution)/shard_map/ppermute | solution.py:112
  62.5 10.8 %collective-permute-start.3 = (f32[1,32896]{1,0:T(1,128)S(1)}, f32[1,32896]{1,0:T(1,128)S(1)}, u32[]{:S(2)}, u32[]{:S(2)}) collective-permute-start(f32[1,32896]{1,0:T(1,128)S(1)} %get-tuple-element.21), channel_id=1, source_target_pairs={{0,2},{1,3},{2,4},{3,5},{4,6},{5,7},{6,0},{7,1},{8,10},{9,11},{10,... | collective-permute-start | bytes 394760 | tf_op jit(solution)/shard_map/ppermute | solution.py:112
  63.8 9.9 %collective-permute-start.4 = (f32[1,32896]{1,0:T(1,128)S(1)}, f32[1,32896]{1,0:T(1,128)S(1)}, u32[]{:S(2)}, u32[]{:S(2)}) collective-permute-start(f32[1,32896]{1,0:T(1,128)S(1)} %get-tuple-element.20), channel_id=1, source_target_pairs={{0,3},{1,4},{2,5},{3,6},{4,7},{5,0},{6,1},{7,2},{8,11},{9,12},{10,... | collective-permute-start | bytes 394760 | tf_op jit(solution)/shard_map/ppermute | solution.py:112
  64.4 13.8 %collective-permute-start.5 = (f32[1,32896]{1,0:T(1,128)S(1)}, f32[1,32896]{1,0:T(1,128)S(1)}, u32[]{:S(2)}, u32[]{:S(2)}) collective-permute-start(f32[1,32896]{1,0:T(1,128)S(1)} %get-tuple-element.19), channel_id=1, source_target_pairs={{0,4},{1,5},{2,6},{3,7},{4,0},{5,1},{6,2},{7,3},{8,12},{9,13},{10,... | collective-permute-start | bytes 394760 | tf_op jit(solution)/shard_map/ppermute | solution.py:112
  66.1 12.0 %collective-permute-start.6 = (f32[1,32896]{1,0:T(1,128)S(1)}, f32[1,32896]{1,0:T(1,128)S(1)}, u32[]{:S(2)}, u32[]{:S(2)}) collective-permute-start(f32[1,32896]{1,0:T(1,128)S(1)} %get-tuple-element.18), channel_id=1, source_target_pairs={{0,5},{1,6},{2,7},{3,0},{4,1},{5,2},{6,3},{7,4},{8,13},{9,14},{10,... | collective-permute-start | bytes 394760 | tf_op jit(solution)/shard_map/ppermute | solution.py:112
  73.3 5.3 %collective-permute-start.7 = (f32[1,32896]{1,0:T(1,128)S(1)}, f32[1,32896]{1,0:T(1,128)S(1)}, u32[]{:S(2)}, u32[]{:S(2)}) collective-permute-start(f32[1,32896]{1,0:T(1,128)S(1)} %get-tuple-element.17), channel_id=1, source_target_pairs={{0,6},{1,7},{2,0},{3,1},{4,2},{5,3},{6,4},{7,5},{8,14},{9,15},{10,... | collective-permute-start | bytes 394760 | tf_op jit(solution)/shard_map/ppermute | solution.py:112
  73.3 5.3 %collective-permute-start.8 = (f32[1,32896]{1,0:T(1,128)S(1)}, f32[1,32896]{1,0:T(1,128)S(1)}, u32[]{:S(2)}, u32[]{:S(2)}) collective-permute-start(f32[1,32896]{1,0:T(1,128)S(1)} %get-tuple-element.16), channel_id=1, source_target_pairs={{0,7},{1,0},{2,1},{3,2},{4,3},{5,4},{6,5},{7,6},{8,15},{9,8},{10,9... | collective-permute-start | bytes 394760 | tf_op jit(solution)/shard_map/ppermute | solution.py:112
  79.1 18.1 %copy-start.1 = (bf16[128,8,1024]{2,1,0:T(8,128)(2,1)S(1)}, bf16[128,8,1024]{2,1,0:T(8,128)(2,1)}, u32[]{:S(2)}) copy-start(bf16[128,8,1024]{2,1,0:T(8,128)(2,1)} %copy-done) | copy-start | bytes 6291460
  93.1 7.2 %collective-permute-start.9 = (bf16[8,32,1152]{2,1,0:T(8,128)(2,1)S(1)}, bf16[8,32,1152]{2,1,0:T(8,128)(2,1)}, u32[]{:S(2)}, u32[]{:S(2)}) collective-permute-start(bf16[8,32,1152]{2,1,0:T(8,128)(2,1)S(1)} %all_to_all.23), channel_id=1, source_target_pairs={{0,16},{16,0},{1,17},{17,1},{2,18},{18,2},{3,19},{19,3},{4,20},{20... | collective-permute-start | bytes 1769480 | tf_op jit(solution)/shard_map/ppermute | solution.py:159
  101.9 1.8 %copy-start.2 = (bf16[1024,1152]{1,0:T(8,128)(2,1)S(1)}, bf16[1024,1152]{1,0:T(8,128)(2,1)}, u32[]{:S(2)}) copy-start(bf16[1024,1152]{1,0:T(8,128)(2,1)} %concatenate.23) | copy-start | bytes 7077892
  105.7 2.9 %collective-permute-start.10 = (f32[8,32,1152]{2,1,0:T(8,128)S(1)}, f32[8,32,1152]{2,1,0:T(8,128)S(1)}, u32[]{:S(2)}, u32[]{:S(2)}) collective-permute-start(f32[8,32,1152]{2,1,0:T(8,128)S(1)} %dynamic-slice_bitcast_fusion), channel_id=1, source_target_pairs={{0,16},{16,0},{1,17},{17,1},{2,18},{18,2},{3,19},{19,3},{4,20},{20... | collective-permute-start | bytes 3538952 | tf_op jit(solution)/shard_map/ppermute | solution.py:125
  108.8 12.1 %collective-permute-start.11 = (f32[1,32,1152]{2,1,0:T(8,128)S(1)}, f32[1,32,1152]{2,1,0:T(8,128)S(1)}, u32[]{:S(2)}, u32[]{:S(2)}) collective-permute-start(f32[1,32,1152]{2,1,0:T(8,128)S(1)} %get-tuple-element.6), channel_id=1, source_target_pairs={{0,1},{1,2},{2,3},{3,4},{4,5},{5,6},{6,7},{7,0},{8,9},{9,10},{10,1... | collective-permute-start | bytes 442376 | tf_op jit(solution)/shard_map/ppermute | solution.py:131
  109.4 11.6 %collective-permute-start.12 = (f32[1,32,1152]{2,1,0:T(8,128)S(1)}, f32[1,32,1152]{2,1,0:T(8,128)S(1)}, u32[]{:S(2)}, u32[]{:S(2)}) collective-permute-start(f32[1,32,1152]{2,1,0:T(8,128)S(1)} %get-tuple-element.12), channel_id=1, source_target_pairs={{0,2},{1,3},{2,4},{3,5},{4,6},{5,7},{6,0},{7,1},{8,10},{9,11},{10,... | collective-permute-start | bytes 442376 | tf_op jit(solution)/shard_map/ppermute | solution.py:131
  111.1 29.7 %collective-permute-start.13 = (f32[1,32,1152]{2,1,0:T(8,128)S(1)}, f32[1,32,1152]{2,1,0:T(8,128)S(1)}, u32[]{:S(2)}, u32[]{:S(2)}) collective-permute-start(f32[1,32,1152]{2,1,0:T(8,128)S(1)} %get-tuple-element.11), channel_id=1, source_target_pairs={{0,3},{1,4},{2,5},{3,6},{4,7},{5,0},{6,1},{7,2},{8,11},{9,12},{10,... | collective-permute-start | bytes 442376 | tf_op jit(solution)/shard_map/ppermute | solution.py:131
  111.9 28.9 %collective-permute-start.14 = (f32[1,32,1152]{2,1,0:T(8,128)S(1)}, f32[1,32,1152]{2,1,0:T(8,128)S(1)}, u32[]{:S(2)}, u32[]{:S(2)}) collective-permute-start(f32[1,32,1152]{2,1,0:T(8,128)S(1)} %get-tuple-element.10), channel_id=1, source_target_pairs={{0,4},{1,5},{2,6},{3,7},{4,0},{5,1},{6,2},{7,3},{8,12},{9,13},{10,... | collective-permute-start | bytes 442376 | tf_op jit(solution)/shard_map/ppermute | solution.py:131
  113.1 27.8 %collective-permute-start.15 = (f32[1,32,1152]{2,1,0:T(8,128)S(1)}, f32[1,32,1152]{2,1,0:T(8,128)S(1)}, u32[]{:S(2)}, u32[]{:S(2)}) collective-permute-start(f32[1,32,1152]{2,1,0:T(8,128)S(1)} %get-tuple-element.9), channel_id=1, source_target_pairs={{0,5},{1,6},{2,7},{3,0},{4,1},{5,2},{6,3},{7,4},{8,13},{9,14},{10,... | collective-permute-start | bytes 442376 | tf_op jit(solution)/shard_map/ppermute | solution.py:131
  120.9 19.9 %collective-permute-start.16 = (f32[1,32,1152]{2,1,0:T(8,128)S(1)}, f32[1,32,1152]{2,1,0:T(8,128)S(1)}, u32[]{:S(2)}, u32[]{:S(2)}) collective-permute-start(f32[1,32,1152]{2,1,0:T(8,128)S(1)} %get-tuple-element.8), channel_id=1, source_target_pairs={{0,6},{1,7},{2,0},{3,1},{4,2},{5,3},{6,4},{7,5},{8,14},{9,15},{10,... | collective-permute-start | bytes 442376 | tf_op jit(solution)/shard_map/ppermute | solution.py:131
  120.9 19.9 %collective-permute-start.17 = (f32[1,32,1152]{2,1,0:T(8,128)S(1)}, f32[1,32,1152]{2,1,0:T(8,128)S(1)}, u32[]{:S(2)}, u32[]{:S(2)}) collective-permute-start(f32[1,32,1152]{2,1,0:T(8,128)S(1)} %get-tuple-element.7), channel_id=1, source_target_pairs={{0,7},{1,0},{2,1},{3,2},{4,3},{5,4},{6,5},{7,6},{8,15},{9,8},{10,9... | collective-permute-start | bytes 442376 | tf_op jit(solution)/shard_map/ppermute | solution.py:131
  141.1 7.8 %collective-permute-start.18 = (f32[32,1024]{1,0:T(8,128)S(1)}, f32[32,1024]{1,0:T(8,128)S(1)}, u32[]{:S(2)}, u32[]{:S(2)}) collective-permute-start(f32[32,1024]{1,0:T(8,128)S(1)} %fusion.32), channel_id=1, source_target_pairs={{0,0},{8,16},{16,8},{24,24},{1,1},{9,17},{17,9},{25,25},{2,2},{10,... | collective-permute-start | bytes 393224 | tf_op jit(solution)/shard_map/ppermute | solution.py:172
